TPU v7x, 32 devices: a whole 2x2x4 slice. The times are simulated.
32 devices in a mesh: groups: 2 (over x), tensor: 16 (over z, y, core).
Axes of the slice: x: 2, y: 2, z: 4, core: 2. Of those that a mesh axis runs over, the one named last changes fastest.
Arguments:
- tokens: bfloat16 [256, 8192], P(('groups', 'tensor')), parts along dimension 0, may hold values from -6 to 6
- gate_weight: bfloat16 [8192, 28672], P(None, 'tensor'), may hold values from -0.0625 to 0.0625
- up_weight: bfloat16 [8192, 28672], P(None, 'tensor'), may hold values from -0.0625 to 0.0625
- adapter_down_weight: bfloat16 [16, 8192, 64], P('tensor'), may hold values from -0.0625 to 0.0625
- adapter_up_weight: bfloat16 [16, 64, 28672], P(None, None, 'tensor'), may hold values from -0.75 to 0.75
- token_adapter_index: int32 [256, 1], P(('groups', 'tensor')), parts along dimension 0, may hold values from 0 to 15; in each aligned block of 128 rows (0 to 127, 128 to 255, ...) at most 16 rows name the same one
- adapter_slot_index: int32 [16], replicated, may hold values from 0 to 15, each once
Outputs:
- hidden: bfloat16 [256, 28672], P('groups', 'tensor'), parts along dimension 0
There are 2 independent parts, one for each index of `groups`. A program takes and returns all parts, laid end to end along the dimension named above; an argument that names none is the same for every part. Nothing has to cross between parts.
Inputs may be any that keep to these rules, and one draw needn't show every extreme that they name: `token_adapter_index`: in every draw at most 16 of all 128 tokens use one adapter, and some adapter is used by exactly 16 tokens; every adapter is used by some token. `adapter_slot_index`: A permutation; slot s is stored on the device of index s along tensor.
All inputs are finite; a program needn't handle non-finite values.
Results may differ from a plain program's by a relative error of at most 0.0039.
Values may be sent and summed in bfloat16 or wider, within the bound.
No kernel may reach another device: no remote copies, remote signals or barrier semaphores. Data moves between devices by JAX's collectives and lax.ppermute only.
A program may use at most 192 MiB of HBM per device.

v0:
```python
import math

import jax
import jax.numpy as jnp
from jax import lax
from jax.sharding import PartitionSpec as P


def body(
    tokens,
    gate_weight,
    up_weight,
    adapter_down_weight,
    adapter_up_weight,
    token_adapter_index,
    adapter_slot_index,
):
    me = lax.axis_index("tensor")
    hidden_per_device = gate_weight.shape[1]
    all_ids = lax.all_gather(token_adapter_index, "tensor", axis=0, tiled=True)[:, 0]
    total = all_ids.shape[0]
    resident_weight = adapter_slot_index.shape[0]
    table_hits = all_ids[:, None] == jnp.arange(resident_weight, dtype=jnp.int32)[None, :]
    slot_of = jnp.sum(jnp.where(table_hits, adapter_slot_index[None, :], 0), axis=1)
    local_portion = lax.all_gather(tokens, "tensor", axis=0, tiled=True)
    mine = slot_of == me
    reduced_input = jnp.dot(
        local_portion, adapter_down_weight[0], preferred_element_type=jnp.float32
    )
    reduced_input = jnp.where(mine[:, None], reduced_input, 0.0)
    products = jnp.concatenate(
        [
            jnp.dot(local_portion, gate_weight, preferred_element_type=jnp.float32),
            jnp.dot(local_portion, up_weight, preferred_element_type=jnp.float32),
            reduced_input,
        ],
        axis=1,
    )
    gate = products[:, :hidden_per_device]
    up = products[:, hidden_per_device : 2 * hidden_per_device]
    low_part = products[:, 2 * hidden_per_device :]
    adapter_delta = lax.psum(low_part, "tensor").astype(jnp.bfloat16)
    device_position = adapter_delta.shape[1]
    up_weight_slice = adapter_up_weight.reshape(
        resident_weight * device_position, hidden_per_device
    )
    block = math.gcd(total, 256)
    low_blocks = adapter_delta.reshape(total // block, block, device_position)
    slot_blocks = slot_of.reshape(total // block, block)
    slot_range = jnp.arange(resident_weight, dtype=jnp.int32)

    def lift(args):
        reduced_input, selected_slot = args
        hits = selected_slot[:, None, None] == slot_range[None, :, None]
        spread = jnp.where(hits, reduced_input[:, None, :], jnp.zeros((), jnp.bfloat16)).reshape(
            reduced_input.shape[0], resident_weight * device_position
        )
        return jnp.dot(spread, up_weight_slice, preferred_element_type=jnp.float32)

    delta = lax.map(lift, (low_blocks, slot_blocks)).reshape(total, hidden_per_device)
    return (jax.nn.silu(gate) * (up + delta)).astype(jnp.bfloat16)


def solution(mesh):
    in_specs = (
        P(("groups", "tensor"), None),
        P(None, "tensor"),
        P(None, "tensor"),
        P("tensor", None, None),
        P(None, None, "tensor"),
        P(("groups", "tensor"), None),
        P(),
    )
    out_specs = P("groups", "tensor")
    return jax.shard_map(body, mesh=mesh, in_specs=in_specs, out_specs=out_specs, check_vma=False)
```

profile of v0, /device:TPU:0, one launch (start us, length us, event | category | flops | bytes accessed | tf_op | source)
XLA Modules:
  0.0 151.4 jit_solution(16022517166369663602)
XLA Ops:
  6.5 0.0 copy-start
  6.5 0.0 all-gather.2.cloned.1.call-start
  6.5 0.7 all-gather.2.cloned.1.call-update
  7.3 1.2 dynamic-slice.2
  9.2 0.8 bitcast_dynamic-update-slice_fusion
  9.9 13.8 %all-reduce = s32[128]{0:T(128)S(1)} all-reduce(s32[128]{0:T(128)S(1)} %bitcast_dynamic-update-slice_fusion), channel_id=1, replica_groups=mesh['groups'=2,'tensor'=16] {'tensor'}, use_global_device_ids=true, to_apply=%add | all-reduce | flops 128 | bytes 1024
  23.7 0.7 select_reduce_fusion
  24.5 29.1 %all-gather.2.cloned.1.call-done = bf16[128,8192]{1,0:T(8,128)(2,1)} async-done(((bf16[8,8192]{1,0:T(8,128)(2,1)}), bf16[128,8192]{1,0:T(8,128)(2,1)}) %all-gather.2.cloned.1.call-update) | async-done | bytes 2097168 | tf_op jit(solution)/shard_map/all_gather | solution.py:25
  53.7 0.0 copy-done
  53.7 0.0 copy-start.2
  53.7 2.6 %convolution_select_fusion = f32[128,64]{0,1:T(8,128)S(1)} fusion(bf16[128,8192]{1,0:T(8,128)(2,1)} %all-gather.2.cloned.1.call-done, bf16[1,8192,64]{1,2,0:T(8,128)(2,1)S(1)} %copy-done, pred[128]{0:T(512)(128)(4,1)S(1)} %broadcast_compare_fusion), kind=kOutput, calls=%fused_computation.4 | convolution fusion | flops 134225920 | bytes 3178624 | tf_op jit(solution)/shard_map/dot_general | solution.py:27
  56.2 59.5 %psum.7 = bf16[128,64]{0,1:T(8,128)(2,1)S(1)} all-reduce(f32[128,64]{0,1:T(8,128)S(1)} %convolution_select_fusion), channel_id=1, replica_groups=mesh['groups'=2,'tensor'=16] {'tensor'}, use_global_device_ids=true, to_apply=%region_1.2 | all-reduce | flops 8192 | bytes 49152 | tf_op jit(solution)/shard_map/psum | solution.py:42
  115.7 2.7 %convolution_bitcast_fusion = f32[128,1792]{1,0:T(8,128)S(1)} fusion(bf16[16,64,1792]{2,1,0:T(8,128)(2,1)} %param.11, pred[128,16]{0,1:T(8,128)(4,1)S(1)} %iota_compare_fusion, bf16[128,64]{0,1:T(8,128)(2,1)S(1)} %psum.7), kind=kOutput, calls=%fused_computation | convolution fusion | flops 469893120 | bytes 4605952 | tf_op jit(solution)/shard_map/while/body/eval_jaxpr/dot_general | solution.py:58
  118.4 0.0 copy-done.2
  118.4 11.7 %fusion.8 = f32[128,1792]{1,0:T(8,128)S(1)} fusion(bf16[128,8192]{1,0:T(8,128)(2,1)S(1)} %copy-done.2, bf16[8192,1792]{1,0:T(8,128)(2,1)} %param.8), kind=kOutput, calls=%fused_computation.16 | convolution fusion | flops 3758096384 | bytes 32374784 | tf_op jit(solution)/shard_map/dot_general | solution.py:33
  130.2 0.0 copy-start.1
  130.2 14.4 %fusion.1 = bf16[128,1792]{1,0:T(8,128)(2,1)} fusion(f32[128,1792]{1,0:T(8,128)S(1)} %convolution_bitcast_fusion, bf16[128,8192]{1,0:T(8,128)(2,1)S(1)} %copy-done.2, bf16[8192,1792]{1,0:T(8,128)(2,1)} %param.9, f32[128,1792]{1,0:T(8,128)S(1)} %fusion.8), kind=kOutput, calls=%fused_computation.3 | convolution fusion | flops 3759702016 | bytes 33751040 | tf_op jit(solution)/shard_map/dot_general | solution.py:34
  144.5 0.0 copy-done.1
  (3 shorter events, 0.0 us)
Async XLA Ops:
  6.5 47.1 %copy-start = (bf16[1,8192,64]{1,2,0:T(8,128)(2,1)S(1)}, bf16[1,8192,64]{1,2,0:T(8,128)(2,1)}, u32[]{:S(2)}) copy-start(bf16[1,8192,64]{1,2,0:T(8,128)(2,1)} %param.10) | copy-start | bytes 3145732
  6.5 47.1 %all-gather.2.cloned.1.call-start = ((), (), s32[]{:S(2)}) async-start(), calls=%async_computation | async-start | bytes 2228224 | tf_op jit(solution)/shard_map/all_gather | solution.py:25
  53.7 64.8 %copy-start.2 = (bf16[128,8192]{1,0:T(8,128)(2,1)S(1)}, bf16[128,8192]{1,0:T(8,128)(2,1)}, u32[]{:S(2)}) copy-start(bf16[128,8192]{1,0:T(8,128)(2,1)} %all-gather.2.cloned.1.call-done) | copy-start | bytes 6291460
  130.2 14.4 %copy-start.1 = (bf16[1,8192,64]{1,2,0:T(8,128)(2,1)S(1)}, bf16[1,8192,64]{1,2,0:T(8,128)(2,1)}, u32[]{:S(2)}) copy-start(bf16[1,8192,64]{1,2,0:T(8,128)(2,1)} %param.10) | copy-start | bytes 3145732
Sparse Core Ops, SparseCore 0:
  9.5 44.0 all-gather.1
where the time goes:
time: 152 us; the launch traced here: 151 us
  blocking collectives  73.3 us (48%)
  matrix products  31.4 us (21%)
  waiting for transfers between devices  29.9 us (20%)
  between operations  14.1 us (9%)
  local copies, waits for them, and re-layouts  2.01 us (1%)
    psum x1, blocking collectives, body(): adapter_delta = lax.psum(low_part, 'tensor').astype(jnp.bfloat16)  59.5 us
    all_gather x1, waiting for transfers between devices, body(): local_portion = lax.all_gather(tokens, 'tensor', axis=0, tiled=True)  29.1 us
    dot_general x1, matrix products, body(): jnp.dot(local_portion, up_weight, preferred_element_type=jnp.float32)  14.4 us
    unnamed x1, blocking collectives  13.8 us
    dot_general x1, matrix products, body(): jnp.dot(local_portion, gate_weight, preferred_element_type=jnp.float32)  11.7 us
  transfers between devices with their start and end apart: 1, of which 1 were waited for; matrix products, arithmetic and copies ran while one was open for 2% of the time, Pallas kernels for 0%

commit v1 on v0

v1 whole, which is shorter than its diff:
```python
import jax
import jax.numpy as jnp
from jax import lax
from jax.sharding import PartitionSpec as P

CHUNKS = 2
LANES = 128


def body(
    tokens,
    gate_weight,
    up_weight,
    adapter_down_weight,
    adapter_up_weight,
    token_adapter_index,
    adapter_slot_index,
):
    me = lax.axis_index("tensor")
    rows, width = tokens.shape
    step = width // CHUNKS
    local_slot = jnp.take(adapter_slot_index, token_adapter_index[:, 0], axis=0)
    slot_cols = jnp.broadcast_to(local_slot.astype(jnp.bfloat16)[:, None], (rows, LANES))

    gate = up = low = None
    slots = None
    for c in range(CHUNKS):
        piece = tokens[:, c * step : (c + 1) * step]
        if c == CHUNKS - 1:
            piece = jnp.concatenate([piece, slot_cols], axis=1)
        gathered = lax.all_gather(piece, "tensor", axis=0, tiled=True)
        if c == CHUNKS - 1:
            slots = gathered[:, step].astype(jnp.int32)
            gathered = gathered[:, :step]
        g = jnp.dot(gathered, gate_weight[c * step : (c + 1) * step], preferred_element_type=jnp.float32)
        u = jnp.dot(gathered, up_weight[c * step : (c + 1) * step], preferred_element_type=jnp.float32)
        d = jnp.dot(gathered, adapter_down_weight[0, c * step : (c + 1) * step], preferred_element_type=jnp.float32)
        gate = g if gate is None else gate + g
        up = u if up is None else up + u
        low = d if low is None else low + d

    mine = slots == me
    low = jnp.where(mine[:, None], low, 0.0).astype(jnp.bfloat16)
    spread = lax.all_gather(low, "tensor", axis=0, tiled=False)
    delta = jnp.einsum("str,srh->th", spread, adapter_up_weight, preferred_element_type=jnp.float32)
    return (jax.nn.silu(gate) * (up + delta)).astype(jnp.bfloat16)


def solution(mesh):
    in_specs = (
        P(("groups", "tensor"), None),
        P(None, "tensor"),
        P(None, "tensor"),
        P("tensor", None, None),
        P(None, None, "tensor"),
        P(("groups", "tensor"), None),
        P(),
    )
    out_specs = P("groups", "tensor")
    return jax.shard_map(body, mesh=mesh, in_specs=in_specs, out_specs=out_specs, check_vma=False)
```

time: 152 us -> 149 us (0.980)
  blocking collectives: 73.3 us -> 20.1 us
  waiting for transfers between devices: 29.9 us -> 76.7 us
  other arithmetic: 0.76 us -> 2.93 us
  matrix products: 31.4 us -> 33.3 us
    psum x1 -> x0, blocking collectives: 59.5 us -> none  [body(): adapter_delta = lax.psum(low_part, 'tensor').astype(jnp.bfloat16)]
    all_gather x1 -> x2, waiting for transfers between devices: 29.1 us -> 76.7 us  [body(): gathered = lax.all_gather(piece, 'tensor', axis=0, tiled=True)]
    all_gather x0 -> x1, blocking collectives: none -> 20.1 us  [body(): spread = lax.all_gather(low, 'tensor', axis=0, tiled=False)]
    unnamed x1 -> x0, blocking collectives: 13.8 us -> none
    unnamed x9 -> x11, local copies, waits for them, and re-layouts: 2.01 us -> 0.06 us
    dot_general x4 -> x7, matrix products: 31.4 us -> 33.3 us  [the longest x2 13.4 us: body(): jnp.dot(gathered, up_weight[c * step:(c + 1) * step], preferred_element_t...]
  transfers between devices with their start and end apart: 1 -> 2, of which waited for: 1 -> 2; matrix products, arithmetic and copies ran while one was open for 2% -> 3% of each run, Pallas kernels for 0% -> 0%
where the time goes in v1:
time: 149 us
  waiting for transfers between devices  76.7 us (51%)
  matrix products  33.3 us (22%)
  blocking collectives  20.1 us (13%)
  between operations  13.5 us (9%)
  other arithmetic  2.93 us (2%)
  local copies, waits for them, and re-layouts  2.29 us (2%)
    all_gather x2, waiting for transfers between devices, body(): gathered = lax.all_gather(piece, 'tensor', axis=0, tiled=True)  76.7 us
    all_gather x1, blocking collectives, body(): spread = lax.all_gather(low, 'tensor', axis=0, tiled=False)  20.1 us
    dot_general x2, matrix products, body(): jnp.dot(gathered, up_weight[c * step:(c + 1) * step], preferred_element_t...  13.4 us
    dot_general x2, matrix products, body(): jnp.dot(gathered, gate_weight[c * step:(c + 1) * step], preferred_element...  13 us
    dot_general x2, matrix products, body(): jnp.dot(gathered, adapter_down_weight[0, c * step:(c + 1) * step], prefer...  3.68 us
    dot_general x1, matrix products, body(): jnp.einsum('str,srh->th', spread, adapter_up_weight, preferred_element_ty...  3.19 us
  transfers between devices with their start and end apart: 2, of which 2 were waited for; matrix products, arithmetic and copies ran while one was open for 3% of the time, Pallas kernels for 0%

profile of v1, /device:TPU:0, one launch (start us, length us, event | category | flops | bytes accessed | tf_op | source)
XLA Modules:
  0.0 148.9 jit_solution(2792847004383480132)
XLA Ops:
  6.5 0.0 copy-start
  6.5 0.0 all-gather.4.cloned.1.call-start
  6.5 1.5 %fusion.40 = (bf16[8,4096]{1,0:T(8,128)(2,1)}, bf16[8,4096]{1,0:T(8,128)(2,1)S(1)}) fusion(bf16[8,8192]{1,0:T(8,128)(2,1)} %param.7), kind=kLoop, calls=%fused_computation.36 | loop fusion | bytes 262144 | tf_op jit(solution)/shard_map/slice | solution.py:28
  8.0 0.0 all-gather.4.cloned.1.call-update
  8.1 0.0 all-gather.6.cloned.1.call-start
  8.1 0.7 fusion.39
  8.8 0.0 copy-done
  8.8 0.6 gather_fusion
  9.4 0.7 convert_bitcast_fusion
  10.1 0.1 broadcast_in_dim.26
  10.2 0.6 pad_maximum_fusion
  10.8 0.0 all-gather.6.cloned.1.call-update
  10.8 39.3 %all-gather.4.cloned.1.call-done = bf16[128,4096]{1,0:T(8,128)(2,1)} async-done(((bf16[8,4096]{1,0:T(8,128)(2,1)}), bf16[128,4096]{1,0:T(8,128)(2,1)}) %all-gather.4.cloned.1.call-update) | async-done | bytes 1048592 | tf_op jit(solution)/shard_map/all_gather | solution.py:31
  50.2 1.8 %fusion.34 = f32[128,64]{0,1:T(8,128)S(1)} fusion(bf16[128,4096]{1,0:T(8,128)(2,1)} %all-gather.4.cloned.1.call-done, bf16[1,8192,64]{1,2,0:T(8,128)(2,1)} %param.10), kind=kOutput, calls=%fused_computation.24 | convolution fusion | flops 67108864 | bytes 1605632 | tf_op jit(solution)/shard_map/dot_general | solution.py:37
  52.0 37.4 %all-gather.6.cloned.1.call-done = bf16[128,4224]{1,0:T(8,128)(2,1)} async-done(((bf16[8,4224]{1,0:T(8,128)(2,1)}), bf16[128,4224]{1,0:T(8,128)(2,1)}) %all-gather.6.cloned.1.call-update) | async-done | bytes 1081360 | tf_op jit(solution)/shard_map/all_gather | solution.py:31
  89.4 0.0 copy-start.3
  89.4 1.0 fusion.38
  90.4 1.8 %fusion.29 = bf16[128,64]{0,1:T(8,128)(2,1)S(1)} fusion(f32[128,64]{0,1:T(8,128)S(1)} %fusion.34, bf16[128,4224]{1,0:T(8,128)(2,1)} %all-gather.6.cloned.1.call-done, bf16[1,8192,64]{1,2,0:T(8,128)(2,1)} %param.10, pred[128]{0:T(512)(128)(4,1)S(1)} %fusion.38), kind=kOutput, calls=%fused_computation.19 | convolution fusion | flops 67133440 | bytes 1622144 | tf_op jit(solution)/shard_map/dot_general | solution.py:37
  92.2 20.1 %all-gather = bf16[2048,64]{0,1:T(8,128)(2,1)S(1)} all-gather(bf16[128,64]{0,1:T(8,128)(2,1)S(1)} %fusion.29), channel_id=2, replica_groups=mesh['groups'=2,'tensor'=16] {'tensor'}, dimensions={0}, use_global_device_ids=true | all-gather | bytes 278528 | tf_op jit(solution)/shard_map/all_gather | solution.py:44
  112.4 6.8 %fusion = f32[128,1792]{1,0:T(8,128)S(1)} fusion(bf16[8192,1792]{1,0:T(8,128)(2,1)} %param.9, bf16[128,4224]{1,0:T(8,128)(2,1)} %all-gather.6.cloned.1.call-done), kind=kOutput, calls=%fused_computation.1 | convolution fusion | flops 1879048192 | bytes 16646144 | tf_op jit(solution)/shard_map/dot_general | solution.py:36
  119.2 0.0 copy-done.3
  119.2 0.0 copy-start.2
  119.2 6.5 %fusion.4 = f32[128,1792]{1,0:T(8,128)S(1)} fusion(bf16[8192,1792]{1,0:T(8,128)(2,1)} %param.8, bf16[128,4224]{1,0:T(8,128)(2,1)S(1)} %copy-done.3), kind=kOutput, calls=%fused_computation.5 | convolution fusion | flops 1879048192 | bytes 16646144 | tf_op jit(solution)/shard_map/dot_general | solution.py:35
  125.7 0.0 copy-done.2
  125.7 6.5 %fusion.13 = f32[128,1792]{1,0:T(8,128)S(1)} fusion(f32[128,1792]{1,0:T(8,128)S(1)} %fusion.4, bf16[128,4096]{1,0:T(8,128)(2,1)S(1)} %copy-done.2, bf16[8192,1792]{1,0:T(8,128)(2,1)} %param.8), kind=kOutput, calls=%fused_computation.12 | convolution fusion | flops 1879277568 | bytes 17563648 | tf_op jit(solution)/shard_map/dot_general | solution.py:35
  132.2 0.0 copy-start.4
  132.2 0.0 copy-start.1
  132.2 6.6 %fusion.16 = f32[128,1792]{1,0:T(8,128)S(1)} fusion(f32[128,1792]{1,0:T(8,128)S(1)} %fusion, bf16[128,4096]{1,0:T(8,128)(2,1)S(1)} %copy-done.2, bf16[8192,1792]{1,0:T(8,128)(2,1)} %param.9), kind=kOutput, calls=%fused_computation.13 | convolution fusion | flops 1879277568 | bytes 17563648 | tf_op jit(solution)/shard_map/dot_general | solution.py:36
  138.9 0.0 copy-done.4
  138.9 3.2 %fusion.25 = bf16[128,1792]{1,0:T(8,128)(2,1)} fusion(f32[128,1792]{1,0:T(8,128)S(1)} %fusion.16, bf16[16,128,64]{1,0,2:T(8,128)(2,1)S(1)} %bitcast.31, bf16[16,64,1792]{2,1,0:T(8,128)(2,1)S(1)} %copy-done.4, f32[128,1792]{1,0:T(8,128)S(1)} %fusion.13), kind=kOutput, calls=%fused_computation.16 | convolution fusion | flops 471367680 | bytes 6225920 | tf_op jit(solution)/shard_map/str,srh->th/dot_general | solution.py:45
  142.1 0.0 copy-done.1
  (2 shorter events, 0.0 us)
Async XLA Ops:
  6.5 2.3 %copy-start = (s32[16]{0:T(128)S(1)}, s32[16]{0:T(128)}, u32[]{:S(2)}) copy-start(s32[16]{0:T(128)} %param.13) | copy-start | bytes 196
  6.5 43.7 %all-gather.4.cloned.1.call-start = ((), (), s32[]{:S(2)}) async-start(), calls=%async_computation | async-start | bytes 1114112 | tf_op jit(solution)/shard_map/all_gather | solution.py:31
  8.1 81.3 %all-gather.6.cloned.1.call-start = ((), (), s32[]{:S(2)}) async-start(), calls=%async_computation.1 | async-start | bytes 1148928 | tf_op jit(solution)/shard_map/all_gather | solution.py:31
  89.4 29.8 %copy-start.3 = (bf16[128,4224]{1,0:T(8,128)(2,1)S(1)}, bf16[128,4224]{1,0:T(8,128)(2,1)}, u32[]{:S(2)}) copy-start(bf16[128,4224]{1,0:T(8,128)(2,1)} %all-gather.6.cloned.1.call-done) | copy-start | bytes 3244036
  119.2 6.6 %copy-start.2 = (bf16[128,4096]{1,0:T(8,128)(2,1)S(1)}, bf16[128,4096]{1,0:T(8,128)(2,1)}, u32[]{:S(2)}) copy-start(bf16[128,4096]{1,0:T(8,128)(2,1)} %all-gather.4.cloned.1.call-done) | copy-start | bytes 3145732
  132.2 6.7 %copy-start.4 = (bf16[16,64,1792]{2,1,0:T(8,128)(2,1)S(1)}, bf16[16,64,1792]{2,1,0:T(8,128)(2,1)}, u32[]{:S(2)}) copy-start(bf16[16,64,1792]{2,1,0:T(8,128)(2,1)} %param.11) | copy-start | bytes 11010052
  132.2 9.8 %copy-start.1 = (s32[16]{0:T(128)S(1)}, s32[16]{0:T(128)}, u32[]{:S(2)}) copy-start(s32[16]{0:T(128)} %param.13) | copy-start | bytes 196
Sparse Core Ops, SparseCore 0:
  9.5 40.6 all-gather.3
  52.4 36.9 all-gather.5

commit v2 on v1

v2 whole, which is shorter than its diff:
```python
import jax
import jax.numpy as jnp
from jax import lax
from jax.sharding import PartitionSpec as P

LANES = 128
ASYNC_BYTES = 65536


def body(
    tokens,
    gate_weight,
    up_weight,
    adapter_down_weight,
    adapter_up_weight,
    token_adapter_index,
    adapter_slot_index,
):
    me = lax.axis_index("tensor")
    rows, width = tokens.shape
    local_slot = jnp.take(adapter_slot_index, token_adapter_index[:, 0], axis=0)
    slot_cols = jnp.broadcast_to(local_slot.astype(jnp.bfloat16)[:, None], (rows, LANES))
    gathered = lax.all_gather(jnp.concatenate([tokens, slot_cols], axis=1), "tensor", axis=0, tiled=True)
    slots = gathered[:, width].astype(jnp.int32)
    acts = gathered[:, :width]

    low = jnp.dot(acts, adapter_down_weight[0], preferred_element_type=jnp.float32)
    low = jnp.where((slots == me)[:, None], low, 0.0).astype(jnp.bfloat16)
    total, rank = low.shape
    padded = max(rank, -(-ASYNC_BYTES // (2 * total * LANES)) * LANES)
    low = jnp.pad(low, ((0, 0), (0, padded - rank)))
    spread = lax.all_gather(low, "tensor", axis=0, tiled=False)[:, :, :rank]

    gate = jnp.dot(acts, gate_weight, preferred_element_type=jnp.float32)
    up = jnp.dot(acts, up_weight, preferred_element_type=jnp.float32)
    gate, up = lax.optimization_barrier((gate, up))
    delta = jnp.einsum("str,srh->th", spread, adapter_up_weight, preferred_element_type=jnp.float32)
    return (jax.nn.silu(gate) * (up + delta)).astype(jnp.bfloat16)


def solution(mesh):
    in_specs = (
        P(("groups", "tensor"), None),
        P(None, "tensor"),
        P(None, "tensor"),
        P("tensor", None, None),
        P(None, None, "tensor"),
        P(("groups", "tensor"), None),
        P(),
    )
    out_specs = P("groups", "tensor")
    return jax.shard_map(body, mesh=mesh, in_specs=in_specs, out_specs=out_specs, check_vma=False)
```

time: 149 us -> 107 us (0.72)
  waiting for transfers between devices: 76.7 us -> 55.3 us
  blocking collectives: 20.1 us -> 0 us
  matrix products: 33.3 us -> 30.9 us
    all_gather x2, waiting for transfers between devices: 76.7 us -> 55.2 us  [the longest x1 44.3 us: body(): lax.all_gather(jnp.concatenate([tokens, slot_cols], axis=1), 'tensor', ax...]
    all_gather x1 -> x0, blocking collectives: 20.1 us -> none  [body(): spread = lax.all_gather(low, 'tensor', axis=0, tiled=False)]
    dot_general x6 -> x3, matrix products: 30.1 us -> 27.3 us  [the longest x1 12.4 us: body(): up = jnp.dot(acts, up_weight, preferred_element_type=jnp.float32)]
  transfers between devices with their start and end apart: 2 -> 2, of which waited for: 2 -> 2; matrix products, arithmetic and copies ran while one was open for 3% -> 23% of each run, Pallas kernels for 0% -> 0%
where the time goes in v2:
time: 107 us
  waiting for transfers between devices  55.3 us (52%)
  matrix products  30.9 us (29%)
  between operations  13.5 us (13%)
  other arithmetic  4.01 us (4%)
  local copies, waits for them, and re-layouts  3.5 us (3%)
    all_gather x1, waiting for transfers between devices, body(): lax.all_gather(jnp.concatenate([tokens, slot_cols], axis=1), 'tensor', ax...  44.3 us
    dot_general x1, matrix products, body(): up = jnp.dot(acts, up_weight, preferred_element_type=jnp.float32)  12.4 us
    dot_general x1, matrix products, body(): gate = jnp.dot(acts, gate_weight, preferred_element_type=jnp.float32)  12.4 us
    all_gather x1, waiting for transfers between devices, body(): spread = lax.all_gather(low, 'tensor', axis=0, tiled=False)[:, :, :rank]  11 us
    dot_general x1, matrix products, body(): jnp.einsum('str,srh->th', spread, adapter_up_weight, preferred_element_ty...  3.68 us
    dot_general x1, matrix products, body(): jnp.dot(acts, adapter_down_weight[0], preferred_element_type=jnp.float32)  2.43 us
  transfers between devices with their start and end apart: 2, of which 2 were waited for; matrix products, arithmetic and copies ran while one was open for 23% of the time, Pallas kernels for 0%

profile of v2, /device:TPU:0, one launch (start us, length us, event | category | flops | bytes accessed | tf_op | source)
XLA Modules:
  0.0 107.2 jit_solution(10720698346084021025)
XLA Ops:
  6.5 0.0 copy-start
  6.5 0.0 all-gather.4.cloned.1.call-start
  6.5 0.7 fusion.18
  7.3 1.3 %gather_fusion = s32[8]{0:T(128)S(1)} fusion(s32[16]{0:T(128)} %param.13, s32[1024]{0:T(1024)S(1)} %pad_clamp_fusion), kind=kCustom, calls=%fused_computation | custom fusion | bytes 96 | tf_op jit(solution)/shard_map/jit(_take)/gather | solution.py:21
  8.6 0.7 convert_bitcast_fusion
  9.3 0.1 broadcast_in_dim.26
  9.3 1.6 %pad_maximum_fusion = bf16[8,8320]{1,0:T(8,128)(2,1)} fusion(bf16[8,128]{1,0:T(8,128)(2,1)S(1)} %broadcast_in_dim.26, bf16[8,8192]{1,0:T(8,128)(2,1)} %param.7), kind=kLoop, calls=%fused_computation.15 | loop fusion | flops 266240 | bytes 266240 | tf_op jit(solution)/shard_map/concatenate | solution.py:23
  10.9 0.0 all-gather.4.cloned.1.call-update
  10.9 0.0 all-gather.6.cloned.1.call-start
  11.0 44.3 %all-gather.4.cloned.1.call-done = bf16[128,8320]{1,0:T(8,128)(2,1)} async-done(((bf16[8,8320]{1,0:T(8,128)(2,1)}), bf16[128,8320]{1,0:T(8,128)(2,1)}) %all-gather.4.cloned.1.call-update) | async-done | bytes 2129936 | tf_op jit(solution)/shard_map/all_gather | solution.py:23
  55.3 0.0 copy-start.2
  55.3 1.0 fusion.17
  56.3 0.0 copy-done
  56.3 2.4 %fusion.12 = bf16[128,64]{0,1:T(8,128)(2,1)S(1)} fusion(bf16[128,8320]{1,0:T(8,128)(2,1)} %all-gather.4.cloned.1.call-done, bf16[1,8192,64]{1,2,0:T(8,128)(2,1)S(1)} %copy-done, pred[128]{0:T(512)(128)(4,1)S(1)} %fusion.17), kind=kOutput, calls=%fused_computation.12 | convolution fusion | flops 134234112 | bytes 3162240 | tf_op jit(solution)/shard_map/dot_general | solution.py:27
  58.7 0.6 pad.4
  59.4 0.0 all-gather.6.cloned.1.call-update
  59.4 0.0 copy-done.2
  59.4 12.4 %fusion.5 = f32[128,1792]{1,0:T(8,128)} fusion(bf16[8192,1792]{1,0:T(8,128)(2,1)} %param.9, bf16[128,8320]{1,0:T(8,128)(2,1)S(1)} %copy-done.2), kind=kOutput, calls=%fused_computation.7 | convolution fusion | flops 3758096384 | bytes 32374784 | tf_op jit(solution)/shard_map/dot_general | solution.py:35
  71.8 12.4 %fusion.7 = f32[128,1792]{1,0:T(8,128)} fusion(bf16[8192,1792]{1,0:T(8,128)(2,1)} %param.8, bf16[128,8320]{1,0:T(8,128)(2,1)S(1)} %copy-done.2), kind=kOutput, calls=%fused_computation.9 | convolution fusion | flops 3758096384 | bytes 32374784 | tf_op jit(solution)/shard_map/dot_general | solution.py:34
  84.2 0.0 copy-start.3
  84.2 0.0 copy-start.4
  84.2 11.0 %all-gather.6.cloned.1.call-done = bf16[2048,256]{0,1:T(8,128)(2,1)} async-done(((bf16[128,256]{0,1:T(8,128)(2,1)}), bf16[2048,256]{0,1:T(8,128)(2,1)}) %all-gather.6.cloned.1.call-update) | async-done | bytes 1048592 | tf_op jit(solution)/shard_map/all_gather | solution.py:32
  95.2 1.4 %copy.11 = bf16[32,8,16,128]{3,2,1,0:T(8,128)(2,1)S(1)} copy(bf16[32,8,16,128]{3,1,2,0:T(8,128)(2,1)} %bitcast.27) | data formatting | bytes 2097152
  96.7 0.0 copy-start.1
  96.7 0.0 copy-done.3
  96.7 0.0 copy-done.4
  96.7 3.7 %fusion.2 = bf16[128,1792]{1,0:T(8,128)(2,1)} fusion(f32[128,1792]{1,0:T(8,128)S(1)} %copy-done.3, bf16[16,64,1792]{2,1,0:T(8,128)(2,1)} %param.11, f32[128,1792]{1,0:T(8,128)S(1)} %copy-done.4, bf16[16,128,64]{1,0,2:T(8,128)(2,1)S(1)} %slice.16), kind=kOutput, calls=%fused_computation.4 | convolution fusion | flops 471367680 | bytes 6225920 | tf_op jit(solution)/shard_map/str,srh->th/dot_general | solution.py:37
  100.4 0.0 copy-done.1
  (2 shorter events, 0.0 us)
Async XLA Ops:
  6.5 49.7 %copy-start = (bf16[1,8192,64]{1,2,0:T(8,128)(2,1)S(1)}, bf16[1,8192,64]{1,2,0:T(8,128)(2,1)}, u32[]{:S(2)}) copy-start(bf16[1,8192,64]{1,2,0:T(8,128)(2,1)} %param.10) | copy-start | bytes 3145732
  6.5 48.7 %all-gather.4.cloned.1.call-start = ((), (), s32[]{:S(2)}) async-start(), calls=%async_computation | async-start | bytes 2263040 | tf_op jit(solution)/shard_map/all_gather | solution.py:23
  10.9 84.3 %all-gather.6.cloned.1.call-start = ((), (), s32[]{:S(2)}) async-start(), calls=%async_computation.1 | async-start | bytes 1114112 | tf_op jit(solution)/shard_map/all_gather | solution.py:32
  55.3 4.1 %copy-start.2 = (bf16[128,8320]{1,0:T(8,128)(2,1)S(1)}, bf16[128,8320]{1,0:T(8,128)(2,1)}, u32[]{:S(2)}) copy-start(bf16[128,8320]{1,0:T(8,128)(2,1)} %all-gather.4.cloned.1.call-done) | copy-start | bytes 6389764
  84.2 12.5 %copy-start.3 = (f32[128,1792]{1,0:T(8,128)S(1)}, f32[128,1792]{1,0:T(8,128)}, u32[]{:S(2)}) copy-start(f32[128,1792]{1,0:T(8,128)} %fusion.5) | copy-start | bytes 2752516
  84.2 12.5 %copy-start.4 = (f32[128,1792]{1,0:T(8,128)S(1)}, f32[128,1792]{1,0:T(8,128)}, u32[]{:S(2)}) copy-start(f32[128,1792]{1,0:T(8,128)} %fusion.7) | copy-start | bytes 2752516
  96.7 3.7 %copy-start.1 = (bf16[1,8192,64]{1,2,0:T(8,128)(2,1)S(1)}, bf16[1,8192,64]{1,2,0:T(8,128)(2,1)}, u32[]{:S(2)}) copy-start(bf16[1,8192,64]{1,2,0:T(8,128)(2,1)} %param.10) | copy-start | bytes 3145732
Sparse Core Ops, SparseCore 0:
  11.0 44.1 all-gather.3
  59.5 35.6 all-gather.5

commit v3 on v2

v3 whole, which is shorter than its diff:
```python
import jax
import jax.numpy as jnp
from jax import lax
from jax.sharding import PartitionSpec as P

LANES = 128
ASYNC_BYTES = 65536


def body(
    tokens,
    gate_weight,
    up_weight,
    adapter_down_weight,
    adapter_up_weight,
    token_adapter_index,
    adapter_slot_index,
):
    rows, width = tokens.shape
    acts = lax.all_gather(tokens, "tensor", axis=0, tiled=True)
    total = acts.shape[0]
    slots_held = adapter_up_weight.shape[0]

    low = jnp.dot(acts, adapter_down_weight[0], preferred_element_type=jnp.float32).astype(jnp.bfloat16)
    rank = low.shape[1]
    local_slot = jnp.take(adapter_slot_index, token_adapter_index[:, 0], axis=0).astype(jnp.bfloat16)
    padded = max(rank + LANES, -(-ASYNC_BYTES // (2 * total * LANES)) * LANES)
    slot_col = jnp.zeros((total,), jnp.bfloat16).at[:rows].set(local_slot)
    payload = jnp.concatenate(
        [low, slot_col[:, None], jnp.zeros((total, padded - rank - 1), jnp.bfloat16)], axis=1
    )
    gathered = lax.all_gather(payload, "tensor", axis=0, tiled=False)
    slots = gathered[:, :rows, rank].reshape(total).astype(jnp.int32)
    hits = slots[None, :, None] == jnp.arange(slots_held, dtype=jnp.int32)[:, None, None]
    spread = jnp.where(hits, gathered[:, :, :rank], jnp.zeros((), jnp.bfloat16))

    gate = jnp.dot(acts, gate_weight, preferred_element_type=jnp.float32)
    up = jnp.dot(acts, up_weight, preferred_element_type=jnp.float32)
    gate, up = lax.optimization_barrier((gate, up))
    delta = jnp.einsum("str,srh->th", spread, adapter_up_weight, preferred_element_type=jnp.float32)
    return (jax.nn.silu(gate) * (up + delta)).astype(jnp.bfloat16)


def solution(mesh):
    in_specs = (
        P(("groups", "tensor"), None),
        P(None, "tensor"),
        P(None, "tensor"),
        P("tensor", None, None),
        P(None, None, "tensor"),
        P(("groups", "tensor"), None),
        P(),
    )
    out_specs = P("groups", "tensor")
    return jax.shard_map(body, mesh=mesh, in_specs=in_specs, out_specs=out_specs, check_vma=False)
```

time: 107 us -> 107 us (level)
  matrix products: 30.9 us -> 33.3 us
  other arithmetic: 4.01 us -> 2.08 us
    dot_general x1, matrix products: 3.68 us -> 5.84 us  [body(): jnp.einsum('str,srh->th', spread, adapter_up_weight, preferred_element_ty...]
  transfers between devices with their start and end apart: 2 -> 2, of which waited for: 2 -> 2; matrix products, arithmetic and copies ran while one was open for 23% -> 26% of each run, Pallas kernels for 0% -> 0%
where the time goes in v3:
time: 107 us
  waiting for transfers between devices  55.2 us (52%)
  matrix products  33.3 us (31%)
  between operations  13.5 us (13%)
  local copies, waits for them, and re-layouts  2.92 us (3%)
  other arithmetic  2.08 us (2%)
    all_gather x1, waiting for transfers between devices, body(): acts = lax.all_gather(tokens, 'tensor', axis=0, tiled=True)  43.6 us
    dot_general x1, matrix products, body(): gate = jnp.dot(acts, gate_weight, preferred_element_type=jnp.float32)  12.5 us
    dot_general x1, matrix products, body(): up = jnp.dot(acts, up_weight, preferred_element_type=jnp.float32)  12.4 us
    all_gather x1, waiting for transfers between devices, body(): gathered = lax.all_gather(payload, 'tensor', axis=0, tiled=False)  10.8 us
    dot_general x1, matrix products, body(): jnp.einsum('str,srh->th', spread, adapter_up_weight, preferred_element_ty...  5.84 us
    dot_general x1, matrix products, body(): jnp.dot(acts, adapter_down_weight[0], preferred_element_type=jnp.float32)  2.58 us
  transfers between devices with their start and end apart: 2, of which 2 were waited for; matrix products, arithmetic and copies ran while one was open for 26% of the time, Pallas kernels for 0%

profile of v3, /device:TPU:0, one launch (start us, length us, event | category | flops | bytes accessed | tf_op | source)
XLA Modules:
  0.0 107.0 jit_solution(7808899869573565267)
XLA Ops:
  6.5 0.0 copy-start
  6.5 0.0 all-gather.4.cloned.1.call-start
  6.5 0.7 all-gather.4.cloned.1.call-update
  7.3 0.0 all-gather.6.cloned.1.call-start
  7.3 0.7 fusion.23
  8.0 1.3 %gather_fusion = s32[8]{0:T(128)S(1)} fusion(s32[16]{0:T(128)} %param.15, s32[1024]{0:T(1024)S(1)} %pad_clamp_fusion), kind=kCustom, calls=%fused_computation | custom fusion | bytes 96 | tf_op jit(solution)/shard_map/jit(_take)/gather | solution.py:26
  9.3 0.1 pad.5.clone
  9.4 0.7 fusion.21
  10.0 43.6 %all-gather.4.cloned.1.call-done = bf16[128,8192]{1,0:T(8,128)(2,1)} async-done(((bf16[8,8192]{1,0:T(8,128)(2,1)}), bf16[128,8192]{1,0:T(8,128)(2,1)}) %all-gather.4.cloned.1.call-update) | async-done | bytes 2097168 | tf_op jit(solution)/shard_map/all_gather | solution.py:20
  53.7 0.0 copy-done
  53.7 0.0 copy-start.2
  53.7 2.6 %convolution_convert_fusion = bf16[128,64]{0,1:T(8,128)(2,1)S(1)} fusion(bf16[128,8192]{1,0:T(8,128)(2,1)} %all-gather.4.cloned.1.call-done, bf16[1,8192,64]{1,2,0:T(8,128)(2,1)S(1)} %copy-done), kind=kOutput, calls=%fused_computation.7 | convolution fusion | flops 134225920 | bytes 3162112 | tf_op jit(solution)/shard_map/dot_general | solution.py:24
  56.2 0.7 fusion.20
  57.0 0.0 all-gather.6.cloned.1.call-update
  57.0 0.0 copy-done.2
  57.0 12.5 %fusion.24 = f32[128,1792]{1,0:T(8,128)} fusion(bf16[128,8192]{1,0:T(8,128)(2,1)S(1)} %copy-done.2, bf16[8192,1792]{1,0:T(8,128)(2,1)} %param.10), kind=kOutput, calls=%fused_computation.26 | convolution fusion | flops 3758096384 | bytes 32374784 | tf_op jit(solution)/shard_map/dot_general | solution.py:37
  69.5 12.4 %fusion.25 = f32[128,1792]{1,0:T(8,128)} fusion(bf16[128,8192]{1,0:T(8,128)(2,1)S(1)} %copy-done.2, bf16[8192,1792]{1,0:T(8,128)(2,1)} %param.11), kind=kOutput, calls=%fused_computation.27 | convolution fusion | flops 3758096384 | bytes 32374784 | tf_op jit(solution)/shard_map/dot_general | solution.py:38
  81.9 10.8 %all-gather.6.cloned.1.call-done = bf16[2048,256]{0,1:T(8,128)(2,1)} async-done(((bf16[128,256]{0,1:T(8,128)(2,1)}), bf16[2048,256]{0,1:T(8,128)(2,1)}) %all-gather.6.cloned.1.call-update) | async-done | bytes 1048592 | tf_op jit(solution)/shard_map/all_gather | solution.py:32
  92.7 1.4 %copy.12 = bf16[32,8,16,128]{3,2,1,0:T(8,128)(2,1)S(1)} copy(bf16[32,8,16,128]{3,1,2,0:T(8,128)(2,1)} %bitcast.30) | data formatting | bytes 2097152
  94.2 0.1 reshape.60
  94.3 0.0 copy-start.1
  94.3 5.8 %fusion.11 = bf16[128,1792]{1,0:T(8,128)(2,1)} fusion(f32[128,1792]{1,0:T(8,128)} %fusion.25, bf16[16,64,1792]{2,1,0:T(8,128)(2,1)} %param.13, f32[128,1792]{1,0:T(8,128)} %fusion.24, bf16[16,128,256]{1,0,2:T(8,128)(2,1)S(1)} %bitcast.29, pred[16,128]{1,0:T(8,128)(4,1)S(1)} %iota_compare_fusion.2), kind=kOutput, calls=%fused_computation.6 | convolution fusion | flops 471498752 | bytes 6227968 | tf_op jit(solution)/shard_map/str,srh->th/dot_general | solution.py:40
  100.2 0.0 copy-done.1
  (4 shorter events, 0.0 us)
Async XLA Ops:
  6.5 47.1 %copy-start = (bf16[1,8192,64]{1,2,0:T(8,128)(2,1)S(1)}, bf16[1,8192,64]{1,2,0:T(8,128)(2,1)}, u32[]{:S(2)}) copy-start(bf16[1,8192,64]{1,2,0:T(8,128)(2,1)} %param.12) | copy-start | bytes 3145732
  6.5 47.1 %all-gather.4.cloned.1.call-start = ((), (), s32[]{:S(2)}) async-start(), calls=%async_computation | async-start | bytes 2228224 | tf_op jit(solution)/shard_map/all_gather | solution.py:20
  7.3 85.5 %all-gather.6.cloned.1.call-start = ((), (), s32[]{:S(2)}) async-start(), calls=%async_computation.1 | async-start | bytes 1114112 | tf_op jit(solution)/shard_map/all_gather | solution.py:32
  53.7 3.3 %copy-start.2 = (bf16[128,8192]{1,0:T(8,128)(2,1)S(1)}, bf16[128,8192]{1,0:T(8,128)(2,1)}, u32[]{:S(2)}) copy-start(bf16[128,8192]{1,0:T(8,128)(2,1)} %all-gather.4.cloned.1.call-done) | copy-start | bytes 6291460
  94.3 5.9 %copy-start.1 = (bf16[1,8192,64]{1,2,0:T(8,128)(2,1)S(1)}, bf16[1,8192,64]{1,2,0:T(8,128)(2,1)}, u32[]{:S(2)}) copy-start(bf16[1,8192,64]{1,2,0:T(8,128)(2,1)} %param.12) | copy-start | bytes 3145732
Sparse Core Ops, SparseCore 0:
  9.5 44.0 all-gather.3
  57.1 35.5 all-gather.5

commit v4 on v3

--- a/solution.py
+++ b/solution.py
@@ -4,7 +4,6 @@
 from jax.sharding import PartitionSpec as P
 
 LANES = 128
-ASYNC_BYTES = 65536
 
 
 def body(
@@ -24,12 +23,13 @@
     low = jnp.dot(acts, adapter_down_weight[0], preferred_element_type=jnp.float32).astype(jnp.bfloat16)
     rank = low.shape[1]
     local_slot = jnp.take(adapter_slot_index, token_adapter_index[:, 0], axis=0).astype(jnp.bfloat16)
-    padded = max(rank + LANES, -(-ASYNC_BYTES // (2 * total * LANES)) * LANES)
+    padded = -(-(rank + 1) // LANES) * LANES
     slot_col = jnp.zeros((total,), jnp.bfloat16).at[:rows].set(local_slot)
     payload = jnp.concatenate(
         [low, slot_col[:, None], jnp.zeros((total, padded - rank - 1), jnp.bfloat16)], axis=1
     )
-    gathered = lax.all_gather(payload, "tensor", axis=0, tiled=False)
+    copies = jnp.broadcast_to(payload[None], (slots_held,) + payload.shape)
+    gathered = lax.all_to_all(copies, "tensor", 0, 0, tiled=False)
     slots = gathered[:, :rows, rank].reshape(total).astype(jnp.int32)
     hits = slots[None, :, None] == jnp.arange(slots_held, dtype=jnp.int32)[:, None, None]
     spread = jnp.where(hits, gathered[:, :, :rank], jnp.zeros((), jnp.bfloat16))

time: 107 us -> 98 us (0.916)
  waiting for transfers between devices: 55.2 us -> 44.4 us
  starting transfers between devices: 0.04 us -> 3.57 us
  matrix products: 33.3 us -> 31.7 us
    all_gather x1 -> x0, waiting for transfers between devices: 10.8 us -> none  [body(): gathered = lax.all_gather(payload, 'tensor', axis=0, tiled=False)]
    all_to_all x0 -> x1, starting transfers between devices: none -> 3.57 us  [body(): gathered = lax.all_to_all(copies, 'tensor', 0, 0, tiled=False)]
    dot_general x1, matrix products: 5.84 us -> 4.29 us  [body(): jnp.einsum('str,srh->th', spread, adapter_up_weight, preferred_element_ty...]
  transfers between devices with their start and end apart: 2 -> 2, of which waited for: 2 -> 1; matrix products, arithmetic and copies ran while one was open for 26% -> 28% of each run, Pallas kernels for 0% -> 0%
where the time goes in v4:
time: 98 us; the launch traced here: 97.7 us
  waiting for transfers between devices  44.4 us (45%)
  matrix products  31.7 us (32%)
  between operations  13.5 us (14%)
  starting transfers between devices  3.57 us (4%)
  local copies, waits for them, and re-layouts  3.19 us (3%)
  other arithmetic  1.46 us (1%)
    all_gather x1, waiting for transfers between devices, body(): acts = lax.all_gather(tokens, 'tensor', axis=0, tiled=True)  43.7 us
    dot_general x1, matrix products, body(): gate = jnp.dot(acts, gate_weight, preferred_element_type=jnp.float32)  12.4 us
    dot_general x1, matrix products, body(): up = jnp.dot(acts, up_weight, preferred_element_type=jnp.float32)  12.4 us
    dot_general x1, matrix products, body(): jnp.einsum('str,srh->th', spread, adapter_up_weight, preferred_element_ty...  4.29 us
    all_to_all x1, starting transfers between devices, body(): gathered = lax.all_to_all(copies, 'tensor', 0, 0, tiled=False)  3.57 us
    dot_general x1, matrix products, body(): jnp.dot(acts, adapter_down_weight[0], preferred_element_type=jnp.float32)  2.58 us
  transfers between devices with their start and end apart: 2, of which 1 were waited for; matrix products, arithmetic and copies ran while one was open for 28% of the time, Pallas kernels for 0%

profile of v4, /device:TPU:0, one launch (start us, length us, event | category | flops | bytes accessed | tf_op | source)
XLA Modules:
  0.0 97.7 jit_solution(5120862423527606099)
XLA Ops:
  6.5 0.0 copy-start
  6.5 0.0 all-gather.2.cloned.1.call-start
  6.5 0.7 all-gather.2.cloned.1.call-update
  7.3 0.7 fusion.13
  7.9 1.3 %gather_fusion = s32[8]{0:T(128)S(1)} fusion(s32[16]{0:T(128)} %param.15, s32[1024]{0:T(1024)S(1)} %pad_clamp_fusion), kind=kCustom, calls=%fused_computation | custom fusion | bytes 96 | tf_op jit(solution)/shard_map/jit(_take)/gather | solution.py:25
  9.2 0.1 pad.5.clone
  9.3 0.7 fusion.11
  10.0 43.7 %all-gather.2.cloned.1.call-done = bf16[128,8192]{1,0:T(8,128)(2,1)} async-done(((bf16[8,8192]{1,0:T(8,128)(2,1)}), bf16[128,8192]{1,0:T(8,128)(2,1)}) %all-gather.2.cloned.1.call-update) | async-done | bytes 2097168 | tf_op jit(solution)/shard_map/all_gather | solution.py:19
  53.7 0.0 copy-done
  53.7 0.0 copy-start.2
  53.7 2.6 %convolution_convert_fusion = bf16[128,64]{0,1:T(8,128)(2,1)S(1)} fusion(bf16[128,8192]{1,0:T(8,128)(2,1)} %all-gather.2.cloned.1.call-done, bf16[1,8192,64]{1,2,0:T(8,128)(2,1)S(1)} %copy-done), kind=kOutput, calls=%fused_computation.5 | convolution fusion | flops 134225920 | bytes 3162112 | tf_op jit(solution)/shard_map/dot_general | solution.py:23
  56.2 0.1 fusion.9
  56.3 0.9 broadcast_in_dim.28
  57.2 3.6 %all-to-all-start = ((bf16[16,128,128]{1,2,0:T(8,128)(2,1)}), bf16[16,128,128]{1,2,0:T(8,128)(2,1)S(1)}, u32[]{:S(2)}, u32[]{:S(2)}) async-start(bf16[16,128,128]{1,2,0:T(8,128)(2,1)} %broadcast_in_dim.28), calls=%async_computation | async-start | bytes 1048576 | tf_op jit(solution)/shard_map/all_to_all | solution.py:32
  60.8 0.0 copy-done.2
  60.8 12.4 %fusion.14 = f32[128,1792]{1,0:T(8,128)} fusion(bf16[128,8192]{1,0:T(8,128)(2,1)S(1)} %copy-done.2, bf16[8192,1792]{1,0:T(8,128)(2,1)} %param.10), kind=kOutput, calls=%fused_computation.25 | convolution fusion | flops 3758096384 | bytes 32374784 | tf_op jit(solution)/shard_map/dot_general | solution.py:37
  73.2 12.4 %fusion.15 = f32[128,1792]{1,0:T(8,128)} fusion(bf16[128,8192]{1,0:T(8,128)(2,1)S(1)} %copy-done.2, bf16[8192,1792]{1,0:T(8,128)(2,1)} %param.11), kind=kOutput, calls=%fused_computation.26 | convolution fusion | flops 3758096384 | bytes 32374784 | tf_op jit(solution)/shard_map/dot_general | solution.py:38
  85.6 0.0 all-to-all-done
  85.6 0.0 copy-start.3
  85.6 0.8 copy-done.3
  86.5 0.1 reshape.61
  86.6 0.0 copy-start.1
  86.6 4.3 %fusion.2 = bf16[128,1792]{1,0:T(8,128)(2,1)} fusion(f32[128,1792]{1,0:T(8,128)} %fusion.15, bf16[16,64,1792]{2,1,0:T(8,128)(2,1)} %param.13, f32[128,1792]{1,0:T(8,128)} %fusion.14, bf16[16,128,128]{1,2,0:T(8,128)(2,1)} %copy-done.3, pred[16,128]{1,0:T(8,128)(4,1)S(1)} %iota_compare_fusion.2), kind=kOutput, calls=%fused_computation.4 | convolution fusion | flops 471498752 | bytes 6227968 | tf_op jit(solution)/shard_map/str,srh->th/dot_general | solution.py:40
  90.9 0.0 copy-done.1
  (4 shorter events, 0.0 us)
Async XLA Ops:
  6.5 47.1 %copy-start = (bf16[1,8192,64]{1,2,0:T(8,128)(2,1)S(1)}, bf16[1,8192,64]{1,2,0:T(8,128)(2,1)}, u32[]{:S(2)}) copy-start(bf16[1,8192,64]{1,2,0:T(8,128)(2,1)} %param.12) | copy-start | bytes 3145732
  6.5 47.1 %all-gather.2.cloned.1.call-start = ((), (), s32[]{:S(2)}) async-start(), calls=%async_computation.1 | async-start | bytes 2228224 | tf_op jit(solution)/shard_map/all_gather | solution.py:19
  53.7 7.2 %copy-start.2 = (bf16[128,8192]{1,0:T(8,128)(2,1)S(1)}, bf16[128,8192]{1,0:T(8,128)(2,1)}, u32[]{:S(2)}) copy-start(bf16[128,8192]{1,0:T(8,128)(2,1)} %all-gather.2.cloned.1.call-done) | copy-start | bytes 6291460
  57.2 28.4 %all-to-all-start = ((bf16[16,128,128]{1,2,0:T(8,128)(2,1)}), bf16[16,128,128]{1,2,0:T(8,128)(2,1)S(1)}, u32[]{:S(2)}, u32[]{:S(2)}) async-start(bf16[16,128,128]{1,2,0:T(8,128)(2,1)} %broadcast_in_dim.28), calls=%async_computation | async-start | bytes 1048576 | tf_op jit(solution)/shard_map/all_to_all | solution.py:32
  85.6 0.8 copy-start.3
  86.6 4.3 %copy-start.1 = (bf16[1,8192,64]{1,2,0:T(8,128)(2,1)S(1)}, bf16[1,8192,64]{1,2,0:T(8,128)(2,1)}, u32[]{:S(2)}) copy-start(bf16[1,8192,64]{1,2,0:T(8,128)(2,1)} %param.12) | copy-start | bytes 3145732
Sparse Core Ops, SparseCore 0:
  9.5 44.0 all-gather.1

commit v5 on v4

--- a/solution.py
+++ b/solution.py
@@ -1,9 +1,50 @@
 import jax
 import jax.numpy as jnp
 from jax import lax
+from jax.experimental import pallas as pl
+from jax.experimental.pallas import tpu as pltpu
 from jax.sharding import PartitionSpec as P
 
 LANES = 128
+BLOCK_ROWS = 1024
+
+
+def _projection_kernel(x_ref, gate_w_ref, up_w_ref, gate_ref, up_ref):
+    @pl.when(pl.program_id(0) == 0)
+    def _():
+        gate_ref[...] = jnp.zeros_like(gate_ref)
+        up_ref[...] = jnp.zeros_like(up_ref)
+
+    x = x_ref[...]
+    gate_ref[...] += jnp.dot(x, gate_w_ref[...], preferred_element_type=jnp.float32)
+    up_ref[...] += jnp.dot(x, up_w_ref[...], preferred_element_type=jnp.float32)
+
+
+def projections(acts, gate_weight, up_weight):
+    total, width = acts.shape
+    hidden = gate_weight.shape[1]
+    step = min(BLOCK_ROWS, width)
+    weight_bytes = 2 * width * hidden * gate_weight.dtype.itemsize
+    return pl.pallas_call(
+        _projection_kernel,
+        grid=(width // step,),
+        in_specs=[
+            pl.BlockSpec((total, step), lambda k: (0, k)),
+            pl.BlockSpec((step, hidden), lambda k: (k, 0)),
+            pl.BlockSpec((step, hidden), lambda k: (k, 0)),
+        ],
+        out_specs=[
+            pl.BlockSpec((total, hidden), lambda k: (0, 0)),
+            pl.BlockSpec((total, hidden), lambda k: (0, 0)),
+        ],
+        out_shape=[jax.ShapeDtypeStruct((total, hidden), jnp.float32)] * 2,
+        compiler_params=pltpu.CompilerParams(dimension_semantics=("arbitrary",)),
+        cost_estimate=pl.CostEstimate(
+            flops=4 * total * width * hidden,
+            transcendentals=0,
+            bytes_accessed=weight_bytes + total * width * 2 + 2 * total * hidden * 4,
+        ),
+    )(acts, gate_weight, up_weight)
 
 
 def body(
@@ -34,9 +75,7 @@
     hits = slots[None, :, None] == jnp.arange(slots_held, dtype=jnp.int32)[:, None, None]
     spread = jnp.where(hits, gathered[:, :, :rank], jnp.zeros((), jnp.bfloat16))
 
-    gate = jnp.dot(acts, gate_weight, preferred_element_type=jnp.float32)
-    up = jnp.dot(acts, up_weight, preferred_element_type=jnp.float32)
-    gate, up = lax.optimization_barrier((gate, up))
+    gate, up = projections(acts, gate_weight, up_weight)
     delta = jnp.einsum("str,srh->th", spread, adapter_up_weight, preferred_element_type=jnp.float32)
     return (jax.nn.silu(gate) * (up + delta)).astype(jnp.bfloat16)
 

time: 98 us -> 93.3 us (0.952)
  matrix products: 31.7 us -> 6.64 us
  Pallas kernels: 0 us -> 21.2 us
    dot_general x2 -> x0, matrix products: 24.8 us -> none  [the longest x1 12.4 us: body(): gate = jnp.dot(acts, gate_weight, preferred_element_type=jnp.float32)]
    pallas_call x0 -> x1, Pallas kernels: none -> 21.2 us  [projections(): pl.pallas_call(_projection_kernel, grid=(width // step,), in_specs=[pl.Bl...]
  transfers between devices with their start and end apart: 2 -> 2, of which waited for: 1 -> 1; matrix products, arithmetic and copies ran while one was open for 28% -> 3% of each run, Pallas kernels for 0% -> 23%
where the time goes in v5:
time: 93.3 us; the launch traced here: 93.1 us
  waiting for transfers between devices  44.4 us (48%)
  Pallas kernels  21.2 us (23%)
  between operations  13.4 us (14%)
  matrix products  6.64 us (7%)
  starting transfers between devices  3.57 us (4%)
  local copies, waits for them, and re-layouts  2.36 us (3%)
  other arithmetic  1.46 us (2%)
    all_gather x1, waiting for transfers between devices, body(): acts = lax.all_gather(tokens, 'tensor', axis=0, tiled=True)  43.7 us
    pallas_call x1, Pallas kernels, projections(): pl.pallas_call(_projection_kernel, grid=(width // step,), in_specs=[pl.Bl...  21.2 us
    dot_general x1, matrix products, body(): jnp.einsum('str,srh->th', spread, adapter_up_weight, preferred_element_ty...  4.21 us
    all_to_all x1, starting transfers between devices, body(): gathered = lax.all_to_all(copies, 'tensor', 0, 0, tiled=False)  3.57 us
    dot_general x1, matrix products, body(): jnp.dot(acts, adapter_down_weight[0], preferred_element_type=jnp.float32)  2.43 us
  transfers between devices with their start and end apart: 2, of which 1 were waited for; matrix products, arithmetic and copies ran while one was open for 3% of the time, Pallas kernels for 23%

profile of v5, /device:TPU:0, one launch (start us, length us, event | category | flops | bytes accessed | tf_op | source)
XLA Modules:
  0.0 93.1 jit_solution(17530325601575935810)
XLA Ops:
  6.5 0.0 copy-start
  6.5 0.0 all-gather.2.cloned.1.call-start
  6.5 0.7 all-gather.2.cloned.1.call-update
  7.3 0.7 fusion.13
  7.9 1.3 %gather_fusion = s32[8]{0:T(128)S(1)} fusion(s32[16]{0:T(128)} %param.15, s32[1024]{0:T(1024)S(1)} %pad_clamp_fusion), kind=kCustom, calls=%fused_computation | custom fusion | bytes 96 | tf_op jit(solution)/shard_map/jit(_take)/gather | solution.py:66
  9.2 0.1 pad.5.clone
  9.3 0.7 fusion.11
  10.0 43.7 %all-gather.2.cloned.1.call-done.x_ref = bf16[128,8192]{1,0:T(8,128)(2,1)} async-done(((bf16[8,8192]{1,0:T(8,128)(2,1)}), bf16[128,8192]{1,0:T(8,128)(2,1)}) %all-gather.2.cloned.1.call-update) | async-done | bytes 2097168 | tf_op jit(solution)/shard_map/all_gather | solution.py:60
  53.7 0.0 copy-done
  53.7 2.4 %convolution_convert_fusion = bf16[128,64]{0,1:T(8,128)(2,1)S(1)} fusion(bf16[128,8192]{1,0:T(8,128)(2,1)} %all-gather.2.cloned.1.call-done.x_ref, bf16[1,8192,64]{1,2,0:T(8,128)(2,1)S(1)} %copy-done), kind=kOutput, calls=%fused_computation.5 | convolution fusion | flops 134225920 | bytes 3162112 | tf_op jit(solution)/shard_map/dot_general | solution.py:64
  56.1 0.1 fusion.9
  56.2 0.9 broadcast_in_dim.28
  57.1 3.6 %all-to-all-start = ((bf16[16,128,128]{1,2,0:T(8,128)(2,1)}), bf16[16,128,128]{1,2,0:T(8,128)(2,1)S(1)}, u32[]{:S(2)}, u32[]{:S(2)}) async-start(bf16[16,128,128]{1,2,0:T(8,128)(2,1)} %broadcast_in_dim.28), calls=%async_computation | async-start | bytes 1048576 | tf_op jit(solution)/shard_map/all_to_all | solution.py:73
  60.6 21.2 %shard_map.73 = (f32[128,1792]{1,0:T(8,128)}, f32[128,1792]{1,0:T(8,128)}) custom-call(bf16[128,8192]{1,0:T(8,128)(2,1)} %all-gather.2.cloned.1.call-done.x_ref, bf16[8192,1792]{1,0:T(8,128)(2,1)} %gate_w_ref.1, bf16[8192,1792]{1,0:T(8,128)(2,1)} %up_w_ref.1), custom_call_target="tpu_custom_call" | custom-call | flops 7516192768 | bytes 62652416 | tf_op jit(solution)/shard_map/pallas_call | solution.py:28
  81.9 0.0 all-to-all-done
  81.9 0.1 reshape.61
  82.0 0.0 copy-start.1
  82.0 4.2 %fusion.2 = bf16[128,1792]{1,0:T(8,128)(2,1)} fusion(f32[128,1792]{1,0:T(8,128)} %get-tuple-element.20, bf16[16,64,1792]{2,1,0:T(8,128)(2,1)} %param.13, f32[128,1792]{1,0:T(8,128)} %get-tuple-element.19, bf16[16,128,128]{1,2,0:T(8,128)(2,1)S(1)} %all-to-all-done, pred[16,128]{1,0:T(8,128)(4,1)S(1)} %iota_compare_fusion.2), kind=kOutput, calls=%fused_computation.4 | convolution fusion | flops 471498752 | bytes 6227968 | tf_op jit(solution)/shard_map/str,srh->th/dot_general | solution.py:79
  86.2 0.0 copy-done.1
  (4 shorter events, 0.1 us)
Async XLA Ops:
  6.5 47.1 %copy-start = (bf16[1,8192,64]{1,2,0:T(8,128)(2,1)S(1)}, bf16[1,8192,64]{1,2,0:T(8,128)(2,1)}, u32[]{:S(2)}) copy-start(bf16[1,8192,64]{1,2,0:T(8,128)(2,1)} %param.12) | copy-start | bytes 3145732
  6.5 47.1 %all-gather.2.cloned.1.call-start = ((), (), s32[]{:S(2)}) async-start(), calls=%async_computation.1 | async-start | bytes 2228224 | tf_op jit(solution)/shard_map/all_gather | solution.py:60
  57.1 24.8 %all-to-all-start = ((bf16[16,128,128]{1,2,0:T(8,128)(2,1)}), bf16[16,128,128]{1,2,0:T(8,128)(2,1)S(1)}, u32[]{:S(2)}, u32[]{:S(2)}) async-start(bf16[16,128,128]{1,2,0:T(8,128)(2,1)} %broadcast_in_dim.28), calls=%async_computation | async-start | bytes 1048576 | tf_op jit(solution)/shard_map/all_to_all | solution.py:73
  82.0 4.2 %copy-start.1 = (bf16[1,8192,64]{1,2,0:T(8,128)(2,1)S(1)}, bf16[1,8192,64]{1,2,0:T(8,128)(2,1)}, u32[]{:S(2)}) copy-start(bf16[1,8192,64]{1,2,0:T(8,128)(2,1)} %param.12) | copy-start | bytes 3145732
Sparse Core Ops, SparseCore 0:
  9.5 44.0 all-gather.1

commit v6 on v5

--- a/solution.py
+++ b/solution.py
@@ -9,30 +9,44 @@
 BLOCK_ROWS = 1024
 
 
-def _projection_kernel(x_ref, gate_w_ref, up_w_ref, gate_ref, up_ref):
+def _projection_kernel(x_ref, gate_w_ref, up_w_ref, *refs):
+    if len(refs) == 4:
+        gate_in_ref, up_in_ref, gate_ref, up_ref = refs
+    else:
+        gate_in_ref = up_in_ref = None
+        gate_ref, up_ref = refs
+
     @pl.when(pl.program_id(0) == 0)
     def _():
-        gate_ref[...] = jnp.zeros_like(gate_ref)
-        up_ref[...] = jnp.zeros_like(up_ref)
+        if gate_in_ref is None:
+            gate_ref[...] = jnp.zeros_like(gate_ref)
+            up_ref[...] = jnp.zeros_like(up_ref)
+        else:
+            gate_ref[...] = gate_in_ref[...]
+            up_ref[...] = up_in_ref[...]
 
     x = x_ref[...]
     gate_ref[...] += jnp.dot(x, gate_w_ref[...], preferred_element_type=jnp.float32)
     up_ref[...] += jnp.dot(x, up_w_ref[...], preferred_element_type=jnp.float32)
 
 
-def projections(acts, gate_weight, up_weight):
+def projections(acts, gate_weight, up_weight, first_row, partial=None):
     total, width = acts.shape
     hidden = gate_weight.shape[1]
     step = min(BLOCK_ROWS, width)
+    offset = first_row // step
     weight_bytes = 2 * width * hidden * gate_weight.dtype.itemsize
+    extra_specs = [] if partial is None else [pl.BlockSpec((total, hidden), lambda k: (0, 0))] * 2
+    extra_args = () if partial is None else tuple(partial)
     return pl.pallas_call(
         _projection_kernel,
         grid=(width // step,),
         in_specs=[
             pl.BlockSpec((total, step), lambda k: (0, k)),
-            pl.BlockSpec((step, hidden), lambda k: (k, 0)),
-            pl.BlockSpec((step, hidden), lambda k: (k, 0)),
-        ],
+            pl.BlockSpec((step, hidden), lambda k: (k + offset, 0)),
+            pl.BlockSpec((step, hidden), lambda k: (k + offset, 0)),
+        ]
+        + extra_specs,
         out_specs=[
             pl.BlockSpec((total, hidden), lambda k: (0, 0)),
             pl.BlockSpec((total, hidden), lambda k: (0, 0)),
@@ -44,7 +58,7 @@
             transcendentals=0,
             bytes_accessed=weight_bytes + total * width * 2 + 2 * total * hidden * 4,
         ),
-    )(acts, gate_weight, up_weight)
+    )(acts, gate_weight, up_weight, *extra_args)
 
 
 def body(
@@ -57,11 +71,17 @@
     adapter_slot_index,
 ):
     rows, width = tokens.shape
-    acts = lax.all_gather(tokens, "tensor", axis=0, tiled=True)
-    total = acts.shape[0]
     slots_held = adapter_up_weight.shape[0]
+    half = width // 2
+    acts_a = lax.all_gather(tokens[:, :half], "tensor", axis=0, tiled=True)
+    copies = jnp.broadcast_to(tokens[None, :, half:], (slots_held, rows, width - half))
+    acts_b = lax.all_to_all(copies, "tensor", 0, 0, tiled=False).reshape(slots_held * rows, width - half)
+    total = acts_a.shape[0]
 
-    low = jnp.dot(acts, adapter_down_weight[0], preferred_element_type=jnp.float32).astype(jnp.bfloat16)
+    down = adapter_down_weight[0]
+    low = jnp.dot(acts_a, down[:half], preferred_element_type=jnp.float32)
+    low = low + jnp.dot(acts_b, down[half:], preferred_element_type=jnp.float32)
+    low = low.astype(jnp.bfloat16)
     rank = low.shape[1]
     local_slot = jnp.take(adapter_slot_index, token_adapter_index[:, 0], axis=0).astype(jnp.bfloat16)
     padded = -(-(rank + 1) // LANES) * LANES
@@ -75,7 +95,8 @@
     hits = slots[None, :, None] == jnp.arange(slots_held, dtype=jnp.int32)[:, None, None]
     spread = jnp.where(hits, gathered[:, :, :rank], jnp.zeros((), jnp.bfloat16))
 
-    gate, up = projections(acts, gate_weight, up_weight)
+    partial = projections(acts_b, gate_weight, up_weight, half)
+    gate, up = projections(acts_a, gate_weight, up_weight, 0, partial)
     delta = jnp.einsum("str,srh->th", spread, adapter_up_weight, preferred_element_type=jnp.float32)
     return (jax.nn.silu(gate) * (up + delta)).astype(jnp.bfloat16)
 

time: 93.3 us -> 102 us (1.093)
  starting transfers between devices: 3.57 us -> 11 us
  Pallas kernels: 21.2 us -> 25.8 us
  waiting for transfers between devices: 44.4 us -> 40 us
  local copies, waits for them, and re-layouts: 2.36 us -> 4.45 us
    all_to_all x0 -> x1, starting transfers between devices: none -> 7.39 us  [body(): lax.all_to_all(copies, 'tensor', 0, 0, tiled=False)]
    pallas_call x1 -> x2, Pallas kernels: 21.2 us -> 25.8 us  [projections(): pl.pallas_call(_projection_kernel, grid=(width // step,), in_specs=[pl.Bl...]
    all_gather x1, waiting for transfers between devices: 43.7 us -> 39.9 us  [body(): acts_a = lax.all_gather(tokens[:, :half], 'tensor', axis=0, tiled=True)]
    slice x0 -> x1, local copies, waits for them, and re-layouts: none -> 1.6 us  [body(): tokens[None, :, half:]]
    broadcast_in_dim x0 -> x1, local copies, waits for them, and re-layouts: none -> 1.11 us  [body(): jnp.broadcast_to(tokens[None, :, half:], (slots_held, rows, width - half))]
    dot_general x1 -> x2, matrix products: 2.43 us -> 2.19 us  [the longest x1 1.71 us: body(): low = jnp.dot(acts_a, down[:half], preferred_element_type=jnp.float32)]
  transfers between devices with their start and end apart: 2 -> 3, of which waited for: 1 -> 1; matrix products, arithmetic and copies ran while one was open for 3% -> 4% of each run, Pallas kernels for 23% -> 25%
where the time goes in v6:
time: 102 us
  waiting for transfers between devices  40 us (39%)
  Pallas kernels  25.8 us (25%)
  between operations  13.5 us (13%)
  starting transfers between devices  11 us (11%)
  matrix products  6.32 us (6%)
  local copies, waits for them, and re-layouts  4.45 us (4%)
    all_gather x1, waiting for transfers between devices, body(): acts_a = lax.all_gather(tokens[:, :half], 'tensor', axis=0, tiled=True)  39.9 us
    pallas_call x2, Pallas kernels, projections(): pl.pallas_call(_projection_kernel, grid=(width // step,), in_specs=[pl.Bl...  25.8 us
    all_to_all x1, starting transfers between devices, body(): lax.all_to_all(copies, 'tensor', 0, 0, tiled=False)  7.39 us
    dot_general x1, matrix products, body(): jnp.einsum('str,srh->th', spread, adapter_up_weight, preferred_element_ty...  4.13 us
    all_to_all x1, starting transfers between devices, body(): gathered = lax.all_to_all(copies, 'tensor', 0, 0, tiled=False)  3.62 us
  transfers between devices with their start and end apart: 3, of which 1 were waited for; matrix products, arithmetic and copies ran while one was open for 4% of the time, Pallas kernels for 25%

profile of v6, /device:TPU:0, one launch (start us, length us, event | category | flops | bytes accessed | tf_op | source)
XLA Modules:
  0.0 101.9 jit_solution(16820388434743861505)
XLA Ops:
  6.5 0.0 copy-start
  6.5 0.0 copy-start.4
  6.5 0.0 copy-start.3
  6.5 0.0 all-gather.2.cloned.1.call-start
  6.5 1.6 %fusion.20 = (bf16[8,4096]{1,0:T(8,128)(2,1)S(1)}, bf16[8,4096]{1,0:T(8,128)(2,1)}) fusion(bf16[8,8192]{1,0:T(8,128)(2,1)} %param.9), kind=kLoop, calls=%fused_computation.31 | loop fusion | bytes 262144 | tf_op jit(solution)/shard_map/slice | solution.py:77
  8.1 0.0 all-gather.2.cloned.1.call-update
  8.2 1.1 %broadcast_in_dim.16 = bf16[16,8,4096]{2,1,0:T(8,128)(2,1)} broadcast(bf16[8,4096]{1,0:T(8,128)(2,1)S(1)} %get-tuple-element.25), dimensions={1,2} | broadcast | bytes 1114112 | tf_op jit(solution)/shard_map/broadcast_in_dim | solution.py:77
  9.3 7.4 %all-to-all-start = ((bf16[16,8,4096]{2,1,0:T(8,128)(2,1)}), bf16[16,8,4096]{2,1,0:T(8,128)(2,1)S(1)}, u32[]{:S(2)}, u32[]{:S(2)}) async-start(bf16[16,8,4096]{2,1,0:T(8,128)(2,1)} %broadcast_in_dim.16), calls=%async_computation | async-start | bytes 2097152 | tf_op jit(solution)/shard_map/all_to_all | solution.py:78
  16.7 0.1 pad.5.clone
  16.8 0.7 fusion.19
  17.4 0.0 copy-done
  17.4 0.6 gather_fusion
  18.1 0.0 copy-done.4
  18.1 39.9 %all-gather.2.cloned.1.call-done.x_ref = bf16[128,4096]{1,0:T(8,128)(2,1)} async-done(((bf16[8,4096]{1,0:T(8,128)(2,1)}), bf16[128,4096]{1,0:T(8,128)(2,1)}) %all-gather.2.cloned.1.call-update) | async-done | bytes 1048592 | tf_op jit(solution)/shard_map/all_gather | solution.py:76
  58.0 0.0 copy-done.3
  58.0 1.7 %fusion.5 = f32[128,64]{0,1:T(8,128)S(1)} fusion(bf16[128,4096]{1,0:T(8,128)(2,1)} %all-gather.2.cloned.1.call-done.x_ref, bf16[1,8192,64]{1,2,0:T(8,128)(2,1)S(1)} %copy-done.3), kind=kOutput, calls=%fused_computation.8 | convolution fusion | flops 67108864 | bytes 1605632 | tf_op jit(solution)/shard_map/dot_general | solution.py:82
  59.8 0.0 all-to-all-done
  59.8 0.0 copy-start.2
  59.8 0.5 fusion.3
  60.3 0.1 fusion.14
  60.4 0.9 broadcast_in_dim.18
  61.3 3.6 %all-to-all-start.1 = ((bf16[16,128,128]{1,2,0:T(8,128)(2,1)}), bf16[16,128,128]{1,2,0:T(8,128)(2,1)S(1)}, u32[]{:S(2)}, u32[]{:S(2)}) async-start(bf16[16,128,128]{1,2,0:T(8,128)(2,1)} %broadcast_in_dim.18), calls=%async_computation.1 | async-start | bytes 1048576 | tf_op jit(solution)/shard_map/all_to_all | solution.py:93
  64.9 0.0 copy-done.2
  64.9 12.2 %shard_map.73 = (f32[128,1792]{1,0:T(8,128)}, f32[128,1792]{1,0:T(8,128)}) custom-call(bf16[128,4096]{1,0:T(8,128)(2,1)} %bitcast.25, bf16[8192,1792]{1,0:T(8,128)(2,1)} %gate_w_ref.3, bf16[8192,1792]{1,0:T(8,128)(2,1)} %up_w_ref.3), custom_call_target="tpu_custom_call" | custom-call | flops 3758096384 | bytes 32243712 | tf_op jit(solution)/shard_map/pallas_call | solution.py:41
  77.1 13.7 %shard_map.74 = (f32[128,1792]{1,0:T(8,128)}, f32[128,1792]{1,0:T(8,128)}) custom-call(bf16[128,4096]{1,0:T(8,128)(2,1)} %all-gather.2.cloned.1.call-done.x_ref, bf16[8192,1792]{1,0:T(8,128)(2,1)} %gate_w_ref.3, bf16[8192,1792]{1,0:T(8,128)(2,1)} %up_w_ref.3, f32[128,1792]{1,0:T(8,128)} %get-tuple-element.21.refs_0_, f32[128,1792]{1,0:T(8,128)} %get-tuple-element.22.refs_1_), custom_call_target="tpu_custom_call" | custom-call | flops 3758096384 | bytes 32243712 | tf_op jit(solution)/shard_map/pallas_call | solution.py:41
  90.7 0.0 all-to-all-done.1
  90.8 0.1 reshape.68
  90.9 0.0 copy-start.1
  90.9 4.1 %fusion.2 = bf16[128,1792]{1,0:T(8,128)(2,1)} fusion(f32[128,1792]{1,0:T(8,128)} %get-tuple-element.24, bf16[16,64,1792]{2,1,0:T(8,128)(2,1)} %param.13, f32[128,1792]{1,0:T(8,128)} %get-tuple-element.23, bf16[16,128,128]{1,2,0:T(8,128)(2,1)S(1)} %all-to-all-done.1, pred[16,128]{1,0:T(8,128)(4,1)S(1)} %iota_compare_fusion.2), kind=kOutput, calls=%fused_computation.4 | convolution fusion | flops 471498752 | bytes 6227968 | tf_op jit(solution)/shard_map/str,srh->th/dot_general | solution.py:100
  95.0 0.0 copy-done.1
  (5 shorter events, 0.1 us)
Async XLA Ops:
  6.5 10.9 %copy-start = (s32[16]{0:T(128)S(1)}, s32[16]{0:T(128)}, u32[]{:S(2)}) copy-start(s32[16]{0:T(128)} %param.15) | copy-start | bytes 196
  6.5 11.5 %copy-start.4 = (s32[8,1]{0,1:T(1,128)S(1)}, s32[8,1]{0,1:T(1,128)}, u32[]{:S(2)}) copy-start(s32[8,1]{0,1:T(1,128)} %param.14) | copy-start | bytes 100
  6.5 51.5 %copy-start.3 = (bf16[1,8192,64]{1,2,0:T(8,128)(2,1)S(1)}, bf16[1,8192,64]{1,2,0:T(8,128)(2,1)}, u32[]{:S(2)}) copy-start(bf16[1,8192,64]{1,2,0:T(8,128)(2,1)} %param.12) | copy-start | bytes 3145732
  6.5 51.5 %all-gather.2.cloned.1.call-start = ((), (), s32[]{:S(2)}) async-start(), calls=%async_computation.2 | async-start | bytes 1114112 | tf_op jit(solution)/shard_map/all_gather | solution.py:76
  9.3 50.5 %all-to-all-start = ((bf16[16,8,4096]{2,1,0:T(8,128)(2,1)}), bf16[16,8,4096]{2,1,0:T(8,128)(2,1)S(1)}, u32[]{:S(2)}, u32[]{:S(2)}) async-start(bf16[16,8,4096]{2,1,0:T(8,128)(2,1)} %broadcast_in_dim.16), calls=%async_computation | async-start | bytes 2097152 | tf_op jit(solution)/shard_map/all_to_all | solution.py:78
  59.8 5.1 %copy-start.2 = (bf16[16,8,4096]{2,1,0:T(8,128)(2,1)}, bf16[16,8,4096]{2,1,0:T(8,128)(2,1)S(1)}, u32[]{:S(2)}) copy-start(bf16[16,8,4096]{2,1,0:T(8,128)(2,1)S(1)} %all-to-all-done) | copy-start | bytes 3145732
  61.3 29.5 %all-to-all-start.1 = ((bf16[16,128,128]{1,2,0:T(8,128)(2,1)}), bf16[16,128,128]{1,2,0:T(8,128)(2,1)S(1)}, u32[]{:S(2)}, u32[]{:S(2)}) async-start(bf16[16,128,128]{1,2,0:T(8,128)(2,1)} %broadcast_in_dim.18), calls=%async_computation.1 | async-start | bytes 1048576 | tf_op jit(solution)/shard_map/all_to_all | solution.py:93
  90.9 4.1 %copy-start.1 = (s32[16]{0:T(128)S(1)}, s32[16]{0:T(128)}, u32[]{:S(2)}) copy-start(s32[16]{0:T(128)} %param.15) | copy-start | bytes 196
Sparse Core Ops, SparseCore 0:
  9.5 48.4 all-gather.1

commit v7 on v5

--- a/solution.py
+++ b/solution.py
@@ -57,9 +57,10 @@
     adapter_slot_index,
 ):
     rows, width = tokens.shape
-    acts = lax.all_gather(tokens, "tensor", axis=0, tiled=True)
+    slots_held = adapter_up_weight.shape[0]
+    copies = jnp.broadcast_to(tokens[None], (slots_held,) + tokens.shape)
+    acts = lax.all_to_all(copies, "tensor", 0, 0, tiled=False).reshape(slots_held * rows, width)
     total = acts.shape[0]
-    slots_held = adapter_up_weight.shape[0]
 
     low = jnp.dot(acts, adapter_down_weight[0], preferred_element_type=jnp.float32).astype(jnp.bfloat16)
     rank = low.shape[1]

time: 93.3 us -> 90.9 us (0.974)
  starting transfers between devices: 3.57 us -> 18.6 us
  between operations: 13.4 us -> 0.1 us
  waiting for transfers between devices: 44.4 us -> 40.3 us
  local copies, waits for them, and re-layouts: 2.36 us -> 5.06 us
  matrix products: 6.64 us -> 5.14 us
  other arithmetic: 1.46 us -> 0.14 us
    all_gather x1 -> x0, waiting for transfers between devices: 43.7 us -> none  [body(): acts = lax.all_gather(tokens, 'tensor', axis=0, tiled=True)]
    all_to_all x0 -> x1, waiting for transfers between devices: none -> 40.3 us  [body(): lax.all_to_all(copies, 'tensor', 0, 0, tiled=False)]
    all_to_all x1, starting transfers between devices: 3.57 us -> 11.2 us  [body(): gathered = lax.all_to_all(copies, 'tensor', 0, 0, tiled=False)]
    all_to_all x0 -> x1, starting transfers between devices: none -> 7.39 us  [body(): lax.all_to_all(copies, 'tensor', 0, 0, tiled=False)]
    broadcast_in_dim x0 -> x1, local copies, waits for them, and re-layouts: none -> 2.54 us  [body(): copies = jnp.broadcast_to(tokens[None], (slots_held,) + tokens.shape)]
    dot_general x1, matrix products: 2.43 us -> 0.84 us  [body(): jnp.dot(acts, adapter_down_weight[0], preferred_element_type=jnp.float32)]
  transfers between devices with their start and end apart: 2 -> 2, of which waited for: 1 -> 1; matrix products, arithmetic and copies ran while one was open for 3% -> 1% of each run, Pallas kernels for 23% -> 23%
where the time goes in v7:
time: 90.9 us; the launch traced here: 90.6 us
  waiting for transfers between devices  40.3 us (44%)
  Pallas kernels  21.2 us (23%)
  starting transfers between devices  18.6 us (20%)
  matrix products  5.14 us (6%)
  local copies, waits for them, and re-layouts  5.06 us (6%)
    all_to_all x1, waiting for transfers between devices, body(): lax.all_to_all(copies, 'tensor', 0, 0, tiled=False)  40.3 us
    pallas_call x1, Pallas kernels, projections(): pl.pallas_call(_projection_kernel, grid=(width // step,), in_specs=[pl.Bl...  21.2 us
    all_to_all x1, starting transfers between devices, body(): gathered = lax.all_to_all(copies, 'tensor', 0, 0, tiled=False)  11.2 us
    all_to_all x1, starting transfers between devices, body(): lax.all_to_all(copies, 'tensor', 0, 0, tiled=False)  7.39 us
    dot_general x1, matrix products, body(): jnp.einsum('str,srh->th', spread, adapter_up_weight, preferred_element_ty...  4.29 us
    broadcast_in_dim x1, local copies, waits for them, and re-layouts, body(): copies = jnp.broadcast_to(tokens[None], (slots_held,) + tokens.shape)  2.54 us
  transfers between devices with their start and end apart: 2, of which 1 were waited for; matrix products, arithmetic and copies ran while one was open for 1% of the time, Pallas kernels for 23%

profile of v7, /device:TPU:0, one launch (start us, length us, event | category | flops | bytes accessed | tf_op | source)
XLA Modules:
  0.0 90.6 jit_solution(672874000264821873)
XLA Ops:
  0.0 0.0 copy-start
  0.0 0.0 copy-start.5
  0.0 0.0 copy-start.2
  0.0 2.5 %broadcast_in_dim.16 = bf16[16,8,8192]{2,1,0:T(8,128)(2,1)} broadcast(bf16[8,8192]{1,0:T(8,128)(2,1)} %param.9), dimensions={1,2} | broadcast | bytes 2228224 | tf_op jit(solution)/shard_map/broadcast_in_dim | solution.py:61
  2.5 7.4 %all-to-all-start = ((bf16[16,8,8192]{2,1,0:T(8,128)(2,1)}), bf16[16,8,8192]{2,1,0:T(8,128)(2,1)S(1)}, u32[]{:S(2)}, u32[]{:S(2)}) async-start(bf16[16,8,8192]{2,1,0:T(8,128)(2,1)} %broadcast_in_dim.16), calls=%async_computation | async-start | bytes 4194304 | tf_op jit(solution)/shard_map/all_to_all | solution.py:62
  9.9 0.0 copy-done.5
  10.0 0.0 copy-done.2
  10.0 0.6 gather_fusion
  10.6 0.1 pad.5.clone
  10.7 40.3 %all-to-all-done = bf16[16,8,8192]{2,1,0:T(8,128)(2,1)S(1)} async-done(((bf16[16,8,8192]{2,1,0:T(8,128)(2,1)}), bf16[16,8,8192]{2,1,0:T(8,128)(2,1)S(1)}, u32[]{:S(2)}, u32[]{:S(2)}) %all-to-all-start) | async-done | bytes 2097184 | tf_op jit(solution)/shard_map/all_to_all | solution.py:62
  51.0 0.0 copy-done
  51.1 0.0 copy-start.3
  51.1 0.8 convolution_convert_fusion
  51.9 0.1 fusion.9
  52.0 0.9 broadcast_in_dim.18
  52.9 11.2 %all-to-all-start.1 = ((bf16[16,128,128]{1,2,0:T(8,128)(2,1)}), bf16[16,128,128]{1,2,0:T(8,128)(2,1)S(1)}, u32[]{:S(2)}, u32[]{:S(2)}) async-start(bf16[16,128,128]{1,2,0:T(8,128)(2,1)} %broadcast_in_dim.18), calls=%async_computation.1 | async-start | bytes 1048576 | tf_op jit(solution)/shard_map/all_to_all | solution.py:74
  64.1 0.0 copy-done.3
  64.1 21.2 %shard_map.73 = (f32[128,1792]{1,0:T(8,128)}, f32[128,1792]{1,0:T(8,128)}) custom-call(bf16[128,8192]{1,0:T(8,128)(2,1)} %bitcast.21, bf16[8192,1792]{1,0:T(8,128)(2,1)} %gate_w_ref.1, bf16[8192,1792]{1,0:T(8,128)(2,1)} %up_w_ref.1), custom_call_target="tpu_custom_call" | custom-call | flops 7516192768 | bytes 62652416 | tf_op jit(solution)/shard_map/pallas_call | solution.py:28
  85.3 0.0 all-to-all-done.1
  85.3 0.0 copy-start.4
  85.3 0.8 copy-done.4
  86.2 0.1 reshape.66
  86.3 0.0 copy-start.1
  86.3 4.3 %fusion.2 = bf16[128,1792]{1,0:T(8,128)(2,1)} fusion(f32[128,1792]{1,0:T(8,128)} %get-tuple-element.20, bf16[16,64,1792]{2,1,0:T(8,128)(2,1)} %param.13, f32[128,1792]{1,0:T(8,128)} %get-tuple-element.19, bf16[16,128,128]{1,2,0:T(8,128)(2,1)} %copy-done.4, pred[16,128]{1,0:T(8,128)(4,1)S(1)} %iota_compare_fusion.2), kind=kOutput, calls=%fused_computation.4 | convolution fusion | flops 471498752 | bytes 6227968 | tf_op jit(solution)/shard_map/str,srh->th/dot_general | solution.py:80
  90.6 0.0 copy-done.1
  (6 shorter events, 0.1 us)
Async XLA Ops:
  0.0 51.1 %copy-start = (bf16[1,8192,64]{1,2,0:T(8,128)(2,1)S(1)}, bf16[1,8192,64]{1,2,0:T(8,128)(2,1)}, u32[]{:S(2)}) copy-start(bf16[1,8192,64]{1,2,0:T(8,128)(2,1)} %param.12) | copy-start | bytes 3145732
  0.0 9.9 %copy-start.5 = (s32[8,1]{0,1:T(1,128)S(1)}, s32[8,1]{0,1:T(1,128)}, u32[]{:S(2)}) copy-start(s32[8,1]{0,1:T(1,128)} %param.14) | copy-start | bytes 100
  0.0 10.0 %copy-start.2 = (s32[16]{0:T(128)S(1)}, s32[16]{0:T(128)}, u32[]{:S(2)}) copy-start(s32[16]{0:T(128)} %param.15) | copy-start | bytes 196
  2.5 48.5 %all-to-all-start = ((bf16[16,8,8192]{2,1,0:T(8,128)(2,1)}), bf16[16,8,8192]{2,1,0:T(8,128)(2,1)S(1)}, u32[]{:S(2)}, u32[]{:S(2)}) async-start(bf16[16,8,8192]{2,1,0:T(8,128)(2,1)} %broadcast_in_dim.16), calls=%async_computation | async-start | bytes 4194304 | tf_op jit(solution)/shard_map/all_to_all | solution.py:62
  51.1 13.1 %copy-start.3 = (bf16[16,8,8192]{2,1,0:T(8,128)(2,1)}, bf16[16,8,8192]{2,1,0:T(8,128)(2,1)S(1)}, u32[]{:S(2)}) copy-start(bf16[16,8,8192]{2,1,0:T(8,128)(2,1)S(1)} %all-to-all-done) | copy-start | bytes 6291460
  52.9 32.5 %all-to-all-start.1 = ((bf16[16,128,128]{1,2,0:T(8,128)(2,1)}), bf16[16,128,128]{1,2,0:T(8,128)(2,1)S(1)}, u32[]{:S(2)}, u32[]{:S(2)}) async-start(bf16[16,128,128]{1,2,0:T(8,128)(2,1)} %broadcast_in_dim.18), calls=%async_computation.1 | async-start | bytes 1048576 | tf_op jit(solution)/shard_map/all_to_all | solution.py:74
  85.3 0.8 copy-start.4
  86.3 4.3 %copy-start.1 = (bf16[1,8192,64]{1,2,0:T(8,128)(2,1)S(1)}, bf16[1,8192,64]{1,2,0:T(8,128)(2,1)}, u32[]{:S(2)}) copy-start(bf16[1,8192,64]{1,2,0:T(8,128)(2,1)} %param.12) | copy-start | bytes 3145732

commit v8 on v4

v8 whole, which is shorter than its diff:
```python
import jax
import jax.numpy as jnp
from jax import lax
from jax.experimental import pallas as pl
from jax.experimental.pallas import tpu as pltpu
from jax.sharding import PartitionSpec as P

LANES = 128
BLOCK_ROWS = 1024


def _projection_kernel(order_ref, mine_ref, other_ref, gate_w_ref, up_w_ref, gate_ref, up_ref):
    k = pl.program_id(0)
    blocks = pl.num_programs(0) // 2

    @pl.when(k == 0)
    def _():
        gate_ref[...] = jnp.zeros_like(gate_ref)
        up_ref[...] = jnp.zeros_like(up_ref)

    def accumulate(x_ref):
        x = x_ref[...]
        gate_ref[...] += jnp.dot(x, gate_w_ref[...], preferred_element_type=jnp.float32)
        up_ref[...] += jnp.dot(x, up_w_ref[...], preferred_element_type=jnp.float32)

    pl.when(k < blocks)(lambda: accumulate(mine_ref))
    pl.when(k >= blocks)(lambda: accumulate(other_ref))


def projections(order, mine, other, gate_weight, up_weight):
    total, half = mine.shape
    hidden = gate_weight.shape[1]
    step = min(BLOCK_ROWS, half)
    blocks = half // step

    def weight_block(k, order_ref):
        first = order_ref[0] * blocks
        second = (1 - order_ref[0]) * blocks
        return (jnp.where(k < blocks, first + k, second + k - blocks), 0)

    weight_bytes = 2 * 2 * half * hidden * gate_weight.dtype.itemsize
    return pl.pallas_call(
        _projection_kernel,
        grid_spec=pltpu.PrefetchScalarGridSpec(
            num_scalar_prefetch=1,
            grid=(2 * blocks,),
            in_specs=[
                pl.BlockSpec((total, step), lambda k, o: (0, jnp.minimum(k, blocks - 1))),
                pl.BlockSpec((total, step), lambda k, o: (0, jnp.maximum(k - blocks, 0))),
                pl.BlockSpec((step, hidden), weight_block),
                pl.BlockSpec((step, hidden), weight_block),
            ],
            out_specs=[
                pl.BlockSpec((total, hidden), lambda k, o: (0, 0)),
                pl.BlockSpec((total, hidden), lambda k, o: (0, 0)),
            ],
        ),
        out_shape=[jax.ShapeDtypeStruct((total, hidden), jnp.float32)] * 2,
        compiler_params=pltpu.CompilerParams(dimension_semantics=("arbitrary",)),
        cost_estimate=pl.CostEstimate(
            flops=4 * total * 2 * half * hidden,
            transcendentals=0,
            bytes_accessed=weight_bytes + total * 2 * half * 2 + 2 * total * hidden * 4,
        ),
    )(order, mine, other, gate_weight, up_weight)


def body(
    tokens,
    gate_weight,
    up_weight,
    adapter_down_weight,
    adapter_up_weight,
    token_adapter_index,
    adapter_slot_index,
):
    rows, width = tokens.shape
    slots_held = adapter_up_weight.shape[0]
    half = width // 2
    me = lax.axis_index("tensor")
    order = me % 2
    halves = jnp.stack([tokens[:, :half], tokens[:, half:]])
    copies = jnp.broadcast_to(halves[None], (slots_held // 2, 2, rows, half)).reshape(slots_held, rows, half)
    mine = lax.all_to_all(copies, "tensor", 0, 0, tiled=False).reshape(slots_held * rows, half)
    other = lax.ppermute(mine, "tensor", [(j, j ^ 1) for j in range(slots_held)])
    total = mine.shape[0]

    down = adapter_down_weight[0]
    low = jnp.dot(mine, lax.dynamic_slice_in_dim(down, order * half, half), preferred_element_type=jnp.float32)
    low = low + jnp.dot(other, lax.dynamic_slice_in_dim(down, (1 - order) * half, half), preferred_element_type=jnp.float32)
    low = low.astype(jnp.bfloat16)
    rank = low.shape[1]
    local_slot = jnp.take(adapter_slot_index, token_adapter_index[:, 0], axis=0).astype(jnp.bfloat16)
    padded = -(-(rank + 1) // LANES) * LANES
    slot_col = jnp.zeros((total,), jnp.bfloat16).at[:rows].set(local_slot)
    payload = jnp.concatenate(
        [low, slot_col[:, None], jnp.zeros((total, padded - rank - 1), jnp.bfloat16)], axis=1
    )
    sent = jnp.broadcast_to(payload[None], (slots_held,) + payload.shape)
    gathered = lax.all_to_all(sent, "tensor", 0, 0, tiled=False)
    slots = gathered[:, :rows, rank].reshape(total).astype(jnp.int32)
    hits = slots[None, :, None] == jnp.arange(slots_held, dtype=jnp.int32)[:, None, None]
    spread = jnp.where(hits, gathered[:, :, :rank], jnp.zeros((), jnp.bfloat16))

    gate, up = projections(order.reshape(1).astype(jnp.int32), mine, other, gate_weight, up_weight)
    delta = jnp.einsum("str,srh->th", spread, adapter_up_weight, preferred_element_type=jnp.float32)
    return (jax.nn.silu(gate) * (up + delta)).astype(jnp.bfloat16)


def solution(mesh):
    in_specs = (
        P(("groups", "tensor"), None),
        P(None, "tensor"),
        P(None, "tensor"),
        P("tensor", None, None),
        P(None, None, "tensor"),
        P(("groups", "tensor"), None),
        P(),
    )
    out_specs = P("groups", "tensor")
    return jax.shard_map(body, mesh=mesh, in_specs=in_specs, out_specs=out_specs, check_vma=False)
```

time: 98 us -> 69.2 us (0.71)
  waiting for transfers between devices: 44.4 us -> 1.03 us
  blocking collectives: 0 us -> 32 us
  matrix products: 31.7 us -> 3.9 us
  Pallas kernels: 0 us -> 21.7 us
  between operations: 13.5 us -> 0.15 us
  starting transfers between devices: 3.57 us -> 5.37 us
    all_gather x1 -> x0, waiting for transfers between devices: 43.7 us -> none  [body(): acts = lax.all_gather(tokens, 'tensor', axis=0, tiled=True)]
    all_to_all x0 -> x1, blocking collectives: none -> 32 us  [body(): lax.all_to_all(copies, 'tensor', 0, 0, tiled=False)]
    dot_general x3 -> x2, matrix products: 27.4 us -> 0.97 us  [the longest x1 0.49 us: body(): jnp.dot(other, lax.dynamic_slice_in_dim(down, (1 - order) * half, half),...]
    pallas_call x0 -> x1, Pallas kernels: none -> 21.7 us  [projections(): pl.pallas_call(_projection_kernel, grid_spec=pltpu.PrefetchScalarGridSpec...]
    dot_general x1, matrix products: 4.29 us -> 2.93 us  [body(): jnp.einsum('str,srh->th', spread, adapter_up_weight, preferred_element_ty...]
    convert_element_type x0 -> x1, other arithmetic: none -> 1.03 us  [body(): return (jax.nn.silu(gate) * (up + delta)).astype(jnp.bfloat16)]
    ppermute x0 -> x1, waiting for transfers between devices: none -> 1.03 us  [body(): lax.ppermute(mine, 'tensor', [(j, j ^ 1) for j in range(slots_held)])]
    all_to_all x1, starting transfers between devices: 3.57 us -> 4.6 us  [body(): gathered = lax.all_to_all(sent, 'tensor', 0, 0, tiled=False)]
  transfers between devices with their start and end apart: 2 -> 2, of which waited for: 1 -> 1; matrix products, arithmetic and copies ran while one was open for 28% -> 2% of each run, Pallas kernels for 0% -> 31%
where the time goes in v8:
time: 69.2 us; the launch traced here: 68.9 us
  blocking collectives  32 us (46%)
  Pallas kernels  21.7 us (31%)
  starting transfers between devices  5.37 us (8%)
  matrix products  3.9 us (6%)
  local copies, waits for them, and re-layouts  3.58 us (5%)
  other arithmetic  1.19 us (2%)
  waiting for transfers between devices  1.03 us (1%)
    all_to_all x1, blocking collectives, body(): lax.all_to_all(copies, 'tensor', 0, 0, tiled=False)  32 us
    pallas_call x1, Pallas kernels, projections(): pl.pallas_call(_projection_kernel, grid_spec=pltpu.PrefetchScalarGridSpec...  21.7 us
    all_to_all x1, starting transfers between devices, body(): gathered = lax.all_to_all(sent, 'tensor', 0, 0, tiled=False)  4.6 us
    dot_general x1, matrix products, body(): jnp.einsum('str,srh->th', spread, adapter_up_weight, preferred_element_ty...  2.93 us
  transfers between devices with their start and end apart: 2, of which 1 were waited for; matrix products, arithmetic and copies ran while one was open for 2% of the time, Pallas kernels for 31%

profile of v8, /device:TPU:0, one launch (start us, length us, event | category | flops | bytes accessed | tf_op | source)
XLA Modules:
  0.0 68.9 jit_solution(18408821512006352790)
XLA Ops:
  0.0 0.0 copy-start
  0.0 0.0 copy-start.8
  0.0 0.0 copy-start.2
  0.0 1.0 %slice_bitcast_fusion.1 = (bf16[1,8,4096]{2,1,0:T(8,128)(2,1)S(1)}, bf16[1,8,4096]{2,1,0:T(8,128)(2,1)S(1)}) fusion(bf16[8,8192]{1,0:T(8,128)(2,1)} %param.9), kind=kLoop, calls=%fused_computation.17 | loop fusion | bytes 262144 | tf_op jit(solution)/shard_map/stack | solution.py:82
  1.0 0.1 broadcast_in_dim.16
  1.1 32.0 %all_to_all.10 = bf16[16,8,4096]{2,1,0:T(8,128)(2,1)S(1)} all-to-all(bf16[16,8,4096]{2,1,0:T(8,128)(2,1)S(1)} %bitcast.27), channel_id=1, replica_groups=mesh['groups'=2,'tensor'=16] {'tensor'}, dimensions={0} | all-to-all | bytes 2097152 | tf_op jit(solution)/shard_map/all_to_all | solution.py:84
  33.1 0.0 copy-start.3
  33.1 0.8 %collective-permute-start = (bf16[128,4096]{1,0:T(8,128)(2,1)S(1)}, bf16[128,4096]{1,0:T(8,128)(2,1)S(1)}, u32[]{:S(2)}, u32[]{:S(2)}) collective-permute-start(bf16[128,4096]{1,0:T(8,128)(2,1)S(1)} %bitcast.25), channel_id=1, source_target_pairs={{0,1},{1,0},{2,3},{3,2},{4,5},{5,4},{6,7},{7,6},{8,9},{9,8},{10,11... | collective-permute-start | bytes 3145736 | tf_op jit(solution)/shard_map/ppermute | solution.py:85
  33.9 0.1 pad.5.clone
  34.0 0.0 copy-done.8
  34.0 0.0 copy-done.2
  34.0 0.6 gather_fusion
  34.7 0.0 copy-done
  34.7 0.5 fusion.2
  35.2 1.0 %collective-permute-done.other_ref = bf16[128,4096]{1,0:T(8,128)(2,1)S(1)} collective-permute-done((bf16[128,4096]{1,0:T(8,128)(2,1)S(1)}, bf16[128,4096]{1,0:T(8,128)(2,1)S(1)}, u32[]{:S(2)}, u32[]{:S(2)}) %collective-permute-start) | collective-permute-done | bytes 1048608 | tf_op jit(solution)/shard_map/ppermute | solution.py:85
  36.2 0.0 copy-start.4
  36.2 0.5 fusion
  36.7 0.1 fusion.11
  36.8 0.9 %broadcast_in_dim.18 = bf16[16,128,128]{1,2,0:T(8,128)(2,1)} broadcast(bf16[128,128]{0,1:T(8,128)(2,1)S(1)} %fusion.11), dimensions={1,2} | broadcast | bytes 557056 | tf_op jit(solution)/shard_map/broadcast_in_dim | solution.py:99
  37.7 4.6 %all-to-all-start.1 = ((bf16[16,128,128]{1,2,0:T(8,128)(2,1)}), bf16[16,128,128]{1,2,0:T(8,128)(2,1)S(1)}, u32[]{:S(2)}, u32[]{:S(2)}) async-start(bf16[16,128,128]{1,2,0:T(8,128)(2,1)} %broadcast_in_dim.18), calls=%async_computation.1 | async-start | bytes 1048576 | tf_op jit(solution)/shard_map/all_to_all | solution.py:100
  42.3 0.0 copy-done.3
  42.3 0.0 copy-done.4
  42.3 21.7 %shard_map.73 = (f32[128,1792]{1,0:T(8,128)}, f32[128,1792]{1,0:T(8,128)}) custom-call(s32[1]{0:T(128)} %bitcast.order_ref, bf16[128,4096]{1,0:T(8,128)(2,1)} %bitcast.26, bf16[128,4096]{1,0:T(8,128)(2,1)} %copy-done.4, bf16[8192,1792]{1,0:T(8,128)(2,1)} %gate_w_ref.1, bf16[8192,1792]{1,0:T(8,128)(2,1)} %up_w_ref.1), custom_call_target="tpu_custom_call" | custom-call | flops 7516192768 | bytes 62652416 | tf_op jit(solution)/shard_map/pallas_call | solution.py:42
  64.0 0.0 copy-start.6
  64.0 0.0 all-to-all-done.1
  64.0 0.0 copy-start.5
  64.0 0.8 %copy-done.5 = bf16[16,128,128]{1,2,0:T(8,128)(2,1)} copy-done((bf16[16,128,128]{1,2,0:T(8,128)(2,1)}, bf16[16,128,128]{1,2,0:T(8,128)(2,1)S(1)}, u32[]{:S(2)}) %copy-start.5) | copy-done | bytes 524312
  64.8 0.1 reshape.76
  64.9 0.0 copy-start.7
  64.9 0.0 copy-start.1
  64.9 2.9 %convolution_bitcast_fusion = f32[128,1792]{1,0:T(8,128)S(1)} fusion(bf16[16,64,1792]{2,1,0:T(8,128)(2,1)} %param.13, bf16[16,128,128]{1,2,0:T(8,128)(2,1)} %copy-done.5, pred[16,128]{1,0:T(8,128)(4,1)S(1)} %iota_compare_fusion.2), kind=kOutput, calls=%fused_computation.1 | convolution fusion | flops 469893120 | bytes 4851712 | tf_op jit(solution)/shard_map/str,srh->th/dot_general | solution.py:106
  67.8 0.0 copy-done.6
  67.9 0.0 copy-done.7
  67.9 1.0 %multiply_convert_fusion = bf16[128,1792]{1,0:T(8,128)(2,1)} fusion(f32[128,1792]{1,0:T(8,128)S(1)} %copy-done.7, f32[128,1792]{1,0:T(8,128)S(1)} %convolution_bitcast_fusion, f32[128,1792]{1,0:T(8,128)S(1)} %copy-done.6), kind=kLoop, calls=%fused_computation.4 | loop fusion | flops 1605632 | bytes 3211264 | tf_op jit(solution)/shard_map/convert_element_type | solution.py:107
  68.9 0.0 copy-done.1
  (7 shorter events, 0.1 us)
Async XLA Ops:
  0.0 34.7 %copy-start = (bf16[1,8192,64]{1,2,0:T(8,128)(2,1)S(1)}, bf16[1,8192,64]{1,2,0:T(8,128)(2,1)}, u32[]{:S(2)}) copy-start(bf16[1,8192,64]{1,2,0:T(8,128)(2,1)} %param.12) | copy-start | bytes 3145732
  0.0 34.0 %copy-start.8 = (s32[8,1]{0,1:T(1,128)S(1)}, s32[8,1]{0,1:T(1,128)}, u32[]{:S(2)}) copy-start(s32[8,1]{0,1:T(1,128)} %param.14) | copy-start | bytes 100
  0.0 34.0 %copy-start.2 = (s32[16]{0:T(128)S(1)}, s32[16]{0:T(128)}, u32[]{:S(2)}) copy-start(s32[16]{0:T(128)} %param.15) | copy-start | bytes 196
  33.1 9.1 %copy-start.3 = (bf16[16,8,4096]{2,1,0:T(8,128)(2,1)}, bf16[16,8,4096]{2,1,0:T(8,128)(2,1)S(1)}, u32[]{:S(2)}) copy-start(bf16[16,8,4096]{2,1,0:T(8,128)(2,1)S(1)} %all_to_all.10) | copy-start | bytes 3145732
  33.1 3.1 %collective-permute-start = (bf16[128,4096]{1,0:T(8,128)(2,1)S(1)}, bf16[128,4096]{1,0:T(8,128)(2,1)S(1)}, u32[]{:S(2)}, u32[]{:S(2)}) collective-permute-start(bf16[128,4096]{1,0:T(8,128)(2,1)S(1)} %bitcast.25), channel_id=1, source_target_pairs={{0,1},{1,0},{2,3},{3,2},{4,5},{5,4},{6,7},{7,6},{8,9},{9,8},{10,11... | collective-permute-start | bytes 3145736 | tf_op jit(solution)/shard_map/ppermute | solution.py:85
  36.2 6.1 %copy-start.4 = (bf16[128,4096]{1,0:T(8,128)(2,1)}, bf16[128,4096]{1,0:T(8,128)(2,1)S(1)}, u32[]{:S(2)}) copy-start(bf16[128,4096]{1,0:T(8,128)(2,1)S(1)} %collective-permute-done.other_ref) | copy-start | bytes 3145732
  37.7 26.3 %all-to-all-start.1 = ((bf16[16,128,128]{1,2,0:T(8,128)(2,1)}), bf16[16,128,128]{1,2,0:T(8,128)(2,1)S(1)}, u32[]{:S(2)}, u32[]{:S(2)}) async-start(bf16[16,128,128]{1,2,0:T(8,128)(2,1)} %broadcast_in_dim.18), calls=%async_computation.1 | async-start | bytes 1048576 | tf_op jit(solution)/shard_map/all_to_all | solution.py:100
  64.0 3.9 %copy-start.6 = (f32[128,1792]{1,0:T(8,128)S(1)}, f32[128,1792]{1,0:T(8,128)}, u32[]{:S(2)}) copy-start(f32[128,1792]{1,0:T(8,128)} %get-tuple-element.19) | copy-start | bytes 2752516
  64.0 0.8 %copy-start.5 = (bf16[16,128,128]{1,2,0:T(8,128)(2,1)}, bf16[16,128,128]{1,2,0:T(8,128)(2,1)S(1)}, u32[]{:S(2)}) copy-start(bf16[16,128,128]{1,2,0:T(8,128)(2,1)S(1)} %all-to-all-done.1) | copy-start | bytes 1572868
  64.9 3.0 %copy-start.7 = (f32[128,1792]{1,0:T(8,128)S(1)}, f32[128,1792]{1,0:T(8,128)}, u32[]{:S(2)}) copy-start(f32[128,1792]{1,0:T(8,128)} %get-tuple-element.20) | copy-start | bytes 2752516
  64.9 4.0 %copy-start.1 = (bf16[1,8192,64]{1,2,0:T(8,128)(2,1)S(1)}, bf16[1,8192,64]{1,2,0:T(8,128)(2,1)}, u32[]{:S(2)}) copy-start(bf16[1,8192,64]{1,2,0:T(8,128)(2,1)} %param.12) | copy-start | bytes 3145732

commit v9 on v8

--- a/solution.py
+++ b/solution.py
@@ -9,7 +9,9 @@
 BLOCK_ROWS = 1024
 
 
-def _projection_kernel(order_ref, mine_ref, other_ref, gate_w_ref, up_w_ref, gate_ref, up_ref):
+def _projection_kernel(
+    order_ref, mine_ref, other_ref, gate_w_ref, up_w_ref, spread_ref, lift_ref, out_ref, gate_ref, up_ref
+):
     k = pl.program_id(0)
     blocks = pl.num_programs(0) // 2
 
@@ -26,8 +28,13 @@
     pl.when(k < blocks)(lambda: accumulate(mine_ref))
     pl.when(k >= blocks)(lambda: accumulate(other_ref))
 
+    @pl.when(k == 2 * blocks - 1)
+    def _():
+        delta = jnp.dot(spread_ref[...], lift_ref[...], preferred_element_type=jnp.float32)
+        out_ref[...] = (jax.nn.silu(gate_ref[...]) * (up_ref[...] + delta)).astype(out_ref.dtype)
 
-def projections(order, mine, other, gate_weight, up_weight):
+
+def gated_hidden(order, mine, other, gate_weight, up_weight, spread, lift):
     total, half = mine.shape
     hidden = gate_weight.shape[1]
     step = min(BLOCK_ROWS, half)
@@ -49,20 +56,20 @@
                 pl.BlockSpec((total, step), lambda k, o: (0, jnp.maximum(k - blocks, 0))),
                 pl.BlockSpec((step, hidden), weight_block),
                 pl.BlockSpec((step, hidden), weight_block),
+                pl.BlockSpec(spread.shape, lambda k, o: (0, 0)),
+                pl.BlockSpec(lift.shape, lambda k, o: (0, 0)),
             ],
-            out_specs=[
-                pl.BlockSpec((total, hidden), lambda k, o: (0, 0)),
-                pl.BlockSpec((total, hidden), lambda k, o: (0, 0)),
-            ],
+            out_specs=pl.BlockSpec((total, hidden), lambda k, o: (0, 0)),
+            scratch_shapes=[pltpu.VMEM((total, hidden), jnp.float32)] * 2,
         ),
-        out_shape=[jax.ShapeDtypeStruct((total, hidden), jnp.float32)] * 2,
+        out_shape=jax.ShapeDtypeStruct((total, hidden), jnp.bfloat16),
         compiler_params=pltpu.CompilerParams(dimension_semantics=("arbitrary",)),
         cost_estimate=pl.CostEstimate(
             flops=4 * total * 2 * half * hidden,
             transcendentals=0,
-            bytes_accessed=weight_bytes + total * 2 * half * 2 + 2 * total * hidden * 4,
+            bytes_accessed=weight_bytes + total * 2 * half * 2 + lift.size * 2 + total * hidden * 2,
         ),
-    )(order, mine, other, gate_weight, up_weight)
+    )(order, mine, other, gate_weight, up_weight, spread, lift)
 
 
 def body(
@@ -101,10 +108,10 @@
     slots = gathered[:, :rows, rank].reshape(total).astype(jnp.int32)
     hits = slots[None, :, None] == jnp.arange(slots_held, dtype=jnp.int32)[:, None, None]
     spread = jnp.where(hits, gathered[:, :, :rank], jnp.zeros((), jnp.bfloat16))
-
-    gate, up = projections(order.reshape(1).astype(jnp.int32), mine, other, gate_weight, up_weight)
-    delta = jnp.einsum("str,srh->th", spread, adapter_up_weight, preferred_element_type=jnp.float32)
-    return (jax.nn.silu(gate) * (up + delta)).astype(jnp.bfloat16)
+    spread = spread.transpose(1, 0, 2).reshape(total, slots_held * rank)
+    lift = adapter_up_weight.reshape(slots_held * rank, adapter_up_weight.shape[2])
+    order = order.reshape(1).astype(jnp.int32)
+    return gated_hidden(order, mine, other, gate_weight, up_weight, spread, lift)
 
 
 def solution(mesh):

time: 69.2 us -> 82.7 us (1.20)
  blocking collectives: 32 us -> 50.8 us
  starting transfers between devices: 5.37 us -> 0.77 us
  matrix products: 3.9 us -> 0.96 us
  Pallas kernels: 21.7 us -> 23 us
  other arithmetic: 1.19 us -> 2.46 us
  waiting for transfers between devices: 1.03 us -> 0.01 us
    all_to_all x0 -> x1, blocking collectives: none -> 18.8 us  [body(): gathered = lax.all_to_all(sent, 'tensor', 0, 0, tiled=False)]
    all_to_all x1 -> x0, starting transfers between devices: 4.6 us -> none  [body(): gathered = lax.all_to_all(sent, 'tensor', 0, 0, tiled=False)]
    dot_general x1 -> x0, matrix products: 2.93 us -> none  [body(): jnp.einsum('str,srh->th', spread, adapter_up_weight, preferred_element_ty...]
    pallas_call x1, Pallas kernels: 21.7 us -> 23 us  [gated_hidden(): pl.pallas_call(_projection_kernel, grid_spec=pltpu.PrefetchScalarGridSpec...]
    convert_element_type x1 -> x0, other arithmetic: 1.03 us -> none  [body(): return (jax.nn.silu(gate) * (up + delta)).astype(jnp.bfloat16)]
    ppermute x1, waiting for transfers between devices: 1.03 us -> 0.01 us  [body(): lax.ppermute(mine, 'tensor', [(j, j ^ 1) for j in range(slots_held)])]
    select_n x0 -> x1, other arithmetic: none -> 0.98 us  [body(): spread = jnp.where(hits, gathered[:, :, :rank], jnp.zeros((), jnp.bfloat16))]
    reshape x0 -> x1, local copies, waits for them, and re-layouts: none -> 0.87 us  [body(): spread = spread.transpose(1, 0, 2).reshape(total, slots_held * rank)]
  transfers between devices with their start and end apart: 2 -> 1, of which waited for: 1 -> 0; matrix products, arithmetic and copies ran while one was open for 2% -> 4% of each run, Pallas kernels for 31% -> 0%
where the time goes in v9:
time: 82.7 us; the launch traced here: 82.4 us
  blocking collectives  50.8 us (61%)
  Pallas kernels  23 us (28%)
  local copies, waits for them, and re-layouts  4.29 us (5%)
  other arithmetic  2.46 us (3%)
  matrix products  0.96 us (1%)
    all_to_all x1, blocking collectives, body(): lax.all_to_all(copies, 'tensor', 0, 0, tiled=False)  32 us
    pallas_call x1, Pallas kernels, gated_hidden(): pl.pallas_call(_projection_kernel, grid_spec=pltpu.PrefetchScalarGridSpec...  23 us
    all_to_all x1, blocking collectives, body(): gathered = lax.all_to_all(sent, 'tensor', 0, 0, tiled=False)  18.8 us
  transfers between devices with their start and end apart: 1, of which 0 were waited for; matrix products, arithmetic and copies ran while one was open for 4% of the time, Pallas kernels for 0%

profile of v9, /device:TPU:0, one launch (start us, length us, event | category | flops | bytes accessed | tf_op | source)
XLA Modules:
  0.0 82.4 jit_solution(3749780958561253168)
XLA Ops:
  0.0 0.0 copy-start
  0.0 1.0 %slice_bitcast_fusion.1 = (bf16[1,8,4096]{2,1,0:T(8,128)(2,1)S(1)}, bf16[1,8,4096]{2,1,0:T(8,128)(2,1)S(1)}) fusion(bf16[8,8192]{1,0:T(8,128)(2,1)} %param.9), kind=kLoop, calls=%fused_computation.13 | loop fusion | bytes 262144 | tf_op jit(solution)/shard_map/stack | solution.py:89
  1.0 0.1 broadcast_in_dim.16
  1.1 32.0 %all_to_all.10 = bf16[16,8,4096]{2,1,0:T(8,128)(2,1)S(1)} all-to-all(bf16[16,8,4096]{2,1,0:T(8,128)(2,1)S(1)} %bitcast.28), channel_id=1, replica_groups=mesh['groups'=2,'tensor'=16] {'tensor'}, dimensions={0} | all-to-all | bytes 2097152 | tf_op jit(solution)/shard_map/all_to_all | solution.py:91
  33.1 0.0 copy-start.1
  33.1 0.8 collective-permute-start
  33.9 0.1 pad.5.clone
  34.0 0.7 fusion.15
  34.7 1.3 %gather_fusion = s32[8]{0:T(128)S(1)} fusion(s32[16]{0:T(128)} %param.15, s32[1024]{0:T(1024)S(1)} %pad_clamp_fusion), kind=kCustom, calls=%fused_computation | custom fusion | bytes 96 | tf_op jit(solution)/shard_map/jit(_take)/gather | solution.py:100
  36.0 0.7 fusion.13
  36.6 0.0 copy-done
  36.6 0.5 fusion.2
  37.1 0.0 collective-permute-done.other_ref
  37.1 0.0 copy-start.2
  37.1 0.5 fusion
  37.6 0.1 fusion.9
  37.7 0.1 broadcast_in_dim.18
  37.8 18.8 %all_to_all.11 = bf16[16,128,128]{1,2,0:T(8,128)(2,1)S(1)} all-to-all(bf16[16,128,128]{1,2,0:T(8,128)(2,1)S(1)} %broadcast_in_dim.18), channel_id=1, replica_groups=mesh['groups'=2,'tensor'=16] {'tensor'}, dimensions={0} | all-to-all | bytes 1048576 | tf_op jit(solution)/shard_map/all_to_all | solution.py:107
  56.6 0.0 copy-start.3
  56.6 0.8 copy-done.3
  57.4 0.1 reshape.84
  57.5 1.0 %slice_select_fusion = bf16[16,128,64]{1,2,0:T(8,128)(2,1)S(1)} fusion(bf16[16,128,128]{1,2,0:T(8,128)(2,1)} %copy-done.3, pred[16,128]{1,0:T(8,128)(4,1)S(1)} %iota_compare_fusion.2), kind=kLoop, calls=%fused_computation.8 | loop fusion | flops 131072 | bytes 526336 | tf_op jit(solution)/shard_map/jit(_where)/select_n | solution.py:110
  58.5 0.9 %copy.9.spread_ref = bf16[128,1024]{1,0:T(8,128)(2,1)} copy(bf16[128,1024]{0,1:T(8,128)(2,1)S(1)} %bitcast.30) | data formatting | bytes 524288 | tf_op jit(solution)/shard_map/reshape | solution.py:111
  59.4 0.0 copy-done.1
  59.4 0.0 copy-done.2
  59.4 23.0 %shard_map.73 = bf16[128,1792]{1,0:T(8,128)(2,1)} custom-call(s32[1]{0:T(128)} %bitcast.order_ref, bf16[128,4096]{1,0:T(8,128)(2,1)} %bitcast.27, bf16[128,4096]{1,0:T(8,128)(2,1)} %copy-done.2, bf16[8192,1792]{1,0:T(8,128)(2,1)} %gate_w_ref.1, bf16[8192,1792]{1,0:T(8,128)(2,1)} %up_w_ref.1, bf16[128,1024]{1,0:T(8,128)(2,1)} %copy.9.spread_ref, ...), custom_call_target="tpu_custom_call" | custom-call | flops 7516192768 | bytes 64946176 | tf_op jit(solution)/shard_map/pallas_call | solution.py:49
  (5 shorter events, 0.1 us)
Async XLA Ops:
  0.0 36.6 %copy-start = (bf16[1,8192,64]{1,2,0:T(8,128)(2,1)S(1)}, bf16[1,8192,64]{1,2,0:T(8,128)(2,1)}, u32[]{:S(2)}) copy-start(bf16[1,8192,64]{1,2,0:T(8,128)(2,1)} %param.12) | copy-start | bytes 3145732
  33.1 26.3 %copy-start.1 = (bf16[16,8,4096]{2,1,0:T(8,128)(2,1)}, bf16[16,8,4096]{2,1,0:T(8,128)(2,1)S(1)}, u32[]{:S(2)}) copy-start(bf16[16,8,4096]{2,1,0:T(8,128)(2,1)S(1)} %all_to_all.10) | copy-start | bytes 3145732
  33.1 4.0 %collective-permute-start = (bf16[128,4096]{1,0:T(8,128)(2,1)S(1)}, bf16[128,4096]{1,0:T(8,128)(2,1)S(1)}, u32[]{:S(2)}, u32[]{:S(2)}) collective-permute-start(bf16[128,4096]{1,0:T(8,128)(2,1)S(1)} %bitcast.26), channel_id=1, source_target_pairs={{0,1},{1,0},{2,3},{3,2},{4,5},{5,4},{6,7},{7,6},{8,9},{9,8},{10,11... | collective-permute-start | bytes 3145736 | tf_op jit(solution)/shard_map/ppermute | solution.py:92
  37.1 22.3 %copy-start.2 = (bf16[128,4096]{1,0:T(8,128)(2,1)}, bf16[128,4096]{1,0:T(8,128)(2,1)S(1)}, u32[]{:S(2)}) copy-start(bf16[128,4096]{1,0:T(8,128)(2,1)S(1)} %collective-permute-done.other_ref) | copy-start | bytes 3145732
  56.6 0.8 copy-start.3

commit v10 on v8

--- a/solution.py
+++ b/solution.py
@@ -65,6 +65,45 @@
     )(order, mine, other, gate_weight, up_weight)
 
 
+def _gating_kernel(slot_ref, gathered_ref, lift_ref, gate_ref, up_ref, out_ref):
+    slot = slot_ref[...]
+    rank = lift_ref.shape[1]
+    slots_held = lift_ref.shape[0]
+
+    def add_slot(s, delta):
+        rows = jnp.where(slot == s, gathered_ref[s][:, :rank], jnp.zeros((), gathered_ref.dtype))
+        return delta + jnp.dot(rows, lift_ref[s], preferred_element_type=jnp.float32)
+
+    delta = lax.fori_loop(0, slots_held, add_slot, jnp.zeros(out_ref.shape, jnp.float32), unroll=min(slots_held, 16))
+    gate = gate_ref[...]
+    out_ref[...] = (jax.nn.silu(gate) * (up_ref[...] + delta)).astype(out_ref.dtype)
+
+
+def gated_hidden(slot, gathered, lift, gate, up):
+    total, hidden = gate.shape
+    slots_held, rank, _ = lift.shape
+    cols = 256 if hidden % 256 == 0 else hidden
+    return pl.pallas_call(
+        _gating_kernel,
+        grid=(hidden // cols,),
+        in_specs=[
+            pl.BlockSpec(slot.shape, lambda j: (0, 0)),
+            pl.BlockSpec(gathered.shape, lambda j: (0, 0, 0)),
+            pl.BlockSpec((slots_held, rank, cols), lambda j: (0, 0, j)),
+            pl.BlockSpec((total, cols), lambda j: (0, j)),
+            pl.BlockSpec((total, cols), lambda j: (0, j)),
+        ],
+        out_specs=pl.BlockSpec((total, cols), lambda j: (0, j)),
+        out_shape=jax.ShapeDtypeStruct((total, hidden), jnp.bfloat16),
+        compiler_params=pltpu.CompilerParams(dimension_semantics=("arbitrary",)),
+        cost_estimate=pl.CostEstimate(
+            flops=2 * total * slots_held * rank * hidden,
+            transcendentals=total * hidden,
+            bytes_accessed=lift.size * 2 + gathered.size * 2 + 2 * total * hidden * 4 + total * hidden * 2,
+        ),
+    )(slot, gathered, lift, gate, up)
+
+
 def body(
     tokens,
     gate_weight,
@@ -98,13 +137,10 @@
     )
     sent = jnp.broadcast_to(payload[None], (slots_held,) + payload.shape)
     gathered = lax.all_to_all(sent, "tensor", 0, 0, tiled=False)
-    slots = gathered[:, :rows, rank].reshape(total).astype(jnp.int32)
-    hits = slots[None, :, None] == jnp.arange(slots_held, dtype=jnp.int32)[:, None, None]
-    spread = jnp.where(hits, gathered[:, :, :rank], jnp.zeros((), jnp.bfloat16))
+    slots = gathered[:, :rows, rank].reshape(total, 1).astype(jnp.int32)
 
     gate, up = projections(order.reshape(1).astype(jnp.int32), mine, other, gate_weight, up_weight)
-    delta = jnp.einsum("str,srh->th", spread, adapter_up_weight, preferred_element_type=jnp.float32)
-    return (jax.nn.silu(gate) * (up + delta)).astype(jnp.bfloat16)
+    return gated_hidden(slots, gathered, adapter_up_weight, gate, up)
 
 
 def solution(mesh):

time: 69.2 us -> 74.6 us (1.078)
  Pallas kernels: 21.7 us -> 29.3 us
  matrix products: 3.9 us -> 0.96 us
  other arithmetic: 1.19 us -> 2.89 us
  waiting for transfers between devices: 1.03 us -> 0.01 us
    pallas_call x0 -> x1, Pallas kernels: none -> 7.64 us  [gated_hidden(): pl.pallas_call(_gating_kernel, grid=(hidden // cols,), in_specs=[pl.Block...]
    dot_general x1 -> x0, matrix products: 2.93 us -> none  [body(): jnp.einsum('str,srh->th', spread, adapter_up_weight, preferred_element_ty...]
    ppermute x1, waiting for transfers between devices: 1.03 us -> 0.01 us  [body(): lax.ppermute(mine, 'tensor', [(j, j ^ 1) for j in range(slots_held)])]
    unnamed x18 -> x6, local copies, waits for them, and re-layouts: 0.81 us -> 0.01 us
  transfers between devices with their start and end apart: 2 -> 2, of which waited for: 1 -> 0; matrix products, arithmetic and copies ran while one was open for 2% -> 4% of each run, Pallas kernels for 31% -> 29%
where the time goes in v10:
time: 74.6 us; the launch traced here: 74.1 us
  blocking collectives  32 us (43%)
  Pallas kernels  29.3 us (39%)
  starting transfers between devices  5.34 us (7%)
  local copies, waits for them, and re-layouts  3.48 us (5%)
  other arithmetic  2.89 us (4%)
  matrix products  0.96 us (1%)
    all_to_all x1, blocking collectives, body(): lax.all_to_all(copies, 'tensor', 0, 0, tiled=False)  32 us
    pallas_call x1, Pallas kernels, projections(): pl.pallas_call(_projection_kernel, grid_spec=pltpu.PrefetchScalarGridSpec...  21.7 us
    pallas_call x1, Pallas kernels, gated_hidden(): pl.pallas_call(_gating_kernel, grid=(hidden // cols,), in_specs=[pl.Block...  7.64 us
    all_to_all x1, starting transfers between devices, body(): gathered = lax.all_to_all(sent, 'tensor', 0, 0, tiled=False)  4.57 us
  transfers between devices with their start and end apart: 2, of which 0 were waited for; matrix products, arithmetic and copies ran while one was open for 4% of the time, Pallas kernels for 29%

profile of v10, /device:TPU:0, one launch (start us, length us, event | category | flops | bytes accessed | tf_op | source)
XLA Modules:
  0.0 74.1 jit_solution(17670885156602037586)
XLA Ops:
  0.0 0.0 copy-start
  0.0 1.0 %slice_bitcast_fusion.1 = (bf16[1,8,4096]{2,1,0:T(8,128)(2,1)S(1)}, bf16[1,8,4096]{2,1,0:T(8,128)(2,1)S(1)}) fusion(bf16[8,8192]{1,0:T(8,128)(2,1)} %param.9), kind=kLoop, calls=%fused_computation.12 | loop fusion | bytes 262144 | tf_op jit(solution)/shard_map/stack | solution.py:121
  1.0 0.1 broadcast_in_dim.8
  1.1 32.0 %all_to_all.10 = bf16[16,8,4096]{2,1,0:T(8,128)(2,1)S(1)} all-to-all(bf16[16,8,4096]{2,1,0:T(8,128)(2,1)S(1)} %bitcast.29), channel_id=1, replica_groups=mesh['groups'=2,'tensor'=16] {'tensor'}, dimensions={0} | all-to-all | bytes 2097152 | tf_op jit(solution)/shard_map/all_to_all | solution.py:123
  33.1 0.0 copy-start.1
  33.1 0.8 %collective-permute-start = (bf16[128,4096]{1,0:T(8,128)(2,1)S(1)}, bf16[128,4096]{1,0:T(8,128)(2,1)S(1)}, u32[]{:S(2)}, u32[]{:S(2)}) collective-permute-start(bf16[128,4096]{1,0:T(8,128)(2,1)S(1)} %bitcast.27), channel_id=1, source_target_pairs={{0,1},{1,0},{2,3},{3,2},{4,5},{5,4},{6,7},{7,6},{8,9},{9,8},{10,11... | collective-permute-start | bytes 3145736 | tf_op jit(solution)/shard_map/ppermute | solution.py:124
  33.9 0.1 pad.5.clone
  34.0 0.7 fusion.15
  34.7 1.3 %gather_fusion = s32[8]{0:T(128)S(1)} fusion(s32[16]{0:T(128)} %param.15, s32[1024]{0:T(1024)S(1)} %pad_clamp_fusion), kind=kCustom, calls=%fused_computation | custom fusion | bytes 96 | tf_op jit(solution)/shard_map/jit(_take)/gather | solution.py:132
  36.0 0.7 fusion.13
  36.6 0.0 copy-done
  36.6 0.5 fusion.2
  37.1 0.0 collective-permute-done.other_ref
  37.1 0.0 copy-start.2
  37.1 0.5 fusion
  37.6 0.1 fusion.9
  37.7 0.1 copy.10
  37.8 0.9 %broadcast_in_dim.10 = bf16[16,128,128]{2,1,0:T(8,128)(2,1)} broadcast(bf16[128,128]{1,0:T(8,128)(2,1)S(1)} %copy.10), dimensions={1,2} | broadcast | bytes 557056 | tf_op jit(solution)/shard_map/broadcast_in_dim | solution.py:138
  38.7 4.6 %all-to-all-start.1 = ((bf16[16,128,128]{2,1,0:T(8,128)(2,1)}), bf16[16,128,128]{2,1,0:T(8,128)(2,1)}, u32[]{:S(2)}, u32[]{:S(2)}) async-start(bf16[16,128,128]{2,1,0:T(8,128)(2,1)} %broadcast_in_dim.10), calls=%async_computation.1 | async-start | bytes 1048576 | tf_op jit(solution)/shard_map/all_to_all | solution.py:139
  43.3 0.0 copy-done.1
  43.3 0.0 copy-done.2
  43.3 21.7 %shard_map.73 = (f32[128,1792]{1,0:T(8,128)}, f32[128,1792]{1,0:T(8,128)}) custom-call(s32[1]{0:T(128)} %bitcast.9.order_ref, bf16[128,4096]{1,0:T(8,128)(2,1)} %bitcast.28, bf16[128,4096]{1,0:T(8,128)(2,1)} %copy-done.2, bf16[8192,1792]{1,0:T(8,128)(2,1)} %gate_w_ref.1, bf16[8192,1792]{1,0:T(8,128)(2,1)} %up_w_ref.1), custom_call_target="tpu_custom_call" | custom-call | flops 7516192768 | bytes 62652416 | tf_op jit(solution)/shard_map/pallas_call | solution.py:42
  65.0 0.0 all-to-all-done.1.gathered_ref
  65.0 1.5 %fusion.10.slot_ref = s32[128,1]{1,0:T(8,128)} fusion(bf16[16,128,128]{2,1,0:T(8,128)(2,1)} %all-to-all-done.1.gathered_ref), kind=kLoop, calls=%fused_computation.18 | loop fusion | flops 128 | bytes 768 | tf_op jit(solution)/shard_map/convert_element_type | solution.py:140
  66.5 7.6 %shard_map.74 = bf16[128,1792]{1,0:T(8,128)(2,1)} custom-call(s32[128,1]{1,0:T(8,128)} %fusion.10.slot_ref, bf16[16,128,128]{2,1,0:T(8,128)(2,1)} %all-to-all-done.1.gathered_ref, bf16[16,64,1792]{2,1,0:T(8,128)(2,1)} %lift_ref.1, f32[128,1792]{1,0:T(8,128)} %get-tuple-element.19.gate_ref, f32[128,1792]{1,0:T(8,128)} %get-tuple-element.20.up_ref), custom_call_target="tpu_custom_call" | custom-call | flops 469762048 | bytes 6488064 | tf_op jit(solution)/shard_map/pallas_call | solution.py:86
  (3 shorter events, 0.0 us)
Async XLA Ops:
  0.0 36.6 %copy-start = (bf16[1,8192,64]{1,2,0:T(8,128)(2,1)S(1)}, bf16[1,8192,64]{1,2,0:T(8,128)(2,1)}, u32[]{:S(2)}) copy-start(bf16[1,8192,64]{1,2,0:T(8,128)(2,1)} %param.12) | copy-start | bytes 3145732
  33.1 10.2 %copy-start.1 = (bf16[16,8,4096]{2,1,0:T(8,128)(2,1)}, bf16[16,8,4096]{2,1,0:T(8,128)(2,1)S(1)}, u32[]{:S(2)}) copy-start(bf16[16,8,4096]{2,1,0:T(8,128)(2,1)S(1)} %all_to_all.10) | copy-start | bytes 3145732
  33.1 4.0 %collective-permute-start = (bf16[128,4096]{1,0:T(8,128)(2,1)S(1)}, bf16[128,4096]{1,0:T(8,128)(2,1)S(1)}, u32[]{:S(2)}, u32[]{:S(2)}) collective-permute-start(bf16[128,4096]{1,0:T(8,128)(2,1)S(1)} %bitcast.27), channel_id=1, source_target_pairs={{0,1},{1,0},{2,3},{3,2},{4,5},{5,4},{6,7},{7,6},{8,9},{9,8},{10,11... | collective-permute-start | bytes 3145736 | tf_op jit(solution)/shard_map/ppermute | solution.py:124
  37.1 6.2 %copy-start.2 = (bf16[128,4096]{1,0:T(8,128)(2,1)}, bf16[128,4096]{1,0:T(8,128)(2,1)S(1)}, u32[]{:S(2)}) copy-start(bf16[128,4096]{1,0:T(8,128)(2,1)S(1)} %collective-permute-done.other_ref) | copy-start | bytes 3145732
  38.7 26.3 %all-to-all-start.1 = ((bf16[16,128,128]{2,1,0:T(8,128)(2,1)}), bf16[16,128,128]{2,1,0:T(8,128)(2,1)}, u32[]{:S(2)}, u32[]{:S(2)}) async-start(bf16[16,128,128]{2,1,0:T(8,128)(2,1)} %broadcast_in_dim.10), calls=%async_computation.1 | async-start | bytes 1048576 | tf_op jit(solution)/shard_map/all_to_all | solution.py:139

commit v11 on v8

--- a/solution.py
+++ b/solution.py
@@ -7,16 +7,26 @@
 
 LANES = 128
 BLOCK_ROWS = 1024
+PIECES = 2
 
 
-def _projection_kernel(order_ref, mine_ref, other_ref, gate_w_ref, up_w_ref, gate_ref, up_ref):
+def _projection_kernel(base_ref, mine_ref, other_ref, gate_w_ref, up_w_ref, *refs):
+    if len(refs) == 4:
+        gate_in_ref, up_in_ref, gate_ref, up_ref = refs
+    else:
+        gate_in_ref = up_in_ref = None
+        gate_ref, up_ref = refs
     k = pl.program_id(0)
     blocks = pl.num_programs(0) // 2
 
     @pl.when(k == 0)
     def _():
-        gate_ref[...] = jnp.zeros_like(gate_ref)
-        up_ref[...] = jnp.zeros_like(up_ref)
+        if gate_in_ref is None:
+            gate_ref[...] = jnp.zeros_like(gate_ref)
+            up_ref[...] = jnp.zeros_like(up_ref)
+        else:
+            gate_ref[...] = gate_in_ref[...]
+            up_ref[...] = up_in_ref[...]
 
     def accumulate(x_ref):
         x = x_ref[...]
@@ -27,17 +37,17 @@
     pl.when(k >= blocks)(lambda: accumulate(other_ref))
 
 
-def projections(order, mine, other, gate_weight, up_weight):
+def projections(base, mine, other, gate_weight, up_weight, partial=None):
     total, half = mine.shape
     hidden = gate_weight.shape[1]
     step = min(BLOCK_ROWS, half)
     blocks = half // step
 
-    def weight_block(k, order_ref):
-        first = order_ref[0] * blocks
-        second = (1 - order_ref[0]) * blocks
-        return (jnp.where(k < blocks, first + k, second + k - blocks), 0)
+    def weight_block(k, base_ref):
+        return (jnp.where(k < blocks, base_ref[0] + k, base_ref[1] + k - blocks), 0)
 
+    extra_specs = [] if partial is None else [pl.BlockSpec((total, hidden), lambda k, o: (0, 0))] * 2
+    extra_args = () if partial is None else tuple(partial)
     weight_bytes = 2 * 2 * half * hidden * gate_weight.dtype.itemsize
     return pl.pallas_call(
         _projection_kernel,
@@ -49,7 +59,8 @@
                 pl.BlockSpec((total, step), lambda k, o: (0, jnp.maximum(k - blocks, 0))),
                 pl.BlockSpec((step, hidden), weight_block),
                 pl.BlockSpec((step, hidden), weight_block),
-            ],
+            ]
+            + extra_specs,
             out_specs=[
                 pl.BlockSpec((total, hidden), lambda k, o: (0, 0)),
                 pl.BlockSpec((total, hidden), lambda k, o: (0, 0)),
@@ -62,7 +73,7 @@
             transcendentals=0,
             bytes_accessed=weight_bytes + total * 2 * half * 2 + 2 * total * hidden * 4,
         ),
-    )(order, mine, other, gate_weight, up_weight)
+    )(base, mine, other, gate_weight, up_weight, *extra_args)
 
 
 def body(
@@ -77,17 +88,30 @@
     rows, width = tokens.shape
     slots_held = adapter_up_weight.shape[0]
     half = width // 2
+    piece = half // PIECES
+    step = min(BLOCK_ROWS, piece)
     me = lax.axis_index("tensor")
     order = me % 2
-    halves = jnp.stack([tokens[:, :half], tokens[:, half:]])
-    copies = jnp.broadcast_to(halves[None], (slots_held // 2, 2, rows, half)).reshape(slots_held, rows, half)
-    mine = lax.all_to_all(copies, "tensor", 0, 0, tiled=False).reshape(slots_held * rows, half)
-    other = lax.ppermute(mine, "tensor", [(j, j ^ 1) for j in range(slots_held)])
+    down = adapter_down_weight[0]
+    partial = None
+    low = None
+    for q in range(PIECES):
+        cols = [tokens[:, h * half + q * piece : h * half + (q + 1) * piece] for h in range(2)]
+        copies = jnp.broadcast_to(jnp.stack(cols)[None], (slots_held // 2, 2, rows, piece))
+        mine = lax.all_to_all(copies.reshape(slots_held, rows, piece), "tensor", 0, 0, tiled=False)
+        mine = mine.reshape(slots_held * rows, piece)
+        if partial is not None:
+            mine, partial = lax.optimization_barrier((mine, partial))
+        other = lax.ppermute(mine, "tensor", [(j, j ^ 1) for j in range(slots_held)])
+        first = order * half + q * piece
+        second = (1 - order) * half + q * piece
+        base = jnp.stack([first // step, second // step]).astype(jnp.int32)
+        partial = projections(base, mine, other, gate_weight, up_weight, partial)
+        part = jnp.dot(mine, lax.dynamic_slice_in_dim(down, first, piece), preferred_element_type=jnp.float32)
+        part = part + jnp.dot(other, lax.dynamic_slice_in_dim(down, second, piece), preferred_element_type=jnp.float32)
+        low = part if low is None else low + part
     total = mine.shape[0]
-
-    down = adapter_down_weight[0]
-    low = jnp.dot(mine, lax.dynamic_slice_in_dim(down, order * half, half), preferred_element_type=jnp.float32)
-    low = low + jnp.dot(other, lax.dynamic_slice_in_dim(down, (1 - order) * half, half), preferred_element_type=jnp.float32)
+    gate, up = partial
     low = low.astype(jnp.bfloat16)
     rank = low.shape[1]
     local_slot = jnp.take(adapter_slot_index, token_adapter_index[:, 0], axis=0).astype(jnp.bfloat16)
@@ -102,7 +126,6 @@
     hits = slots[None, :, None] == jnp.arange(slots_held, dtype=jnp.int32)[:, None, None]
     spread = jnp.where(hits, gathered[:, :, :rank], jnp.zeros((), jnp.bfloat16))
 
-    gate, up = projections(order.reshape(1).astype(jnp.int32), mine, other, gate_weight, up_weight)
     delta = jnp.einsum("str,srh->th", spread, adapter_up_weight, preferred_element_type=jnp.float32)
     return (jax.nn.silu(gate) * (up + delta)).astype(jnp.bfloat16)
 

time: 69.2 us -> 73.2 us (1.058)
  blocking collectives: 32 us -> 21.7 us
  starting transfers between devices: 5.37 us -> 10.7 us
  Pallas kernels: 21.7 us -> 26.8 us
  matrix products: 3.9 us -> 6.15 us
  other arithmetic: 1.19 us -> 2.47 us
  local copies, waits for them, and re-layouts: 3.58 us -> 4.38 us
    all_to_all x1, blocking collectives: 32 us -> 21.7 us  [body(): lax.all_to_all(copies.reshape(slots_held, rows, piece), 'tensor', 0, 0, t...]
    pallas_call x1 -> x2, Pallas kernels: 21.7 us -> 26.8 us  [projections(): pl.pallas_call(_projection_kernel, grid_spec=pltpu.PrefetchScalarGridSpec...]
    all_to_all x0 -> x1, starting transfers between devices: none -> 4.1 us  [body(): lax.all_to_all(copies.reshape(slots_held, rows, piece), 'tensor', 0, 0, t...]
    dot_general x2 -> x4, matrix products: 0.97 us -> 3.29 us  [the longest x2 1.65 us: body(): jnp.dot(other, lax.dynamic_slice_in_dim(down, second, piece), preferred_e...]
    another operation x1 -> x3, other arithmetic: 0.02 us -> 1.27 us  [the longest x2 1.26 us: body(): base = jnp.stack([first // step, second // step]).astype(jnp.int32)]
    all_to_all x1, starting transfers between devices: 4.6 us -> 5.76 us  [body(): gathered = lax.all_to_all(sent, 'tensor', 0, 0, tiled=False)]
    ppermute x1 -> x2, waiting for transfers between devices: 1.03 us -> 0.16 us  [body(): lax.ppermute(mine, 'tensor', [(j, j ^ 1) for j in range(slots_held)])]
    broadcast_in_dim x1 -> x2, local copies, waits for them, and re-layouts: 0.09 us -> 0.95 us  [body(): jnp.broadcast_to(jnp.stack(cols)[None], (slots_held // 2, 2, rows, piece))]
  transfers between devices with their start and end apart: 2 -> 4, of which waited for: 1 -> 2; matrix products, arithmetic and copies ran while one was open for 2% -> 7% of each run, Pallas kernels for 31% -> 37%
where the time goes in v11:
time: 73.2 us; the launch traced here: 72.7 us
  Pallas kernels  26.8 us (37%)
  blocking collectives  21.7 us (30%)
  starting transfers between devices  10.7 us (15%)
  matrix products  6.15 us (8%)
  local copies, waits for them, and re-layouts  4.38 us (6%)
  other arithmetic  2.47 us (3%)
    pallas_call x2, Pallas kernels, projections(): pl.pallas_call(_projection_kernel, grid_spec=pltpu.PrefetchScalarGridSpec...  26.8 us
    all_to_all x1, blocking collectives, body(): lax.all_to_all(copies.reshape(slots_held, rows, piece), 'tensor', 0, 0, t...  21.7 us
    all_to_all x1, starting transfers between devices, body(): gathered = lax.all_to_all(sent, 'tensor', 0, 0, tiled=False)  5.76 us
    all_to_all x1, starting transfers between devices, body(): lax.all_to_all(copies.reshape(slots_held, rows, piece), 'tensor', 0, 0, t...  4.1 us
    dot_general x1, matrix products, body(): jnp.einsum('str,srh->th', spread, adapter_up_weight, preferred_element_ty...  2.86 us
    dot_general x2, matrix products, body(): jnp.dot(other, lax.dynamic_slice_in_dim(down, second, piece), preferred_e...  1.65 us
    dot_general x2, matrix products, body(): jnp.dot(mine, lax.dynamic_slice_in_dim(down, first, piece), preferred_ele...  1.64 us
  transfers between devices with their start and end apart: 4, of which 2 were waited for; matrix products, arithmetic and copies ran while one was open for 7% of the time, Pallas kernels for 37%

profile of v11, /device:TPU:0, one launch (start us, length us, event | category | flops | bytes accessed | tf_op | source)
XLA Modules:
  0.0 72.7 jit_solution(1577058350657291066)
XLA Ops:
  0.0 0.0 copy-start
  0.0 0.0 copy-start.9
  0.0 0.0 copy-start.2
  0.0 0.9 %slice_bitcast_fusion.1 = (bf16[1,8,2048]{2,1,0:T(8,128)(2,1)S(1)}, bf16[1,8,2048]{2,1,0:T(8,128)(2,1)S(1)}, bf16[1,8,2048]{2,1,0:T(8,128)(2,1)S(1)}, bf16[1,8,2048]{2,1,0:T(8,128)(2,1)S(1)}) fusion(bf16[8,8192]{1,0:T(8,128)(2,1)} %param.9), kind=kLoop, calls=%fused_computation.29 | loop fusion | bytes 262144 | tf_op jit(solution)/shard_map/stack | solution.py:100
  1.0 21.7 %all_to_all.15 = bf16[16,8,2048]{2,1,0:T(8,128)(2,1)S(1)} all-to-all(bf16[16,8,2048]{2,1,0:T(8,128)(2,1)S(1)} %bitcast.47), channel_id=1, replica_groups=mesh['groups'=2,'tensor'=16] {'tensor'}, dimensions={0} | all-to-all | bytes 1048576 | tf_op jit(solution)/shard_map/all_to_all | solution.py:101
  22.6 0.0 copy-start.4
  22.6 0.9 %broadcast_in_dim.18 = bf16[8,2,8,2048]{3,2,1,0:T(8,128)(2,1)} broadcast(bf16[2,8,2048]{2,1,0:T(8,128)(2,1)S(1)} %get-tuple-element.35), dimensions={1,2,3} | broadcast | bytes 589824 | tf_op jit(solution)/shard_map/broadcast_in_dim | solution.py:100
  23.6 4.1 %all-to-all-start = ((bf16[16,8,2048]{2,1,0:T(8,128)(2,1)}), bf16[16,8,2048]{2,1,0:T(8,128)(2,1)S(1)}, u32[]{:S(2)}, u32[]{:S(2)}) async-start(bf16[16,8,2048]{2,1,0:T(8,128)(2,1)} %bitcast.4), calls=%async_computation | async-start | bytes 1048576 | tf_op jit(solution)/shard_map/all_to_all | solution.py:101
  27.7 0.4 collective-permute-start
  28.1 0.0 copy-done.9
  28.1 0.1 pad.5.clone
  28.2 0.0 copy-done.2
  28.2 0.6 gather_fusion
  28.8 0.7 pad_add_fusion.1.base_ref
  29.5 0.2 collective-permute-done.other_ref
  29.6 0.0 copy-done.4
  29.6 0.0 copy-start.5
  29.6 0.8 %copy-done.5 = bf16[128,2048]{1,0:T(8,128)(2,1)} copy-done((bf16[128,2048]{1,0:T(8,128)(2,1)}, bf16[128,2048]{1,0:T(8,128)(2,1)S(1)}, u32[]{:S(2)}) %copy-start.5) | copy-done | bytes 524312
  30.4 13.2 %shard_map.73 = (f32[128,1792]{1,0:T(8,128)}, f32[128,1792]{1,0:T(8,128)}) custom-call(s32[2]{0:T(128)} %pad_add_fusion.1.base_ref, bf16[128,2048]{1,0:T(8,128)(2,1)} %bitcast.46, bf16[128,2048]{1,0:T(8,128)(2,1)} %copy-done.5, bf16[8192,1792]{1,0:T(8,128)(2,1)} %gate_w_ref.3, bf16[8192,1792]{1,0:T(8,128)(2,1)} %up_w_ref.3), custom_call_target="tpu_custom_call" | custom-call | flops 3758096384 | bytes 32243712 | tf_op jit(solution)/shard_map/pallas_call | solution.py:52
  43.6 0.0 all-to-all-done
  43.6 0.0 copy-start.3
  43.6 0.4 collective-permute-start.1
  44.0 0.0 copy-done
  44.0 1.3 %fusion.6 = f32[128,64]{0,1:T(8,128)S(1)} fusion(bf16[1,8192,64]{1,2,0:T(8,128)(2,1)S(1)} %copy-done, s32[]{:T(128)S(6)} %select_n.53, bf16[16,8,2048]{2,1,0:T(8,128)(2,1)} %copy-done.4), kind=kOutput, calls=%fused_computation.12 | convolution fusion | flops 33554432 | bytes 819204 | tf_op jit(solution)/shard_map/dot_general | solution.py:110
  45.4 0.3 fusion.3
  45.7 1.3 %convolution_add_fusion.1 = f32[128,64]{0,1:T(8,128)S(1)} fusion(f32[128,64]{0,1:T(8,128)S(1)} %fusion.6, bf16[128,2048]{1,0:T(8,128)(2,1)} %copy-done.5, bf16[1,8192,64]{1,2,0:T(8,128)(2,1)S(1)} %copy-done, s32[]{:T(128)S(6)} %select_n.54), kind=kOutput, calls=%fused_computation.4 | convolution fusion | flops 33562624 | bytes 851972 | tf_op jit(solution)/shard_map/dot_general | solution.py:111
  47.0 0.0 collective-permute-done.1.other_ref
  47.0 0.0 copy-start.6
  47.1 0.3 fusion.1
  47.4 0.1 fusion.17
  47.5 0.9 %broadcast_in_dim.21 = bf16[16,128,128]{1,2,0:T(8,128)(2,1)} broadcast(bf16[128,128]{0,1:T(8,128)(2,1)S(1)} %fusion.17), dimensions={1,2} | broadcast | bytes 557056 | tf_op jit(solution)/shard_map/broadcast_in_dim | solution.py:123
  48.4 5.8 %all-to-all-start.2 = ((bf16[16,128,128]{1,2,0:T(8,128)(2,1)}), bf16[16,128,128]{1,2,0:T(8,128)(2,1)S(1)}, u32[]{:S(2)}, u32[]{:S(2)}) async-start(bf16[16,128,128]{1,2,0:T(8,128)(2,1)} %broadcast_in_dim.21), calls=%async_computation.2 | async-start | bytes 1048576 | tf_op jit(solution)/shard_map/all_to_all | solution.py:124
  54.2 0.6 pad_add_fusion.base_ref
  54.8 0.0 copy-done.3
  54.8 0.0 copy-done.6
  54.8 13.6 %shard_map.74 = (f32[128,1792]{1,0:T(8,128)}, f32[128,1792]{1,0:T(8,128)}) custom-call(s32[2]{0:T(128)} %pad_add_fusion.base_ref, bf16[128,2048]{1,0:T(8,128)(2,1)} %bitcast.44, bf16[128,2048]{1,0:T(8,128)(2,1)} %copy-done.6, bf16[8192,1792]{1,0:T(8,128)(2,1)} %gate_w_ref.3, bf16[8192,1792]{1,0:T(8,128)(2,1)} %up_w_ref.3, ...), custom_call_target="tpu_custom_call" | custom-call | flops 3758096384 | bytes 32243712 | tf_op jit(solution)/shard_map/pallas_call | solution.py:52
  68.4 0.0 copy-start.7
  68.4 0.2 all-to-all-done.2
  68.6 0.1 reshape.83
  68.7 0.0 copy-start.8
  68.7 0.0 copy-start.1
  68.8 2.9 %convolution_bitcast_fusion = f32[128,1792]{1,0:T(8,128)S(1)} fusion(bf16[16,64,1792]{2,1,0:T(8,128)(2,1)} %param.13, bf16[16,128,128]{1,2,0:T(8,128)(2,1)S(1)} %all-to-all-done.2, pred[16,128]{1,0:T(8,128)(4,1)S(1)} %iota_compare_fusion.2), kind=kOutput, calls=%fused_computation.1 | convolution fusion | flops 469893120 | bytes 4851712 | tf_op jit(solution)/shard_map/str,srh->th/dot_general | solution.py:129
  71.6 0.0 copy-done.7
  71.6 0.0 copy-done.8
  71.6 1.1 %multiply_convert_fusion = bf16[128,1792]{1,0:T(8,128)(2,1)} fusion(f32[128,1792]{1,0:T(8,128)S(1)} %copy-done.8, f32[128,1792]{1,0:T(8,128)S(1)} %convolution_bitcast_fusion, f32[128,1792]{1,0:T(8,128)S(1)} %copy-done.7), kind=kLoop, calls=%fused_computation.6 | loop fusion | flops 1605632 | bytes 3211264 | tf_op jit(solution)/shard_map/convert_element_type | solution.py:130
  72.7 0.0 copy-done.1
  (8 shorter events, 0.1 us)
Async XLA Ops:
  0.0 44.0 %copy-start = (bf16[1,8192,64]{1,2,0:T(8,128)(2,1)S(1)}, bf16[1,8192,64]{1,2,0:T(8,128)(2,1)}, u32[]{:S(2)}) copy-start(bf16[1,8192,64]{1,2,0:T(8,128)(2,1)} %param.12) | copy-start | bytes 3145732
  0.0 28.1 %copy-start.9 = (s32[8,1]{0,1:T(1,128)S(1)}, s32[8,1]{0,1:T(1,128)}, u32[]{:S(2)}) copy-start(s32[8,1]{0,1:T(1,128)} %param.14) | copy-start | bytes 100
  0.0 28.2 %copy-start.2 = (s32[16]{0:T(128)S(1)}, s32[16]{0:T(128)}, u32[]{:S(2)}) copy-start(s32[16]{0:T(128)} %param.15) | copy-start | bytes 196
  22.6 7.0 %copy-start.4 = (bf16[16,8,2048]{2,1,0:T(8,128)(2,1)}, bf16[16,8,2048]{2,1,0:T(8,128)(2,1)S(1)}, u32[]{:S(2)}) copy-start(bf16[16,8,2048]{2,1,0:T(8,128)(2,1)S(1)} %all_to_all.15) | copy-start | bytes 1572868
  23.6 20.1 %all-to-all-start = ((bf16[16,8,2048]{2,1,0:T(8,128)(2,1)}), bf16[16,8,2048]{2,1,0:T(8,128)(2,1)S(1)}, u32[]{:S(2)}, u32[]{:S(2)}) async-start(bf16[16,8,2048]{2,1,0:T(8,128)(2,1)} %bitcast.4), calls=%async_computation | async-start | bytes 1048576 | tf_op jit(solution)/shard_map/all_to_all | solution.py:101
  27.7 2.0 %collective-permute-start = (bf16[128,2048]{1,0:T(8,128)(2,1)S(1)}, bf16[128,2048]{1,0:T(8,128)(2,1)S(1)}, u32[]{:S(2)}, u32[]{:S(2)}) collective-permute-start(bf16[128,2048]{1,0:T(8,128)(2,1)S(1)} %bitcast.45), channel_id=1, source_target_pairs={{0,1},{1,0},{2,3},{3,2},{4,5},{5,4},{6,7},{7,6},{8,9},{9,8},{10,11... | collective-permute-start | bytes 1572872 | tf_op jit(solution)/shard_map/ppermute | solution.py:105
  29.6 0.8 %copy-start.5 = (bf16[128,2048]{1,0:T(8,128)(2,1)}, bf16[128,2048]{1,0:T(8,128)(2,1)S(1)}, u32[]{:S(2)}) copy-start(bf16[128,2048]{1,0:T(8,128)(2,1)S(1)} %collective-permute-done.other_ref) | copy-start | bytes 1572868
  43.6 11.2 %copy-start.3 = (bf16[16,8,2048]{2,1,0:T(8,128)(2,1)}, bf16[16,8,2048]{2,1,0:T(8,128)(2,1)S(1)}, u32[]{:S(2)}) copy-start(bf16[16,8,2048]{2,1,0:T(8,128)(2,1)S(1)} %all-to-all-done) | copy-start | bytes 1572868
  43.6 3.4 %collective-permute-start.1 = (bf16[128,2048]{1,0:T(8,128)(2,1)S(1)}, bf16[128,2048]{1,0:T(8,128)(2,1)S(1)}, u32[]{:S(2)}, u32[]{:S(2)}) collective-permute-start(bf16[128,2048]{1,0:T(8,128)(2,1)S(1)} %bitcast.42), channel_id=1, source_target_pairs={{0,1},{1,0},{2,3},{3,2},{4,5},{5,4},{6,7},{7,6},{8,9},{9,8},{10,11... | collective-permute-start | bytes 1572872 | tf_op jit(solution)/shard_map/ppermute | solution.py:105
  47.0 7.7 %copy-start.6 = (bf16[128,2048]{1,0:T(8,128)(2,1)}, bf16[128,2048]{1,0:T(8,128)(2,1)S(1)}, u32[]{:S(2)}) copy-start(bf16[128,2048]{1,0:T(8,128)(2,1)S(1)} %collective-permute-done.1.other_ref) | copy-start | bytes 1572868
  48.4 20.2 %all-to-all-start.2 = ((bf16[16,128,128]{1,2,0:T(8,128)(2,1)}), bf16[16,128,128]{1,2,0:T(8,128)(2,1)S(1)}, u32[]{:S(2)}, u32[]{:S(2)}) async-start(bf16[16,128,128]{1,2,0:T(8,128)(2,1)} %broadcast_in_dim.21), calls=%async_computation.2 | async-start | bytes 1048576 | tf_op jit(solution)/shard_map/all_to_all | solution.py:124
  68.4 3.2 %copy-start.7 = (f32[128,1792]{1,0:T(8,128)S(1)}, f32[128,1792]{1,0:T(8,128)}, u32[]{:S(2)}) copy-start(f32[128,1792]{1,0:T(8,128)} %get-tuple-element.29) | copy-start | bytes 2752516
  68.7 2.9 %copy-start.8 = (f32[128,1792]{1,0:T(8,128)S(1)}, f32[128,1792]{1,0:T(8,128)}, u32[]{:S(2)}) copy-start(f32[128,1792]{1,0:T(8,128)} %get-tuple-element.30) | copy-start | bytes 2752516
  68.7 4.0 %copy-start.1 = (bf16[1,8192,64]{1,2,0:T(8,128)(2,1)S(1)}, bf16[1,8192,64]{1,2,0:T(8,128)(2,1)}, u32[]{:S(2)}) copy-start(bf16[1,8192,64]{1,2,0:T(8,128)(2,1)} %param.12) | copy-start | bytes 3145732

commit v12 on v8

--- a/solution.py
+++ b/solution.py
@@ -5,7 +5,7 @@
 from jax.experimental.pallas import tpu as pltpu
 from jax.sharding import PartitionSpec as P
 
-LANES = 128
+SUBLANES = 8
 BLOCK_ROWS = 1024
 
 
@@ -91,19 +91,16 @@
     low = low.astype(jnp.bfloat16)
     rank = low.shape[1]
     local_slot = jnp.take(adapter_slot_index, token_adapter_index[:, 0], axis=0).astype(jnp.bfloat16)
-    padded = -(-(rank + 1) // LANES) * LANES
-    slot_col = jnp.zeros((total,), jnp.bfloat16).at[:rows].set(local_slot)
-    payload = jnp.concatenate(
-        [low, slot_col[:, None], jnp.zeros((total, padded - rank - 1), jnp.bfloat16)], axis=1
-    )
+    slot_rows = jnp.zeros((SUBLANES, total), jnp.bfloat16).at[0, :rows].set(local_slot)
+    payload = jnp.concatenate([low.T, slot_rows], axis=0)
     sent = jnp.broadcast_to(payload[None], (slots_held,) + payload.shape)
     gathered = lax.all_to_all(sent, "tensor", 0, 0, tiled=False)
-    slots = gathered[:, :rows, rank].reshape(total).astype(jnp.int32)
-    hits = slots[None, :, None] == jnp.arange(slots_held, dtype=jnp.int32)[:, None, None]
-    spread = jnp.where(hits, gathered[:, :, :rank], jnp.zeros((), jnp.bfloat16))
+    slots = gathered[:, rank, :rows].reshape(total).astype(jnp.int32)
+    hits = slots[None, None, :] == jnp.arange(slots_held, dtype=jnp.int32)[:, None, None]
+    spread = jnp.where(hits, gathered[:, :rank, :], jnp.zeros((), jnp.bfloat16))
 
     gate, up = projections(order.reshape(1).astype(jnp.int32), mine, other, gate_weight, up_weight)
-    delta = jnp.einsum("str,srh->th", spread, adapter_up_weight, preferred_element_type=jnp.float32)
+    delta = jnp.einsum("srt,srh->th", spread, adapter_up_weight, preferred_element_type=jnp.float32)
     return (jax.nn.silu(gate) * (up + delta)).astype(jnp.bfloat16)
 
 

time: 69.2 us -> 68.1 us (0.984)
  local copies, waits for them, and re-layouts: 3.58 us -> 2.58 us
    unnamed x18 -> x16, local copies, waits for them, and re-layouts: 0.81 us -> 0.03 us
  transfers between devices with their start and end apart: 2 -> 2, of which waited for: 1 -> 1; matrix products, arithmetic and copies ran while one was open for 2% -> 2% of each run, Pallas kernels for 31% -> 32%
where the time goes in v12:
time: 68.1 us; the launch traced here: 67.9 us
  blocking collectives  32 us (47%)
  Pallas kernels  21.7 us (32%)
  starting transfers between devices  5.37 us (8%)
  matrix products  3.84 us (6%)
  local copies, waits for them, and re-layouts  2.58 us (4%)
  other arithmetic  1.12 us (2%)
  waiting for transfers between devices  1.11 us (2%)
    all_to_all x1, blocking collectives, body(): lax.all_to_all(copies, 'tensor', 0, 0, tiled=False)  32 us
    pallas_call x1, Pallas kernels, projections(): pl.pallas_call(_projection_kernel, grid_spec=pltpu.PrefetchScalarGridSpec...  21.7 us
    all_to_all x1, starting transfers between devices, body(): gathered = lax.all_to_all(sent, 'tensor', 0, 0, tiled=False)  4.6 us
    dot_general x1, matrix products, body(): jnp.einsum('srt,srh->th', spread, adapter_up_weight, preferred_element_ty...  2.87 us
  transfers between devices with their start and end apart: 2, of which 1 were waited for; matrix products, arithmetic and copies ran while one was open for 2% of the time, Pallas kernels for 32%

profile of v12, /device:TPU:0, one launch (start us, length us, event | category | flops | bytes accessed | tf_op | source)
XLA Modules:
  0.0 67.9 jit_solution(9371791165270694079)
XLA Ops:
  0.0 0.0 copy-start
  0.0 0.0 copy-start.7
  0.0 0.0 copy-start.2
  0.0 1.0 %slice_bitcast_fusion.1 = (bf16[1,8,4096]{2,1,0:T(8,128)(2,1)S(1)}, bf16[1,8,4096]{2,1,0:T(8,128)(2,1)S(1)}) fusion(bf16[8,8192]{1,0:T(8,128)(2,1)} %param.9), kind=kLoop, calls=%fused_computation.15 | loop fusion | bytes 262144 | tf_op jit(solution)/shard_map/stack | solution.py:82
  1.0 0.1 broadcast_in_dim.14
  1.1 32.0 %all_to_all.10 = bf16[16,8,4096]{2,1,0:T(8,128)(2,1)S(1)} all-to-all(bf16[16,8,4096]{2,1,0:T(8,128)(2,1)S(1)} %bitcast.31), channel_id=1, replica_groups=mesh['groups'=2,'tensor'=16] {'tensor'}, dimensions={0} | all-to-all | bytes 2097152 | tf_op jit(solution)/shard_map/all_to_all | solution.py:84
  33.1 0.0 copy-start.3
  33.1 0.8 %collective-permute-start = (bf16[128,4096]{1,0:T(8,128)(2,1)S(1)}, bf16[128,4096]{1,0:T(8,128)(2,1)S(1)}, u32[]{:S(2)}, u32[]{:S(2)}) collective-permute-start(bf16[128,4096]{1,0:T(8,128)(2,1)S(1)} %bitcast.29), channel_id=1, source_target_pairs={{0,1},{1,0},{2,3},{3,2},{4,5},{5,4},{6,7},{7,6},{8,9},{9,8},{10,11... | collective-permute-start | bytes 3145736 | tf_op jit(solution)/shard_map/ppermute | solution.py:85
  33.9 0.0 copy-done.7
  33.9 0.0 copy-done.2
  33.9 0.6 gather_fusion
  34.6 0.0 copy-done
  34.6 0.5 fusion.2
  35.1 1.1 %collective-permute-done.other_ref = bf16[128,4096]{1,0:T(8,128)(2,1)S(1)} collective-permute-done((bf16[128,4096]{1,0:T(8,128)(2,1)S(1)}, bf16[128,4096]{1,0:T(8,128)(2,1)S(1)}, u32[]{:S(2)}, u32[]{:S(2)}) %collective-permute-start) | collective-permute-done | bytes 1048608 | tf_op jit(solution)/shard_map/ppermute | solution.py:85
  36.2 0.0 copy-start.4
  36.2 0.5 fusion
  36.7 0.8 %broadcast_in_dim.15 = bf16[16,72,128]{2,1,0:T(8,128)(2,1)} broadcast(bf16[72,128]{1,0:T(8,128)(2,1)S(1)} %fusion.9), dimensions={1,2} | broadcast | bytes 313344 | tf_op jit(solution)/shard_map/broadcast_in_dim | solution.py:96
  37.5 4.6 %all-to-all-start.1 = ((bf16[16,72,128]{2,1,0:T(8,128)(2,1)}), bf16[16,72,128]{2,1,0:T(8,128)(2,1)S(1)}, u32[]{:S(2)}, u32[]{:S(2)}) async-start(bf16[16,72,128]{2,1,0:T(8,128)(2,1)} %broadcast_in_dim.15), calls=%async_computation.1 | async-start | bytes 589824 | tf_op jit(solution)/shard_map/all_to_all | solution.py:97
  42.1 0.0 copy-done.3
  42.1 0.0 copy-done.4
  42.1 21.7 %shard_map.73 = (f32[128,1792]{1,0:T(8,128)}, f32[128,1792]{1,0:T(8,128)}) custom-call(s32[1]{0:T(128)} %bitcast.order_ref, bf16[128,4096]{1,0:T(8,128)(2,1)} %bitcast.30, bf16[128,4096]{1,0:T(8,128)(2,1)} %copy-done.4, bf16[8192,1792]{1,0:T(8,128)(2,1)} %gate_w_ref.1, bf16[8192,1792]{1,0:T(8,128)(2,1)} %up_w_ref.1), custom_call_target="tpu_custom_call" | custom-call | flops 7516192768 | bytes 62652416 | tf_op jit(solution)/shard_map/pallas_call | solution.py:42
  63.8 0.0 copy-start.5
  63.8 0.0 all-to-all-done.1
  63.8 0.1 reshape.89
  63.9 0.0 copy-start.6
  63.9 0.0 copy-start.1
  63.9 2.9 %convolution_bitcast_fusion = f32[128,1792]{1,0:T(8,128)S(1)} fusion(bf16[16,64,1792]{2,1,0:T(8,128)(2,1)} %param.13, bf16[16,72,128]{2,1,0:T(8,128)(2,1)S(1)} %all-to-all-done.1, pred[16,128]{1,0:T(8,128)(4,1)S(1)} %iota_compare_fusion.1), kind=kOutput, calls=%fused_computation.1 | convolution fusion | flops 469893120 | bytes 4851712 | tf_op jit(solution)/shard_map/srt,srh->th/dot_general | solution.py:103
  66.8 0.0 copy-done.5
  66.8 0.0 copy-done.6
  66.8 1.0 %multiply_convert_fusion = bf16[128,1792]{1,0:T(8,128)(2,1)} fusion(f32[128,1792]{1,0:T(8,128)S(1)} %copy-done.6, f32[128,1792]{1,0:T(8,128)S(1)} %convolution_bitcast_fusion, f32[128,1792]{1,0:T(8,128)S(1)} %copy-done.5), kind=kLoop, calls=%fused_computation.4 | loop fusion | flops 1605632 | bytes 3211264 | tf_op jit(solution)/shard_map/convert_element_type | solution.py:104
  67.9 0.0 copy-done.1
  (7 shorter events, 0.1 us)
Async XLA Ops:
  0.0 34.6 %copy-start = (bf16[1,8192,64]{1,2,0:T(8,128)(2,1)S(1)}, bf16[1,8192,64]{1,2,0:T(8,128)(2,1)}, u32[]{:S(2)}) copy-start(bf16[1,8192,64]{1,2,0:T(8,128)(2,1)} %param.12) | copy-start | bytes 3145732
  0.0 33.9 %copy-start.7 = (s32[8,1]{0,1:T(1,128)S(1)}, s32[8,1]{0,1:T(1,128)}, u32[]{:S(2)}) copy-start(s32[8,1]{0,1:T(1,128)} %param.14) | copy-start | bytes 100
  0.0 33.9 %copy-start.2 = (s32[16]{0:T(128)S(1)}, s32[16]{0:T(128)}, u32[]{:S(2)}) copy-start(s32[16]{0:T(128)} %param.15) | copy-start | bytes 196
  33.1 8.9 %copy-start.3 = (bf16[16,8,4096]{2,1,0:T(8,128)(2,1)}, bf16[16,8,4096]{2,1,0:T(8,128)(2,1)S(1)}, u32[]{:S(2)}) copy-start(bf16[16,8,4096]{2,1,0:T(8,128)(2,1)S(1)} %all_to_all.10) | copy-start | bytes 3145732
  33.1 3.1 %collective-permute-start = (bf16[128,4096]{1,0:T(8,128)(2,1)S(1)}, bf16[128,4096]{1,0:T(8,128)(2,1)S(1)}, u32[]{:S(2)}, u32[]{:S(2)}) collective-permute-start(bf16[128,4096]{1,0:T(8,128)(2,1)S(1)} %bitcast.29), channel_id=1, source_target_pairs={{0,1},{1,0},{2,3},{3,2},{4,5},{5,4},{6,7},{7,6},{8,9},{9,8},{10,11... | collective-permute-start | bytes 3145736 | tf_op jit(solution)/shard_map/ppermute | solution.py:85
  36.2 5.9 %copy-start.4 = (bf16[128,4096]{1,0:T(8,128)(2,1)}, bf16[128,4096]{1,0:T(8,128)(2,1)S(1)}, u32[]{:S(2)}) copy-start(bf16[128,4096]{1,0:T(8,128)(2,1)S(1)} %collective-permute-done.other_ref) | copy-start | bytes 3145732
  37.5 26.3 %all-to-all-start.1 = ((bf16[16,72,128]{2,1,0:T(8,128)(2,1)}), bf16[16,72,128]{2,1,0:T(8,128)(2,1)S(1)}, u32[]{:S(2)}, u32[]{:S(2)}) async-start(bf16[16,72,128]{2,1,0:T(8,128)(2,1)} %broadcast_in_dim.15), calls=%async_computation.1 | async-start | bytes 589824 | tf_op jit(solution)/shard_map/all_to_all | solution.py:97
  63.8 3.0 %copy-start.5 = (f32[128,1792]{1,0:T(8,128)S(1)}, f32[128,1792]{1,0:T(8,128)}, u32[]{:S(2)}) copy-start(f32[128,1792]{1,0:T(8,128)} %get-tuple-element.19) | copy-start | bytes 2752516
  63.9 2.9 %copy-start.6 = (f32[128,1792]{1,0:T(8,128)S(1)}, f32[128,1792]{1,0:T(8,128)}, u32[]{:S(2)}) copy-start(f32[128,1792]{1,0:T(8,128)} %get-tuple-element.20) | copy-start | bytes 2752516
  63.9 4.0 %copy-start.1 = (bf16[1,8192,64]{1,2,0:T(8,128)(2,1)S(1)}, bf16[1,8192,64]{1,2,0:T(8,128)(2,1)}, u32[]{:S(2)}) copy-start(bf16[1,8192,64]{1,2,0:T(8,128)(2,1)} %param.12) | copy-start | bytes 3145732

commit v13 on v12

--- a/solution.py
+++ b/solution.py
@@ -90,7 +90,8 @@
     low = low + jnp.dot(other, lax.dynamic_slice_in_dim(down, (1 - order) * half, half), preferred_element_type=jnp.float32)
     low = low.astype(jnp.bfloat16)
     rank = low.shape[1]
-    local_slot = jnp.take(adapter_slot_index, token_adapter_index[:, 0], axis=0).astype(jnp.bfloat16)
+    named = token_adapter_index[:, :1] == jnp.arange(adapter_slot_index.shape[0], dtype=jnp.int32)[None, :]
+    local_slot = jnp.sum(jnp.where(named, adapter_slot_index[None, :], 0), axis=1).astype(jnp.bfloat16)
     slot_rows = jnp.zeros((SUBLANES, total), jnp.bfloat16).at[0, :rows].set(local_slot)
     payload = jnp.concatenate([low.T, slot_rows], axis=0)
     sent = jnp.broadcast_to(payload[None], (slots_held,) + payload.shape)

time: 68.1 us -> 68.1 us (level)
  transfers between devices with their start and end apart: 2 -> 2, of which waited for: 1 -> 1; matrix products, arithmetic and copies ran while one was open for 2% -> 1% of each run, Pallas kernels for 32% -> 32%
where the time goes in v13:
time: 68.1 us; the launch traced here: 67.9 us
  blocking collectives  32 us (47%)
  Pallas kernels  21.7 us (32%)
  starting transfers between devices  5.36 us (8%)
  matrix products  3.82 us (6%)
  local copies, waits for them, and re-layouts  1.93 us (3%)
  waiting for transfers between devices  1.6 us (2%)
  other arithmetic  1.3 us (2%)
    all_to_all x1, blocking collectives, body(): lax.all_to_all(copies, 'tensor', 0, 0, tiled=False)  32 us
    pallas_call x1, Pallas kernels, projections(): pl.pallas_call(_projection_kernel, grid_spec=pltpu.PrefetchScalarGridSpec...  21.7 us
    all_to_all x1, starting transfers between devices, body(): gathered = lax.all_to_all(sent, 'tensor', 0, 0, tiled=False)  4.59 us
    dot_general x1, matrix products, body(): jnp.einsum('srt,srh->th', spread, adapter_up_weight, preferred_element_ty...  2.86 us
    ppermute x1, waiting for transfers between devices, body(): lax.ppermute(mine, 'tensor', [(j, j ^ 1) for j in range(slots_held)])  1.6 us
  transfers between devices with their start and end apart: 2, of which 1 were waited for; matrix products, arithmetic and copies ran while one was open for 1% of the time, Pallas kernels for 32%

profile of v13, /device:TPU:0, one launch (start us, length us, event | category | flops | bytes accessed | tf_op | source)
XLA Modules:
  0.0 67.9 jit_solution(8381520602394270952)
XLA Ops:
  0.0 0.0 copy-start
  0.0 0.0 copy-start.6
  0.0 0.0 copy-start.7
  0.0 1.0 %slice_bitcast_fusion.1 = (bf16[1,8,4096]{2,1,0:T(8,128)(2,1)S(1)}, bf16[1,8,4096]{2,1,0:T(8,128)(2,1)S(1)}) fusion(bf16[8,8192]{1,0:T(8,128)(2,1)} %param.9), kind=kLoop, calls=%fused_computation.14 | loop fusion | bytes 262144 | tf_op jit(solution)/shard_map/stack | solution.py:82
  1.0 0.1 broadcast_in_dim.24
  1.1 32.0 %all_to_all.10 = bf16[16,8,4096]{2,1,0:T(8,128)(2,1)S(1)} all-to-all(bf16[16,8,4096]{2,1,0:T(8,128)(2,1)S(1)} %bitcast.24), channel_id=1, replica_groups=mesh['groups'=2,'tensor'=16] {'tensor'}, dimensions={0} | all-to-all | bytes 2097152 | tf_op jit(solution)/shard_map/all_to_all | solution.py:84
  33.1 0.0 copy-start.2
  33.1 0.8 %collective-permute-start = (bf16[128,4096]{1,0:T(8,128)(2,1)S(1)}, bf16[128,4096]{1,0:T(8,128)(2,1)S(1)}, u32[]{:S(2)}, u32[]{:S(2)}) collective-permute-start(bf16[128,4096]{1,0:T(8,128)(2,1)S(1)} %bitcast.22), channel_id=1, source_target_pairs={{0,1},{1,0},{2,3},{3,2},{4,5},{5,4},{6,7},{7,6},{8,9},{9,8},{10,11... | collective-permute-start | bytes 3145736 | tf_op jit(solution)/shard_map/ppermute | solution.py:85
  33.9 0.0 copy-done.6
  33.9 0.0 copy-done.7
  33.9 0.2 select_reduce_fusion
  34.1 0.0 copy-done
  34.1 0.5 fusion.2
  34.6 1.6 %collective-permute-done.other_ref = bf16[128,4096]{1,0:T(8,128)(2,1)S(1)} collective-permute-done((bf16[128,4096]{1,0:T(8,128)(2,1)S(1)}, bf16[128,4096]{1,0:T(8,128)(2,1)S(1)}, u32[]{:S(2)}, u32[]{:S(2)}) %collective-permute-start) | collective-permute-done | bytes 1048608 | tf_op jit(solution)/shard_map/ppermute | solution.py:85
  36.2 0.0 copy-start.3
  36.2 0.5 fusion
  36.7 0.8 %broadcast_in_dim.44 = bf16[16,72,128]{2,1,0:T(8,128)(2,1)} broadcast(bf16[72,128]{1,0:T(8,128)(2,1)S(1)} %fusion.9), dimensions={1,2} | broadcast | bytes 313344 | tf_op jit(solution)/shard_map/broadcast_in_dim | solution.py:97
  37.5 4.6 %all-to-all-start.1 = ((bf16[16,72,128]{2,1,0:T(8,128)(2,1)}), bf16[16,72,128]{2,1,0:T(8,128)(2,1)S(1)}, u32[]{:S(2)}, u32[]{:S(2)}) async-start(bf16[16,72,128]{2,1,0:T(8,128)(2,1)} %broadcast_in_dim.44), calls=%async_computation.1 | async-start | bytes 589824 | tf_op jit(solution)/shard_map/all_to_all | solution.py:98
  42.1 0.0 copy-done.2
  42.1 0.0 copy-done.3
  42.1 21.7 %shard_map.73 = (f32[128,1792]{1,0:T(8,128)}, f32[128,1792]{1,0:T(8,128)}) custom-call(s32[1]{0:T(128)} %bitcast.order_ref, bf16[128,4096]{1,0:T(8,128)(2,1)} %bitcast.23, bf16[128,4096]{1,0:T(8,128)(2,1)} %copy-done.3, bf16[8192,1792]{1,0:T(8,128)(2,1)} %gate_w_ref.1, bf16[8192,1792]{1,0:T(8,128)(2,1)} %up_w_ref.1), custom_call_target="tpu_custom_call" | custom-call | flops 7516192768 | bytes 62652416 | tf_op jit(solution)/shard_map/pallas_call | solution.py:42
  63.7 0.0 copy-start.4
  63.7 0.0 all-to-all-done.1
  63.8 0.1 reshape.80
  63.9 0.0 copy-start.5
  63.9 0.0 copy-start.1
  63.9 2.9 %convolution_bitcast_fusion = f32[128,1792]{1,0:T(8,128)S(1)} fusion(bf16[16,64,1792]{2,1,0:T(8,128)(2,1)} %param.13, bf16[16,72,128]{2,1,0:T(8,128)(2,1)S(1)} %all-to-all-done.1, pred[16,128]{1,0:T(8,128)(4,1)S(1)} %iota_compare_fusion.1), kind=kOutput, calls=%fused_computation | convolution fusion | flops 469893120 | bytes 4851712 | tf_op jit(solution)/shard_map/srt,srh->th/dot_general | solution.py:104
  66.8 0.0 copy-done.4
  66.8 0.0 copy-done.5
  66.8 1.1 %multiply_convert_fusion = bf16[128,1792]{1,0:T(8,128)(2,1)} fusion(f32[128,1792]{1,0:T(8,128)S(1)} %copy-done.5, f32[128,1792]{1,0:T(8,128)S(1)} %convolution_bitcast_fusion, f32[128,1792]{1,0:T(8,128)S(1)} %copy-done.4), kind=kLoop, calls=%fused_computation.3 | loop fusion | flops 1605632 | bytes 3211264 | tf_op jit(solution)/shard_map/convert_element_type | solution.py:105
  67.9 0.0 copy-done.1
  (5 shorter events, 0.1 us)
Async XLA Ops:
  0.0 34.1 %copy-start = (bf16[1,8192,64]{1,2,0:T(8,128)(2,1)S(1)}, bf16[1,8192,64]{1,2,0:T(8,128)(2,1)}, u32[]{:S(2)}) copy-start(bf16[1,8192,64]{1,2,0:T(8,128)(2,1)} %param.12) | copy-start | bytes 3145732
  0.0 33.9 %copy-start.6 = (s32[16]{0:T(128)S(1)}, s32[16]{0:T(128)}, u32[]{:S(2)}) copy-start(s32[16]{0:T(128)} %param.15) | copy-start | bytes 196
  0.0 33.9 %copy-start.7 = (s32[8,1]{0,1:T(1,128)S(1)}, s32[8,1]{0,1:T(1,128)}, u32[]{:S(2)}) copy-start(s32[8,1]{0,1:T(1,128)} %param.14) | copy-start | bytes 100
  33.1 8.9 %copy-start.2 = (bf16[16,8,4096]{2,1,0:T(8,128)(2,1)}, bf16[16,8,4096]{2,1,0:T(8,128)(2,1)S(1)}, u32[]{:S(2)}) copy-start(bf16[16,8,4096]{2,1,0:T(8,128)(2,1)S(1)} %all_to_all.10) | copy-start | bytes 3145732
  33.1 3.1 %collective-permute-start = (bf16[128,4096]{1,0:T(8,128)(2,1)S(1)}, bf16[128,4096]{1,0:T(8,128)(2,1)S(1)}, u32[]{:S(2)}, u32[]{:S(2)}) collective-permute-start(bf16[128,4096]{1,0:T(8,128)(2,1)S(1)} %bitcast.22), channel_id=1, source_target_pairs={{0,1},{1,0},{2,3},{3,2},{4,5},{5,4},{6,7},{7,6},{8,9},{9,8},{10,11... | collective-permute-start | bytes 3145736 | tf_op jit(solution)/shard_map/ppermute | solution.py:85
  36.2 5.9 %copy-start.3 = (bf16[128,4096]{1,0:T(8,128)(2,1)}, bf16[128,4096]{1,0:T(8,128)(2,1)S(1)}, u32[]{:S(2)}) copy-start(bf16[128,4096]{1,0:T(8,128)(2,1)S(1)} %collective-permute-done.other_ref) | copy-start | bytes 3145732
  37.5 26.3 %all-to-all-start.1 = ((bf16[16,72,128]{2,1,0:T(8,128)(2,1)}), bf16[16,72,128]{2,1,0:T(8,128)(2,1)S(1)}, u32[]{:S(2)}, u32[]{:S(2)}) async-start(bf16[16,72,128]{2,1,0:T(8,128)(2,1)} %broadcast_in_dim.44), calls=%async_computation.1 | async-start | bytes 589824 | tf_op jit(solution)/shard_map/all_to_all | solution.py:98
  63.7 3.0 %copy-start.4 = (f32[128,1792]{1,0:T(8,128)S(1)}, f32[128,1792]{1,0:T(8,128)}, u32[]{:S(2)}) copy-start(f32[128,1792]{1,0:T(8,128)} %get-tuple-element.19) | copy-start | bytes 2752516
  63.9 2.9 %copy-start.5 = (f32[128,1792]{1,0:T(8,128)S(1)}, f32[128,1792]{1,0:T(8,128)}, u32[]{:S(2)}) copy-start(f32[128,1792]{1,0:T(8,128)} %get-tuple-element.20) | copy-start | bytes 2752516
  63.9 4.0 %copy-start.1 = (bf16[1,8192,64]{1,2,0:T(8,128)(2,1)S(1)}, bf16[1,8192,64]{1,2,0:T(8,128)(2,1)}, u32[]{:S(2)}) copy-start(bf16[1,8192,64]{1,2,0:T(8,128)(2,1)} %param.12) | copy-start | bytes 3145732

commit v14 on v13

v14 whole, which is shorter than its diff:
```python
import jax
import jax.numpy as jnp
from jax import lax
from jax.experimental import pallas as pl
from jax.experimental.pallas import tpu as pltpu
from jax.sharding import PartitionSpec as P

SUBLANES = 8
PIECES = 4


def _projection_kernel(block_ref, mine_ref, other_ref, gate_w_ref, up_w_ref, gate_ref, up_ref):
    k = pl.program_id(0)
    pieces = pl.num_programs(0) // 2

    @pl.when(k == 0)
    def _():
        gate_ref[...] = jnp.zeros_like(gate_ref)
        up_ref[...] = jnp.zeros_like(up_ref)

    def accumulate(x_ref):
        x = x_ref[...]
        gate_ref[...] += jnp.dot(x, gate_w_ref[...], preferred_element_type=jnp.float32)
        up_ref[...] += jnp.dot(x, up_w_ref[...], preferred_element_type=jnp.float32)

    pl.when(k < pieces)(lambda: accumulate(mine_ref))
    pl.when(k >= pieces)(lambda: accumulate(other_ref))


def projections(blocks, mine, other, gate_weight, up_weight):
    pieces, total, step = mine.shape
    width, hidden = gate_weight.shape
    weight_bytes = 2 * width * hidden * gate_weight.dtype.itemsize

    def weight_block(k, block_ref):
        return (block_ref[k], 0)

    return pl.pallas_call(
        _projection_kernel,
        grid_spec=pltpu.PrefetchScalarGridSpec(
            num_scalar_prefetch=1,
            grid=(2 * pieces,),
            in_specs=[
                pl.BlockSpec((None, total, step), lambda k, b: (jnp.minimum(k, pieces - 1), 0, 0)),
                pl.BlockSpec((None, total, step), lambda k, b: (jnp.maximum(k - pieces, 0), 0, 0)),
                pl.BlockSpec((step, hidden), weight_block),
                pl.BlockSpec((step, hidden), weight_block),
            ],
            out_specs=[
                pl.BlockSpec((total, hidden), lambda k, b: (0, 0)),
                pl.BlockSpec((total, hidden), lambda k, b: (0, 0)),
            ],
        ),
        out_shape=[jax.ShapeDtypeStruct((total, hidden), jnp.float32)] * 2,
        compiler_params=pltpu.CompilerParams(dimension_semantics=("arbitrary",)),
        cost_estimate=pl.CostEstimate(
            flops=4 * total * width * hidden,
            transcendentals=0,
            bytes_accessed=weight_bytes + total * width * 2 + 2 * total * hidden * 4,
        ),
    )(blocks, mine, other, gate_weight, up_weight)


def body(
    tokens,
    gate_weight,
    up_weight,
    adapter_down_weight,
    adapter_up_weight,
    token_adapter_index,
    adapter_slot_index,
):
    rows, width = tokens.shape
    slots_held = adapter_up_weight.shape[0]
    half = width // 2
    piece = half // PIECES
    me = lax.axis_index("tensor")
    core = me % 2
    spot = (me // 2) % PIECES
    cuts = tokens.reshape(rows, 2, PIECES, piece).transpose(2, 1, 0, 3).reshape(1, 2 * PIECES, rows, piece)
    copies = jnp.broadcast_to(cuts, (slots_held // (2 * PIECES), 2 * PIECES, rows, piece))
    own = lax.all_to_all(copies.reshape(slots_held, rows, piece), "tensor", 0, 0, tiled=False)
    own = own.reshape(slots_held * rows, piece)
    masks = [2 * m for m in range(PIECES)]
    got = [own] + [lax.ppermute(own, "tensor", [(j, j ^ m) for j in range(slots_held)]) for m in masks[1:]]
    mine = jnp.stack(got)
    other = lax.ppermute(mine, "tensor", [(j, j ^ 1) for j in range(slots_held)])
    total = own.shape[0]
    spots = spot ^ jnp.arange(PIECES, dtype=jnp.int32)
    blocks = jnp.concatenate([core * PIECES + spots, (1 - core) * PIECES + spots]).astype(jnp.int32)

    down = adapter_down_weight[0].reshape(2 * PIECES, piece, -1)
    low = jnp.einsum("ktc,kcr->tr", mine, jnp.take(down, blocks[:PIECES], axis=0), preferred_element_type=jnp.float32)
    low = low + jnp.einsum("ktc,kcr->tr", other, jnp.take(down, blocks[PIECES:], axis=0), preferred_element_type=jnp.float32)
    low = low.astype(jnp.bfloat16)
    rank = low.shape[1]
    named = token_adapter_index[:, :1] == jnp.arange(adapter_slot_index.shape[0], dtype=jnp.int32)[None, :]
    local_slot = jnp.sum(jnp.where(named, adapter_slot_index[None, :], 0), axis=1).astype(jnp.bfloat16)
    slot_rows = jnp.zeros((SUBLANES, total), jnp.bfloat16).at[0, :rows].set(local_slot)
    payload = jnp.concatenate([low.T, slot_rows], axis=0)
    sent = jnp.broadcast_to(payload[None], (slots_held,) + payload.shape)
    gathered = lax.all_to_all(sent, "tensor", 0, 0, tiled=False)
    slots = gathered[:, rank, :rows].reshape(total).astype(jnp.int32)
    hits = slots[None, None, :] == jnp.arange(slots_held, dtype=jnp.int32)[:, None, None]
    spread = jnp.where(hits, gathered[:, :rank, :], jnp.zeros((), jnp.bfloat16))

    gate, up = projections(blocks, mine, other, gate_weight, up_weight)
    delta = jnp.einsum("srt,srh->th", spread, adapter_up_weight, preferred_element_type=jnp.float32)
    return (jax.nn.silu(gate) * (up + delta)).astype(jnp.bfloat16)


def solution(mesh):
    in_specs = (
        P(("groups", "tensor"), None),
        P(None, "tensor"),
        P(None, "tensor"),
        P("tensor", None, None),
        P(None, None, "tensor"),
        P(("groups", "tensor"), None),
        P(),
    )
    out_specs = P("groups", "tensor")
    return jax.shard_map(body, mesh=mesh, in_specs=in_specs, out_specs=out_specs, check_vma=False)
```

time: 68.1 us -> 69.2 us (1.016)
  blocking collectives: 32 us -> 17.2 us
  waiting for transfers between devices: 1.6 us -> 9.34 us
  local copies, waits for them, and re-layouts: 1.93 us -> 5.5 us
  starting transfers between devices: 5.36 us -> 7.11 us
  matrix products: 3.82 us -> 5.08 us
  other arithmetic: 1.3 us -> 2.11 us
    all_to_all x1, blocking collectives: 32 us -> 17.2 us  [body(): lax.all_to_all(copies.reshape(slots_held, rows, piece), 'tensor', 0, 0, t...]
    ppermute x0 -> x3, waiting for transfers between devices: none -> 8.63 us  [body(): lax.ppermute(own, 'tensor', [(j, j ^ m) for j in range(slots_held)])]
    ppermute x0 -> x3, starting transfers between devices: none -> 3.49 us  [body(): lax.ppermute(own, 'tensor', [(j, j ^ m) for j in range(slots_held)])]
    unnamed x16 -> x11, local copies, waits for them, and re-layouts: 0.03 us -> 1.85 us
    dot_general x2, matrix products: 0.96 us -> 2.27 us  [the longest x1 1.75 us: body(): jnp.einsum('ktc,kcr->tr', other, jnp.take(down, blocks[PIECES:], axis=0),...]
    gather x0 -> x2, local copies, waits for them, and re-layouts: none -> 1.16 us  [the longest x1 0.58 us: body(): jnp.take(down, blocks[PIECES:], axis=0)]
    all_to_all x1, starting transfers between devices: 4.59 us -> 3.54 us  [body(): gathered = lax.all_to_all(sent, 'tensor', 0, 0, tiled=False)]
    reshape x0 -> x1, local copies, waits for them, and re-layouts: none -> 0.98 us  [body(): tokens.reshape(rows, 2, PIECES, piece).transpose(2, 1, 0, 3)]
  transfers between devices with their start and end apart: 2 -> 5, of which waited for: 1 -> 4; matrix products, arithmetic and copies ran while one was open for 1% -> 6% of each run, Pallas kernels for 32% -> 32%
where the time goes in v14:
time: 69.2 us; the launch traced here: 68.9 us
  Pallas kernels  22.3 us (32%)
  blocking collectives  17.2 us (25%)
  waiting for transfers between devices  9.34 us (13%)
  starting transfers between devices  7.11 us (10%)
  local copies, waits for them, and re-layouts  5.5 us (8%)
  matrix products  5.08 us (7%)
  other arithmetic  2.11 us (3%)
    pallas_call x1, Pallas kernels, projections(): pl.pallas_call(_projection_kernel, grid_spec=pltpu.PrefetchScalarGridSpec...  22.3 us
    all_to_all x1, blocking collectives, body(): lax.all_to_all(copies.reshape(slots_held, rows, piece), 'tensor', 0, 0, t...  17.2 us
    ppermute x3, waiting for transfers between devices, body(): lax.ppermute(own, 'tensor', [(j, j ^ m) for j in range(slots_held)])  8.63 us
    all_to_all x1, starting transfers between devices, body(): gathered = lax.all_to_all(sent, 'tensor', 0, 0, tiled=False)  3.54 us
    ppermute x3, starting transfers between devices, body(): lax.ppermute(own, 'tensor', [(j, j ^ m) for j in range(slots_held)])  3.49 us
    dot_general x1, matrix products, body(): jnp.einsum('srt,srh->th', spread, adapter_up_weight, preferred_element_ty...  2.82 us
    unnamed x11, local copies, waits for them, and re-layouts  1.85 us
    dot_general x1, matrix products, body(): jnp.einsum('ktc,kcr->tr', other, jnp.take(down, blocks[PIECES:], axis=0),...  1.75 us
  transfers between devices with their start and end apart: 5, of which 4 were waited for; matrix products, arithmetic and copies ran while one was open for 6% of the time, Pallas kernels for 32%

profile of v14, /device:TPU:0, one launch (start us, length us, event | category | flops | bytes accessed | tf_op | source)
XLA Modules:
  0.0 68.9 jit_solution(14985555608058094182)
XLA Ops:
  0.0 1.0 %reshape.81 = bf16[8,2,4,1024]{3,2,1,0:T(4,128)(2,1)S(1)} reshape(bf16[8,8192]{1,0:T(8,128)(2,1)} %param.11) | data formatting | bytes 262144 | tf_op jit(solution)/shard_map/reshape | solution.py:80
  1.0 0.1 copy.19
  1.1 17.2 %all_to_all.10 = bf16[16,8,1024]{2,1,0:T(8,128)(2,1)S(1)} all-to-all(bf16[16,8,1024]{2,1,0:T(8,128)(2,1)S(1)} %bitcast.31), channel_id=1, replica_groups=mesh['groups'=2,'tensor'=16] {'tensor'}, dimensions={0} | all-to-all | bytes 524288 | tf_op jit(solution)/shard_map/all_to_all | solution.py:82
  18.3 0.6 collective-permute-start.2
  18.9 0.3 collective-permute-start.1
  19.2 2.6 %collective-permute-start = (bf16[128,1024]{1,0:T(8,128)(2,1)S(1)}, bf16[128,1024]{1,0:T(8,128)(2,1)S(1)}, u32[]{:S(2)}, u32[]{:S(2)}) collective-permute-start(bf16[128,1024]{1,0:T(8,128)(2,1)S(1)} %bitcast.34), channel_id=1, source_target_pairs={{0,2},{1,3},{2,0},{3,1},{4,6},{5,7},{6,4},{7,5},{8,10},{9,11},{10,... | collective-permute-start | bytes 786440 | tf_op jit(solution)/shard_map/ppermute | solution.py:85
  21.8 1.8 %copy.22 = bf16[8,8,8,1024]{3,2,1,0:T(8,128)(2,1)S(1)} copy(bf16[8,8,8,1024]{3,1,2,0:T(8,128)(2,1)} %bitcast.30) | data formatting | bytes 2097152
  23.6 0.6 copy.20
  24.2 0.0 copy-start.3
  24.2 0.0 copy-start.4
  24.3 4.2 %collective-permute-done.2 = bf16[128,1024]{1,0:T(8,128)(2,1)S(1)} collective-permute-done((bf16[128,1024]{1,0:T(8,128)(2,1)S(1)}, bf16[128,1024]{1,0:T(8,128)(2,1)S(1)}, u32[]{:S(2)}, u32[]{:S(2)}) %collective-permute-start.2) | collective-permute-done | bytes 262176 | tf_op jit(solution)/shard_map/ppermute | solution.py:85
  28.5 3.4 %collective-permute-done.1 = bf16[128,1024]{1,0:T(8,128)(2,1)S(1)} collective-permute-done((bf16[128,1024]{1,0:T(8,128)(2,1)S(1)}, bf16[128,1024]{1,0:T(8,128)(2,1)S(1)}, u32[]{:S(2)}, u32[]{:S(2)}) %collective-permute-start.1) | collective-permute-done | bytes 262176 | tf_op jit(solution)/shard_map/ppermute | solution.py:85
  31.9 1.0 %collective-permute-done = bf16[128,1024]{1,0:T(8,128)(2,1)S(1)} collective-permute-done((bf16[128,1024]{1,0:T(8,128)(2,1)S(1)}, bf16[128,1024]{1,0:T(8,128)(2,1)S(1)}, u32[]{:S(2)}, u32[]{:S(2)}) %collective-permute-start) | collective-permute-done | bytes 262176 | tf_op jit(solution)/shard_map/ppermute | solution.py:85
  32.9 0.1 pad_maximum_fusion.mine_ref
  33.0 0.0 copy-start
  33.1 0.1 collective-permute-start.3
  33.2 0.6 gather_fusion.1
  33.8 0.6 gather_fusion
  34.4 0.6 pad_add_fusion.block_ref
  35.0 0.0 copy-done.3
  35.0 0.0 copy-done.4
  35.0 0.2 select_reduce_fusion
  35.2 0.7 %collective-permute-done.3.other_ref = bf16[4,128,1024]{2,1,0:T(8,128)(2,1)} collective-permute-done((bf16[4,128,1024]{2,1,0:T(8,128)(2,1)S(1)}, bf16[4,128,1024]{2,1,0:T(8,128)(2,1)}, u32[]{:S(2)}, u32[]{:S(2)}) %collective-permute-start.3) | collective-permute-done | bytes 1048608 | tf_op jit(solution)/shard_map/ppermute | solution.py:87
  35.9 1.7 %convolution_bitcast_fusion.1 = f32[64,128]{1,0:T(8,128)S(1)} fusion(bf16[4,128,1024]{2,1,0:T(8,128)(2,1)} %collective-permute-done.3.other_ref, bf16[4,1024,64]{1,2,0:T(8,128)(2,1)S(1)} %gather_fusion.1, pred[4]{0:T(512)(128)(4,1)S(1)} %get-tuple-element.24), kind=kOutput, calls=%fused_computation.3 | convolution fusion | flops 67371008 | bytes 1605636 | tf_op jit(solution)/shard_map/ktc,kcr->tr/dot_general | solution.py:94
  37.7 0.5 fusion.1
  38.2 0.0 copy-done
  38.2 0.8 %broadcast_in_dim.55 = bf16[16,72,128]{2,1,0:T(8,128)(2,1)} broadcast(bf16[72,128]{1,0:T(8,128)(2,1)S(1)} %fusion.11), dimensions={1,2} | broadcast | bytes 313344 | tf_op jit(solution)/shard_map/broadcast_in_dim | solution.py:101
  39.0 3.5 %all-to-all-start.1 = ((bf16[16,72,128]{2,1,0:T(8,128)(2,1)}), bf16[16,72,128]{2,1,0:T(8,128)(2,1)S(1)}, u32[]{:S(2)}, u32[]{:S(2)}) async-start(bf16[16,72,128]{2,1,0:T(8,128)(2,1)} %broadcast_in_dim.55), calls=%async_computation.1 | async-start | bytes 589824 | tf_op jit(solution)/shard_map/all_to_all | solution.py:102
  42.5 22.3 %shard_map.73 = (f32[128,1792]{1,0:T(8,128)}, f32[128,1792]{1,0:T(8,128)}) custom-call(s32[8]{0:T(128)} %pad_add_fusion.block_ref, bf16[4,128,1024]{2,1,0:T(8,128)(2,1)} %copy-done, bf16[4,128,1024]{2,1,0:T(8,128)(2,1)} %collective-permute-done.3.other_ref, bf16[8192,1792]{1,0:T(8,128)(2,1)} %gate_w_ref.1, bf16[8192,1792]{1,0:T(8,128)(2,1)} %up_w_ref.1), custom_call_target="tpu_custom_call" | custom-call | flops 7516192768 | bytes 62652416 | tf_op jit(solution)/shard_map/pallas_call | solution.py:38
  64.8 0.0 copy-start.1
  64.8 0.0 copy-start.2
  64.8 0.0 all-to-all-done.1
  64.9 0.1 reshape.84
  65.0 2.8 %convolution_bitcast_fusion = f32[128,1792]{1,0:T(8,128)S(1)} fusion(bf16[16,64,1792]{2,1,0:T(8,128)(2,1)} %param.15, bf16[16,72,128]{2,1,0:T(8,128)(2,1)S(1)} %all-to-all-done.1, pred[16,128]{1,0:T(8,128)(4,1)S(1)} %iota_compare_fusion.1), kind=kOutput, calls=%fused_computation.2 | convolution fusion | flops 469893120 | bytes 4851712 | tf_op jit(solution)/shard_map/srt,srh->th/dot_general | solution.py:108
  67.8 0.0 copy-done.1
  67.8 0.0 copy-done.2
  67.8 1.1 %multiply_convert_fusion = bf16[128,1792]{1,0:T(8,128)(2,1)} fusion(f32[128,1792]{1,0:T(8,128)S(1)} %copy-done.2, f32[128,1792]{1,0:T(8,128)S(1)} %convolution_bitcast_fusion, f32[128,1792]{1,0:T(8,128)S(1)} %copy-done.1), kind=kLoop, calls=%fused_computation.8 | loop fusion | flops 1605632 | bytes 3211264 | tf_op jit(solution)/shard_map/convert_element_type | solution.py:109
  (10 shorter events, 0.1 us)
Async XLA Ops:
  18.3 10.1 %collective-permute-start.2 = (bf16[128,1024]{1,0:T(8,128)(2,1)S(1)}, bf16[128,1024]{1,0:T(8,128)(2,1)S(1)}, u32[]{:S(2)}, u32[]{:S(2)}) collective-permute-start(bf16[128,1024]{1,0:T(8,128)(2,1)S(1)} %bitcast.32), channel_id=1, source_target_pairs={{0,6},{1,7},{2,4},{3,5},{4,2},{5,3},{6,0},{7,1},{8,14},{9,15},{10,... | collective-permute-start | bytes 786440 | tf_op jit(solution)/shard_map/ppermute | solution.py:85
  18.9 13.0 %collective-permute-start.1 = (bf16[128,1024]{1,0:T(8,128)(2,1)S(1)}, bf16[128,1024]{1,0:T(8,128)(2,1)S(1)}, u32[]{:S(2)}, u32[]{:S(2)}) collective-permute-start(bf16[128,1024]{1,0:T(8,128)(2,1)S(1)} %bitcast.33), channel_id=1, source_target_pairs={{0,4},{1,5},{2,6},{3,7},{4,0},{5,1},{6,2},{7,3},{8,12},{9,13},{10,... | collective-permute-start | bytes 786440 | tf_op jit(solution)/shard_map/ppermute | solution.py:85
  19.2 13.7 %collective-permute-start = (bf16[128,1024]{1,0:T(8,128)(2,1)S(1)}, bf16[128,1024]{1,0:T(8,128)(2,1)S(1)}, u32[]{:S(2)}, u32[]{:S(2)}) collective-permute-start(bf16[128,1024]{1,0:T(8,128)(2,1)S(1)} %bitcast.34), channel_id=1, source_target_pairs={{0,2},{1,3},{2,0},{3,1},{4,6},{5,7},{6,4},{7,5},{8,10},{9,11},{10,... | collective-permute-start | bytes 786440 | tf_op jit(solution)/shard_map/ppermute | solution.py:85
  24.2 10.8 %copy-start.3 = (s32[16]{0:T(128)S(1)}, s32[16]{0:T(128)}, u32[]{:S(2)}) copy-start(s32[16]{0:T(128)} %param.17) | copy-start | bytes 196
  24.2 10.8 %copy-start.4 = (s32[8,1]{0,1:T(1,128)S(1)}, s32[8,1]{0,1:T(1,128)}, u32[]{:S(2)}) copy-start(s32[8,1]{0,1:T(1,128)} %param.16) | copy-start | bytes 100
  33.0 5.1 %copy-start = (bf16[4,128,1024]{2,1,0:T(8,128)(2,1)}, bf16[4,128,1024]{2,1,0:T(8,128)(2,1)S(1)}, u32[]{:S(2)}) copy-start(bf16[4,128,1024]{2,1,0:T(8,128)(2,1)S(1)} %pad_maximum_fusion.mine_ref) | copy-start | bytes 3145732
  33.1 2.9 %collective-permute-start.3 = (bf16[4,128,1024]{2,1,0:T(8,128)(2,1)S(1)}, bf16[4,128,1024]{2,1,0:T(8,128)(2,1)}, u32[]{:S(2)}, u32[]{:S(2)}) collective-permute-start(bf16[4,128,1024]{2,1,0:T(8,128)(2,1)S(1)} %pad_maximum_fusion.mine_ref), channel_id=1, source_target_pairs={{0,1},{1,0},{2,3},{3,2},{4,5},{5,4},{6,7},{7,6},{8,9},{9,8},{10,11... | collective-permute-start | bytes 3145736 | tf_op jit(solution)/shard_map/ppermute | solution.py:87
  39.0 25.9 %all-to-all-start.1 = ((bf16[16,72,128]{2,1,0:T(8,128)(2,1)}), bf16[16,72,128]{2,1,0:T(8,128)(2,1)S(1)}, u32[]{:S(2)}, u32[]{:S(2)}) async-start(bf16[16,72,128]{2,1,0:T(8,128)(2,1)} %broadcast_in_dim.55), calls=%async_computation.1 | async-start | bytes 589824 | tf_op jit(solution)/shard_map/all_to_all | solution.py:102
  64.8 3.0 %copy-start.1 = (f32[128,1792]{1,0:T(8,128)S(1)}, f32[128,1792]{1,0:T(8,128)}, u32[]{:S(2)}) copy-start(f32[128,1792]{1,0:T(8,128)} %get-tuple-element.20) | copy-start | bytes 2752516
  64.8 3.0 %copy-start.2 = (f32[128,1792]{1,0:T(8,128)S(1)}, f32[128,1792]{1,0:T(8,128)}, u32[]{:S(2)}) copy-start(f32[128,1792]{1,0:T(8,128)} %get-tuple-element.21) | copy-start | bytes 2752516

commit v15 on v14

--- a/solution.py
+++ b/solution.py
@@ -6,7 +6,7 @@
 from jax.sharding import PartitionSpec as P
 
 SUBLANES = 8
-PIECES = 4
+PIECES = 2
 
 
 def _projection_kernel(block_ref, mine_ref, other_ref, gate_w_ref, up_w_ref, gate_ref, up_ref):

time: 69.2 us -> 75.2 us (1.087)
  blocking collectives: 17.2 us -> 21.7 us
  starting transfers between devices: 7.11 us -> 4.85 us
  waiting for transfers between devices: 9.34 us -> 11.6 us
  matrix products: 5.08 us -> 6.29 us
    all_to_all x1, blocking collectives: 17.2 us -> 21.7 us  [body(): lax.all_to_all(copies.reshape(slots_held, rows, piece), 'tensor', 0, 0, t...]
    ppermute x3 -> x1, starting transfers between devices: 3.49 us -> 0.4 us  [body(): lax.ppermute(own, 'tensor', [(j, j ^ m) for j in range(slots_held)])]
    ppermute x3 -> x1, waiting for transfers between devices: 8.63 us -> 11 us  [body(): lax.ppermute(own, 'tensor', [(j, j ^ m) for j in range(slots_held)])]
    another operation x1 -> x2, local copies, waits for them, and re-layouts: 0.58 us -> 2.42 us  [body(): down = adapter_down_weight[0].reshape(2 * PIECES, piece, -1)]
    unnamed x11 -> x14, local copies, waits for them, and re-layouts: 1.85 us -> 0.03 us
    dot_general x1, matrix products: 0.52 us -> 1.72 us  [body(): jnp.einsum('ktc,kcr->tr', mine, jnp.take(down, blocks[:PIECES], axis=0),...]
    all_to_all x1, starting transfers between devices: 3.54 us -> 4.38 us  [body(): gathered = lax.all_to_all(sent, 'tensor', 0, 0, tiled=False)]
  transfers between devices with their start and end apart: 5 -> 3, of which waited for: 4 -> 2; matrix products, arithmetic and copies ran while one was open for 6% -> 6% of each run, Pallas kernels for 32% -> 30%
where the time goes in v15:
time: 75.2 us; the launch traced here: 74.8 us
  Pallas kernels  22.5 us (30%)
  blocking collectives  21.7 us (29%)
  waiting for transfers between devices  11.6 us (15%)
  matrix products  6.29 us (8%)
  local copies, waits for them, and re-layouts  5.56 us (7%)
  starting transfers between devices  4.85 us (6%)
  other arithmetic  2.07 us (3%)
    pallas_call x1, Pallas kernels, projections(): pl.pallas_call(_projection_kernel, grid_spec=pltpu.PrefetchScalarGridSpec...  22.5 us
    all_to_all x1, blocking collectives, body(): lax.all_to_all(copies.reshape(slots_held, rows, piece), 'tensor', 0, 0, t...  21.7 us
    ppermute x1, waiting for transfers between devices, body(): lax.ppermute(own, 'tensor', [(j, j ^ m) for j in range(slots_held)])  11 us
    all_to_all x1, starting transfers between devices, body(): gathered = lax.all_to_all(sent, 'tensor', 0, 0, tiled=False)  4.38 us
    dot_general x1, matrix products, body(): jnp.einsum('srt,srh->th', spread, adapter_up_weight, preferred_element_ty...  2.83 us
    another operation x2, local copies, waits for them, and re-layouts, body(): down = adapter_down_weight[0].reshape(2 * PIECES, piece, -1)  2.42 us
    dot_general x1, matrix products, body(): jnp.einsum('ktc,kcr->tr', other, jnp.take(down, blocks[PIECES:], axis=0),...  1.75 us
    dot_general x1, matrix products, body(): jnp.einsum('ktc,kcr->tr', mine, jnp.take(down, blocks[:PIECES], axis=0),...  1.72 us
  transfers between devices with their start and end apart: 3, of which 2 were waited for; matrix products, arithmetic and copies ran while one was open for 6% of the time, Pallas kernels for 30%

profile of v15, /device:TPU:0, one launch (start us, length us, event | category | flops | bytes accessed | tf_op | source)
XLA Modules:
  0.0 74.8 jit_solution(524023698879495776)
XLA Ops:
  0.0 1.0 %reshape.81 = bf16[8,2,2,2048]{3,2,1,0:T(2,128)(2,1)S(1)} reshape(bf16[8,8192]{1,0:T(8,128)(2,1)} %param.11) | data formatting | bytes 262144 | tf_op jit(solution)/shard_map/reshape | solution.py:80
  1.0 0.1 copy.19
  1.1 21.7 %all_to_all.10 = bf16[16,8,2048]{2,1,0:T(8,128)(2,1)S(1)} all-to-all(bf16[16,8,2048]{2,1,0:T(8,128)(2,1)S(1)} %bitcast.23), channel_id=1, replica_groups=mesh['groups'=2,'tensor'=16] {'tensor'}, dimensions={0} | all-to-all | bytes 1048576 | tf_op jit(solution)/shard_map/all_to_all | solution.py:82
  22.8 0.0 copy-start.1
  22.8 0.4 collective-permute-start
  23.2 1.8 %reshape_squeeze.4 = bf16[4,2048,64]{1,0,2:T(4,128)(2,1)S(1)} reshape(bf16[1,8192,64]{1,2,0:T(8,128)(2,1)} %param.14) | data formatting | bytes 2097152 | tf_op jit(solution)/shard_map/reshape;squeeze | solution.py:92
  25.0 0.6 copy.20
  25.6 0.0 copy-start.5
  25.6 0.0 copy-start.6
  25.7 11.0 %collective-permute-done = bf16[128,2048]{1,0:T(8,128)(2,1)S(1)} collective-permute-done((bf16[128,2048]{1,0:T(8,128)(2,1)S(1)}, bf16[128,2048]{1,0:T(8,128)(2,1)S(1)}, u32[]{:S(2)}, u32[]{:S(2)}) %collective-permute-start) | collective-permute-done | bytes 524320 | tf_op jit(solution)/shard_map/ppermute | solution.py:85
  36.6 0.0 copy-start.4
  36.6 0.1 pad_maximum_fusion.mine_ref
  36.7 0.0 copy-start
  36.7 0.1 collective-permute-start.1
  36.8 0.0 copy-done.1
  36.9 0.6 gather_fusion.1
  37.5 0.0 copy-done.4
  37.5 0.6 gather_fusion
  38.1 0.6 pad_add_fusion.block_ref
  38.7 0.0 copy-done.5
  38.7 0.0 copy-done.6
  38.7 0.2 select_reduce_fusion
  38.9 0.7 collective-permute-done.1.other_ref
  39.6 1.7 %convolution_bitcast_fusion.1 = f32[64,128]{1,0:T(8,128)S(1)} fusion(bf16[2,128,2048]{2,1,0:T(8,128)(2,1)} %collective-permute-done.1.other_ref, bf16[2,2048,64]{1,2,0:T(8,128)(2,1)S(1)} %gather_fusion.1, pred[2]{0:T(512)(128)(4,1)S(1)} %get-tuple-element.24), kind=kOutput, calls=%fused_computation.3 | convolution fusion | flops 67371008 | bytes 1605634 | tf_op jit(solution)/shard_map/ktc,kcr->tr/dot_general | solution.py:94
  41.3 1.7 %fusion.1 = bf16[64,128]{1,0:T(8,128)(2,1)S(1)} fusion(f32[64,128]{1,0:T(8,128)S(1)} %convolution_bitcast_fusion.1, bf16[2,2048,64]{1,2,0:T(8,128)(2,1)S(1)} %gather_fusion, pred[2]{0:T(512)(128)(4,1)S(1)} %get-tuple-element.26, bf16[1,128,2048]{2,1,0:T(8,128)(2,1)} %bitcast.30, bf16[1,128,2048]{2,1,0:T(8,128)(2,1)} %bitcast.26), kind=kOutput, calls=%fused_computation.6 | convolution fusion | flops 67911680 | bytes 1622018 | tf_op jit(solution)/shard_map/ktc,kcr->tr/dot_general | solution.py:93
  43.1 0.0 copy-done
  43.1 0.8 %broadcast_in_dim.55 = bf16[16,72,128]{2,1,0:T(8,128)(2,1)} broadcast(bf16[72,128]{1,0:T(8,128)(2,1)S(1)} %fusion.11), dimensions={1,2} | broadcast | bytes 313344 | tf_op jit(solution)/shard_map/broadcast_in_dim | solution.py:101
  43.8 4.4 %all-to-all-start.1 = ((bf16[16,72,128]{2,1,0:T(8,128)(2,1)}), bf16[16,72,128]{2,1,0:T(8,128)(2,1)S(1)}, u32[]{:S(2)}, u32[]{:S(2)}) async-start(bf16[16,72,128]{2,1,0:T(8,128)(2,1)} %broadcast_in_dim.55), calls=%async_computation.1 | async-start | bytes 589824 | tf_op jit(solution)/shard_map/all_to_all | solution.py:102
  48.2 22.5 %shard_map.73 = (f32[128,1792]{1,0:T(8,128)}, f32[128,1792]{1,0:T(8,128)}) custom-call(s32[4]{0:T(128)} %pad_add_fusion.block_ref, bf16[2,128,2048]{2,1,0:T(8,128)(2,1)} %copy-done, bf16[2,128,2048]{2,1,0:T(8,128)(2,1)} %collective-permute-done.1.other_ref, bf16[8192,1792]{1,0:T(8,128)(2,1)} %gate_w_ref.1, bf16[8192,1792]{1,0:T(8,128)(2,1)} %up_w_ref.1), custom_call_target="tpu_custom_call" | custom-call | flops 7516192768 | bytes 62652416 | tf_op jit(solution)/shard_map/pallas_call | solution.py:38
  70.8 0.0 copy-start.2
  70.8 0.0 copy-start.3
  70.8 0.0 all-to-all-done.1
  70.8 0.1 reshape.84
  70.9 2.8 %convolution_bitcast_fusion = f32[128,1792]{1,0:T(8,128)S(1)} fusion(bf16[16,64,1792]{2,1,0:T(8,128)(2,1)} %param.15, bf16[16,72,128]{2,1,0:T(8,128)(2,1)S(1)} %all-to-all-done.1, pred[16,128]{1,0:T(8,128)(4,1)S(1)} %iota_compare_fusion.1), kind=kOutput, calls=%fused_computation.2 | convolution fusion | flops 469893120 | bytes 4851712 | tf_op jit(solution)/shard_map/srt,srh->th/dot_general | solution.py:108
  73.8 0.0 copy-done.2
  73.8 0.0 copy-done.3
  73.8 1.1 %multiply_convert_fusion = bf16[128,1792]{1,0:T(8,128)(2,1)} fusion(f32[128,1792]{1,0:T(8,128)S(1)} %copy-done.3, f32[128,1792]{1,0:T(8,128)S(1)} %convolution_bitcast_fusion, f32[128,1792]{1,0:T(8,128)S(1)} %copy-done.2), kind=kLoop, calls=%fused_computation.8 | loop fusion | flops 1605632 | bytes 3211264 | tf_op jit(solution)/shard_map/convert_element_type | solution.py:109
  (10 shorter events, 0.1 us)
Async XLA Ops:
  22.8 14.1 %copy-start.1 = (bf16[16,8,2048]{2,1,0:T(8,128)(2,1)}, bf16[16,8,2048]{2,1,0:T(8,128)(2,1)S(1)}, u32[]{:S(2)}) copy-start(bf16[16,8,2048]{2,1,0:T(8,128)(2,1)S(1)} %all_to_all.10) | copy-start | bytes 1572868
  22.8 13.8 %collective-permute-start = (bf16[128,2048]{1,0:T(8,128)(2,1)S(1)}, bf16[128,2048]{1,0:T(8,128)(2,1)S(1)}, u32[]{:S(2)}, u32[]{:S(2)}) collective-permute-start(bf16[128,2048]{1,0:T(8,128)(2,1)S(1)} %bitcast.24), channel_id=1, source_target_pairs={{0,2},{1,3},{2,0},{3,1},{4,6},{5,7},{6,4},{7,5},{8,10},{9,11},{10,... | collective-permute-start | bytes 1572872 | tf_op jit(solution)/shard_map/ppermute | solution.py:85
  25.6 13.1 %copy-start.5 = (s32[16]{0:T(128)S(1)}, s32[16]{0:T(128)}, u32[]{:S(2)}) copy-start(s32[16]{0:T(128)} %param.17) | copy-start | bytes 196
  25.6 13.1 %copy-start.6 = (s32[8,1]{0,1:T(1,128)S(1)}, s32[8,1]{0,1:T(1,128)}, u32[]{:S(2)}) copy-start(s32[8,1]{0,1:T(1,128)} %param.16) | copy-start | bytes 100
  36.6 0.8 %copy-start.4 = (bf16[128,2048]{1,0:T(8,128)(2,1)}, bf16[128,2048]{1,0:T(8,128)(2,1)S(1)}, u32[]{:S(2)}) copy-start(bf16[128,2048]{1,0:T(8,128)(2,1)S(1)} %collective-permute-done) | copy-start | bytes 1572868
  36.7 6.3 %copy-start = (bf16[2,128,2048]{2,1,0:T(8,128)(2,1)}, bf16[2,128,2048]{2,1,0:T(8,128)(2,1)S(1)}, u32[]{:S(2)}) copy-start(bf16[2,128,2048]{2,1,0:T(8,128)(2,1)S(1)} %pad_maximum_fusion.mine_ref) | copy-start | bytes 3145732
  36.7 2.9 %collective-permute-start.1 = (bf16[2,128,2048]{2,1,0:T(8,128)(2,1)S(1)}, bf16[2,128,2048]{2,1,0:T(8,128)(2,1)}, u32[]{:S(2)}, u32[]{:S(2)}) collective-permute-start(bf16[2,128,2048]{2,1,0:T(8,128)(2,1)S(1)} %pad_maximum_fusion.mine_ref), channel_id=1, source_target_pairs={{0,1},{1,0},{2,3},{3,2},{4,5},{5,4},{6,7},{7,6},{8,9},{9,8},{10,11... | collective-permute-start | bytes 3145736 | tf_op jit(solution)/shard_map/ppermute | solution.py:87
  43.8 26.9 %all-to-all-start.1 = ((bf16[16,72,128]{2,1,0:T(8,128)(2,1)}), bf16[16,72,128]{2,1,0:T(8,128)(2,1)S(1)}, u32[]{:S(2)}, u32[]{:S(2)}) async-start(bf16[16,72,128]{2,1,0:T(8,128)(2,1)} %broadcast_in_dim.55), calls=%async_computation.1 | async-start | bytes 589824 | tf_op jit(solution)/shard_map/all_to_all | solution.py:102
  70.8 3.0 %copy-start.2 = (f32[128,1792]{1,0:T(8,128)S(1)}, f32[128,1792]{1,0:T(8,128)}, u32[]{:S(2)}) copy-start(f32[128,1792]{1,0:T(8,128)} %get-tuple-element.20) | copy-start | bytes 2752516
  70.8 3.0 %copy-start.3 = (f32[128,1792]{1,0:T(8,128)S(1)}, f32[128,1792]{1,0:T(8,128)}, u32[]{:S(2)}) copy-start(f32[128,1792]{1,0:T(8,128)} %get-tuple-element.21) | copy-start | bytes 2752516

commit v16 on v12

--- a/solution.py
+++ b/solution.py
@@ -85,10 +85,12 @@
     other = lax.ppermute(mine, "tensor", [(j, j ^ 1) for j in range(slots_held)])
     total = mine.shape[0]
 
+    partners = [(j, j ^ 1) for j in range(slots_held)]
     down = adapter_down_weight[0]
+    lent = lax.ppermute(lax.dynamic_slice_in_dim(down, (1 - order) * half, half), "tensor", partners)
     low = jnp.dot(mine, lax.dynamic_slice_in_dim(down, order * half, half), preferred_element_type=jnp.float32)
-    low = low + jnp.dot(other, lax.dynamic_slice_in_dim(down, (1 - order) * half, half), preferred_element_type=jnp.float32)
-    low = low.astype(jnp.bfloat16)
+    lent_part = jnp.dot(mine, lent, preferred_element_type=jnp.float32)
+    low = (low + lax.ppermute(lent_part, "tensor", partners)).astype(jnp.bfloat16)
     rank = low.shape[1]
     local_slot = jnp.take(adapter_slot_index, token_adapter_index[:, 0], axis=0).astype(jnp.bfloat16)
     slot_rows = jnp.zeros((SUBLANES, total), jnp.bfloat16).at[0, :rows].set(local_slot)

time: 68.1 us -> 79.9 us (1.17)
  blocking collectives: 32 us -> 0 us
  waiting for transfers between devices: 1.11 us -> 32.3 us
  starting transfers between devices: 5.37 us -> 15.5 us
  other arithmetic: 1.12 us -> 2.63 us
  local copies, waits for them, and re-layouts: 2.58 us -> 3.58 us
    all_to_all x1 -> x0, blocking collectives: 32 us -> none  [body(): lax.all_to_all(copies, 'tensor', 0, 0, tiled=False)]
    all_to_all x0 -> x1, waiting for transfers between devices: none -> 20.9 us  [body(): lax.all_to_all(copies, 'tensor', 0, 0, tiled=False)]
    all_to_all x1, waiting for transfers between devices: 0.01 us -> 10.2 us  [body(): gathered = lax.all_to_all(sent, 'tensor', 0, 0, tiled=False)]
    all_to_all x0 -> x1, starting transfers between devices: none -> 7.39 us  [body(): lax.all_to_all(copies, 'tensor', 0, 0, tiled=False)]
    all_to_all x1, starting transfers between devices: 4.6 us -> 6.61 us  [body(): gathered = lax.all_to_all(sent, 'tensor', 0, 0, tiled=False)]
    convert_element_type x1, other arithmetic: 1.03 us -> 2.54 us  [body(): return (jax.nn.silu(gate) * (up + delta)).astype(jnp.bfloat16)]
    ppermute x0 -> x2, waiting for transfers between devices: none -> 1.23 us  [the longest x1 0.85 us: body(): lax.ppermute(lax.dynamic_slice_in_dim(down, (1 - order) * half, half), 't...]
    ppermute x0 -> x2, starting transfers between devices: none -> 1.13 us  [the longest x1 0.67 us: body(): lax.ppermute(lent_part, 'tensor', partners)]
  transfers between devices with their start and end apart: 2 -> 5, of which waited for: 1 -> 4; matrix products, arithmetic and copies ran while one was open for 2% -> 5% of each run, Pallas kernels for 32% -> 0%
where the time goes in v16:
time: 79.9 us; the launch traced here: 79.6 us
  waiting for transfers between devices  32.3 us (40%)
  Pallas kernels  21.7 us (27%)
  starting transfers between devices  15.5 us (19%)
  matrix products  3.7 us (5%)
  local copies, waits for them, and re-layouts  3.58 us (4%)
  other arithmetic  2.63 us (3%)
    pallas_call x1, Pallas kernels, projections(): pl.pallas_call(_projection_kernel, grid_spec=pltpu.PrefetchScalarGridSpec...  21.7 us
    all_to_all x1, waiting for transfers between devices, body(): lax.all_to_all(copies, 'tensor', 0, 0, tiled=False)  20.9 us
    all_to_all x1, waiting for transfers between devices, body(): gathered = lax.all_to_all(sent, 'tensor', 0, 0, tiled=False)  10.2 us
    all_to_all x1, starting transfers between devices, body(): lax.all_to_all(copies, 'tensor', 0, 0, tiled=False)  7.39 us
    all_to_all x1, starting transfers between devices, body(): gathered = lax.all_to_all(sent, 'tensor', 0, 0, tiled=False)  6.61 us
    dot_general x1, matrix products, body(): jnp.einsum('srt,srh->th', spread, adapter_up_weight, preferred_element_ty...  2.72 us
    convert_element_type x1, other arithmetic, body(): return (jax.nn.silu(gate) * (up + delta)).astype(jnp.bfloat16)  2.54 us
  transfers between devices with their start and end apart: 5, of which 4 were waited for; matrix products, arithmetic and copies ran while one was open for 5% of the time, Pallas kernels for 0%

profile of v16, /device:TPU:0, one launch (start us, length us, event | category | flops | bytes accessed | tf_op | source)
XLA Modules:
  0.0 79.6 jit_solution(18022657161831349024)
XLA Ops:
  0.0 0.0 copy-start
  0.0 0.0 copy-start.4
  0.0 0.0 copy-start.2
  0.0 1.0 %slice_bitcast_fusion.1 = (bf16[1,8,4096]{2,1,0:T(8,128)(2,1)S(1)}, bf16[1,8,4096]{2,1,0:T(8,128)(2,1)S(1)}) fusion(bf16[8,8192]{1,0:T(8,128)(2,1)} %param.9), kind=kLoop, calls=%fused_computation.12 | loop fusion | bytes 262144 | tf_op jit(solution)/shard_map/stack | solution.py:82
  1.0 1.1 %broadcast_in_dim.14 = bf16[8,2,8,4096]{3,2,1,0:T(8,128)(2,1)} broadcast(bf16[2,8,4096]{2,1,0:T(8,128)(2,1)S(1)} %pad_maximum_fusion), dimensions={1,2,3} | broadcast | bytes 1179648 | tf_op jit(solution)/shard_map/broadcast_in_dim | solution.py:83
  2.1 7.4 %all-to-all-start = ((bf16[16,8,4096]{2,1,0:T(8,128)(2,1)}), bf16[16,8,4096]{2,1,0:T(8,128)(2,1)S(1)}, u32[]{:S(2)}, u32[]{:S(2)}) async-start(bf16[16,8,4096]{2,1,0:T(8,128)(2,1)} %bitcast.3), calls=%async_computation | async-start | bytes 2097152 | tf_op jit(solution)/shard_map/all_to_all | solution.py:84
  9.5 0.0 copy-done
  9.5 0.5 collective-permute-start.1
  10.0 0.0 copy-done.4
  10.0 0.0 copy-done.2
  10.0 0.6 gather_fusion
  10.7 0.9 %collective-permute-done.1 = bf16[4096,64]{0,1:T(8,128)(2,1)S(1)} collective-permute-done((bf16[4096,64]{0,1:T(8,128)(2,1)S(1)}, bf16[4096,64]{0,1:T(8,128)(2,1)S(1)}, u32[]{:S(2)}, u32[]{:S(2)}) %collective-permute-start.1) | collective-permute-done | bytes 524320 | tf_op jit(solution)/shard_map/ppermute | solution.py:90
  11.5 20.9 %all-to-all-done = bf16[16,8,4096]{2,1,0:T(8,128)(2,1)S(1)} async-done(((bf16[16,8,4096]{2,1,0:T(8,128)(2,1)}), bf16[16,8,4096]{2,1,0:T(8,128)(2,1)S(1)}, u32[]{:S(2)}, u32[]{:S(2)}) %all-to-all-start) | async-done | bytes 1048608 | tf_op jit(solution)/shard_map/all_to_all | solution.py:84
  32.4 0.0 copy-start.3
  32.4 0.5 fusion.11
  32.9 0.7 collective-permute-start.2
  33.6 0.5 fusion
  34.1 0.4 collective-permute-done.2
  34.5 0.8 broadcast_in_dim.15
  35.2 6.6 %all-to-all-start.1 = ((bf16[16,72,128]{2,1,0:T(8,128)(2,1)}), bf16[16,72,128]{2,1,0:T(8,128)(2,1)S(1)}, u32[]{:S(2)}, u32[]{:S(2)}) async-start(bf16[16,72,128]{2,1,0:T(8,128)(2,1)} %broadcast_in_dim.15), calls=%async_computation.1 | async-start | bytes 589824 | tf_op jit(solution)/shard_map/all_to_all | solution.py:99
  41.8 0.4 collective-permute-start
  42.2 10.2 %all-to-all-done.1 = bf16[16,72,128]{2,1,0:T(8,128)(2,1)S(1)} async-done(((bf16[16,72,128]{2,1,0:T(8,128)(2,1)}), bf16[16,72,128]{2,1,0:T(8,128)(2,1)S(1)}, u32[]{:S(2)}, u32[]{:S(2)}) %all-to-all-start.1) | async-done | bytes 294944 | tf_op jit(solution)/shard_map/all_to_all | solution.py:99
  52.4 0.1 reshape.89
  52.5 2.7 %convolution_bitcast_fusion = f32[128,1792]{1,0:T(8,128)S(1)} fusion(bf16[16,64,1792]{2,1,0:T(8,128)(2,1)} %param.13, bf16[16,72,128]{2,1,0:T(8,128)(2,1)S(1)} %all-to-all-done.1, pred[16,128]{1,0:T(8,128)(4,1)S(1)} %iota_compare_fusion.1), kind=kOutput, calls=%fused_computation.1 | convolution fusion | flops 469893120 | bytes 4851712 | tf_op jit(solution)/shard_map/srt,srh->th/dot_general | solution.py:105
  55.3 0.0 copy-done.3
  55.3 0.0 collective-permute-done.other_ref
  55.3 0.0 copy-start.1
  55.3 21.7 %shard_map.73 = (f32[128,1792]{1,0:T(8,128)}, f32[128,1792]{1,0:T(8,128)}) custom-call(s32[1]{0:T(128)} %bitcast.order_ref, bf16[128,4096]{1,0:T(8,128)(2,1)} %bitcast.33, bf16[128,4096]{1,0:T(8,128)(2,1)} %collective-permute-done.other_ref, bf16[8192,1792]{1,0:T(8,128)(2,1)} %gate_w_ref.1, bf16[8192,1792]{1,0:T(8,128)(2,1)} %up_w_ref.1), custom_call_target="tpu_custom_call" | custom-call | flops 7516192768 | bytes 62652416 | tf_op jit(solution)/shard_map/pallas_call | solution.py:42
  77.0 2.5 %multiply_convert_fusion = bf16[128,1792]{1,0:T(8,128)(2,1)} fusion(f32[128,1792]{1,0:T(8,128)} %get-tuple-element.20, f32[128,1792]{1,0:T(8,128)S(1)} %convolution_bitcast_fusion, f32[128,1792]{1,0:T(8,128)} %get-tuple-element.19), kind=kLoop, calls=%fused_computation.2 | loop fusion | flops 1605632 | bytes 3211264 | tf_op jit(solution)/shard_map/convert_element_type | solution.py:106
  79.6 0.0 copy-done.1
  (9 shorter events, 0.1 us)
Async XLA Ops:
  0.0 9.5 %copy-start = (bf16[1,8192,64]{1,2,0:T(8,128)(2,1)S(1)}, bf16[1,8192,64]{1,2,0:T(8,128)(2,1)}, u32[]{:S(2)}) copy-start(bf16[1,8192,64]{1,2,0:T(8,128)(2,1)} %param.12) | copy-start | bytes 3145732
  0.0 10.0 %copy-start.4 = (s32[8,1]{0,1:T(1,128)S(1)}, s32[8,1]{0,1:T(1,128)}, u32[]{:S(2)}) copy-start(s32[8,1]{0,1:T(1,128)} %param.14) | copy-start | bytes 100
  0.0 10.0 %copy-start.2 = (s32[16]{0:T(128)S(1)}, s32[16]{0:T(128)}, u32[]{:S(2)}) copy-start(s32[16]{0:T(128)} %param.15) | copy-start | bytes 196
  2.1 30.3 %all-to-all-start = ((bf16[16,8,4096]{2,1,0:T(8,128)(2,1)}), bf16[16,8,4096]{2,1,0:T(8,128)(2,1)S(1)}, u32[]{:S(2)}, u32[]{:S(2)}) async-start(bf16[16,8,4096]{2,1,0:T(8,128)(2,1)} %bitcast.3), calls=%async_computation | async-start | bytes 2097152 | tf_op jit(solution)/shard_map/all_to_all | solution.py:84
  9.5 2.0 %collective-permute-start.1 = (bf16[4096,64]{0,1:T(8,128)(2,1)S(1)}, bf16[4096,64]{0,1:T(8,128)(2,1)S(1)}, u32[]{:S(2)}, u32[]{:S(2)}) collective-permute-start(bf16[4096,64]{0,1:T(8,128)(2,1)S(1)} %dynamic-slice_bitcast_fusion), channel_id=1, source_target_pairs={{0,1},{1,0},{2,3},{3,2},{4,5},{5,4},{6,7},{7,6},{8,9},{9,8},{10,11... | collective-permute-start | bytes 1572872 | tf_op jit(solution)/shard_map/ppermute | solution.py:90
  32.4 22.9 %copy-start.3 = (bf16[16,8,4096]{2,1,0:T(8,128)(2,1)}, bf16[16,8,4096]{2,1,0:T(8,128)(2,1)S(1)}, u32[]{:S(2)}) copy-start(bf16[16,8,4096]{2,1,0:T(8,128)(2,1)S(1)} %all-to-all-done) | copy-start | bytes 3145732
  32.9 1.5 %collective-permute-start.2 = (f32[128,64]{0,1:T(8,128)S(1)}, f32[128,64]{0,1:T(8,128)S(1)}, u32[]{:S(2)}, u32[]{:S(2)}) collective-permute-start(f32[128,64]{0,1:T(8,128)S(1)} %fusion.11), channel_id=1, source_target_pairs={{0,1},{1,0},{2,3},{3,2},{4,5},{5,4},{6,7},{7,6},{8,9},{9,8},{10,11... | collective-permute-start | bytes 98312 | tf_op jit(solution)/shard_map/ppermute | solution.py:93
  35.2 17.2 %all-to-all-start.1 = ((bf16[16,72,128]{2,1,0:T(8,128)(2,1)}), bf16[16,72,128]{2,1,0:T(8,128)(2,1)S(1)}, u32[]{:S(2)}, u32[]{:S(2)}) async-start(bf16[16,72,128]{2,1,0:T(8,128)(2,1)} %broadcast_in_dim.15), calls=%async_computation.1 | async-start | bytes 589824 | tf_op jit(solution)/shard_map/all_to_all | solution.py:99
  41.8 13.4 %collective-permute-start = (bf16[128,4096]{1,0:T(8,128)(2,1)S(1)}, bf16[128,4096]{1,0:T(8,128)(2,1)}, u32[]{:S(2)}, u32[]{:S(2)}) collective-permute-start(bf16[128,4096]{1,0:T(8,128)(2,1)S(1)} %bitcast.32), channel_id=1, source_target_pairs={{0,1},{1,0},{2,3},{3,2},{4,5},{5,4},{6,7},{7,6},{8,9},{9,8},{10,11... | collective-permute-start | bytes 3145736 | tf_op jit(solution)/shard_map/ppermute | solution.py:85
  55.3 24.3 %copy-start.1 = (bf16[1,8192,64]{1,2,0:T(8,128)(2,1)S(1)}, bf16[1,8192,64]{1,2,0:T(8,128)(2,1)}, u32[]{:S(2)}) copy-start(bf16[1,8192,64]{1,2,0:T(8,128)(2,1)} %param.12) | copy-start | bytes 3145732

commit v17 on v16

--- a/solution.py
+++ b/solution.py
@@ -97,11 +97,12 @@
     payload = jnp.concatenate([low.T, slot_rows], axis=0)
     sent = jnp.broadcast_to(payload[None], (slots_held,) + payload.shape)
     gathered = lax.all_to_all(sent, "tensor", 0, 0, tiled=False)
+    gate, up = projections(order.reshape(1).astype(jnp.int32), mine, other, gate_weight, up_weight)
+    gathered, gate, up = lax.optimization_barrier((gathered, gate, up))
     slots = gathered[:, rank, :rows].reshape(total).astype(jnp.int32)
     hits = slots[None, None, :] == jnp.arange(slots_held, dtype=jnp.int32)[:, None, None]
     spread = jnp.where(hits, gathered[:, :rank, :], jnp.zeros((), jnp.bfloat16))
 
-    gate, up = projections(order.reshape(1).astype(jnp.int32), mine, other, gate_weight, up_weight)
     delta = jnp.einsum("srt,srh->th", spread, adapter_up_weight, preferred_element_type=jnp.float32)
     return (jax.nn.silu(gate) * (up + delta)).astype(jnp.bfloat16)
 

time: 79.9 us -> 70.3 us (0.88)
  waiting for transfers between devices: 32.3 us -> 21.4 us
  local copies, waits for them, and re-layouts: 3.58 us -> 5.42 us
  other arithmetic: 2.63 us -> 1.15 us
  matrix products: 3.7 us -> 4.86 us
    all_to_all x1, waiting for transfers between devices: 10.2 us -> 0.01 us  [body(): gathered = lax.all_to_all(sent, 'tensor', 0, 0, tiled=False)]
    convert_element_type x1, other arithmetic: 2.54 us -> 1.06 us  [body(): return (jax.nn.silu(gate) * (up + delta)).astype(jnp.bfloat16)]
    dot_general x1, matrix products: 0.5 us -> 1.52 us  [body(): lent_part = jnp.dot(mine, lent, preferred_element_type=jnp.float32)]
    unnamed x10 -> x16, local copies, waits for them, and re-layouts: 0.02 us -> 1.01 us
    ppermute x1, waiting for transfers between devices: 0.85 us -> 0.01 us  [body(): lax.ppermute(lax.dynamic_slice_in_dim(down, (1 - order) * half, half), 't...]
    dynamic_slice x1, local copies, waits for them, and re-layouts: 0.04 us -> 0.88 us  [body(): lax.dynamic_slice_in_dim(down, (1 - order) * half, half)]
  transfers between devices with their start and end apart: 5 -> 5, of which waited for: 4 -> 2; matrix products, arithmetic and copies ran while one was open for 5% -> 6% of each run, Pallas kernels for 0% -> 31%
where the time goes in v17:
time: 70.3 us; the launch traced here: 70 us
  Pallas kernels  21.6 us (31%)
  waiting for transfers between devices  21.4 us (30%)
  starting transfers between devices  15.4 us (22%)
  local copies, waits for them, and re-layouts  5.42 us (8%)
  matrix products  4.86 us (7%)
  other arithmetic  1.15 us (2%)
    pallas_call x1, Pallas kernels, projections(): pl.pallas_call(_projection_kernel, grid_spec=pltpu.PrefetchScalarGridSpec...  21.6 us
    all_to_all x1, waiting for transfers between devices, body(): lax.all_to_all(copies, 'tensor', 0, 0, tiled=False)  21 us
    all_to_all x1, starting transfers between devices, body(): lax.all_to_all(copies, 'tensor', 0, 0, tiled=False)  7.39 us
    all_to_all x1, starting transfers between devices, body(): gathered = lax.all_to_all(sent, 'tensor', 0, 0, tiled=False)  6.58 us
    dot_general x1, matrix products, body(): jnp.einsum('srt,srh->th', spread, adapter_up_weight, preferred_element_ty...  2.87 us
    dot_general x1, matrix products, body(): lent_part = jnp.dot(mine, lent, preferred_element_type=jnp.float32)  1.52 us
  transfers between devices with their start and end apart: 5, of which 2 were waited for; matrix products, arithmetic and copies ran while one was open for 6% of the time, Pallas kernels for 31%

profile of v17, /device:TPU:0, one launch (start us, length us, event | category | flops | bytes accessed | tf_op | source)
XLA Modules:
  0.0 70.0 jit_solution(17132443087580347133)
XLA Ops:
  0.0 0.0 copy-start
  0.0 0.0 copy-start.7
  0.0 0.0 copy-start.2
  0.0 1.0 %slice_bitcast_fusion.1 = (bf16[1,8,4096]{2,1,0:T(8,128)(2,1)S(1)}, bf16[1,8,4096]{2,1,0:T(8,128)(2,1)S(1)}) fusion(bf16[8,8192]{1,0:T(8,128)(2,1)} %param.9), kind=kLoop, calls=%fused_computation.13 | loop fusion | bytes 262144 | tf_op jit(solution)/shard_map/stack | solution.py:82
  1.0 1.1 %broadcast_in_dim.14 = bf16[8,2,8,4096]{3,2,1,0:T(8,128)(2,1)} broadcast(bf16[2,8,4096]{2,1,0:T(8,128)(2,1)S(1)} %pad_maximum_fusion), dimensions={1,2,3} | broadcast | bytes 1179648 | tf_op jit(solution)/shard_map/broadcast_in_dim | solution.py:83
  2.1 7.4 %all-to-all-start = ((bf16[16,8,4096]{2,1,0:T(8,128)(2,1)}), bf16[16,8,4096]{2,1,0:T(8,128)(2,1)S(1)}, u32[]{:S(2)}, u32[]{:S(2)}) async-start(bf16[16,8,4096]{2,1,0:T(8,128)(2,1)} %bitcast.2), calls=%async_computation | async-start | bytes 2097152 | tf_op jit(solution)/shard_map/all_to_all | solution.py:84
  9.5 0.0 copy-done
  9.5 0.9 %dynamic-slice_bitcast_fusion = bf16[4096,64]{0,1:T(8,128)(2,1)} fusion(bf16[1,8192,64]{1,2,0:T(8,128)(2,1)S(1)} %copy-done, s32[]{:T(128)S(6)} %select_n.35), kind=kLoop, calls=%fused_computation.5 | loop fusion | bytes 1048580 | tf_op jit(solution)/shard_map/dynamic_slice | solution.py:90
  10.4 0.4 collective-permute-start
  10.8 0.0 copy-done.7
  10.8 0.0 copy-done.2
  10.8 0.6 gather_fusion
  11.4 21.0 %all-to-all-done = bf16[16,8,4096]{2,1,0:T(8,128)(2,1)S(1)} async-done(((bf16[16,8,4096]{2,1,0:T(8,128)(2,1)}), bf16[16,8,4096]{2,1,0:T(8,128)(2,1)S(1)}, u32[]{:S(2)}, u32[]{:S(2)}) %all-to-all-start) | async-done | bytes 1048608 | tf_op jit(solution)/shard_map/all_to_all | solution.py:84
  32.4 0.0 copy-start.3
  32.4 0.6 collective-permute-start.2
  33.0 0.0 collective-permute-done
  33.0 1.5 %fusion.12 = f32[128,64]{0,1:T(8,128)S(1)} fusion(bf16[4096,64]{0,1:T(8,128)(2,1)} %collective-permute-done, bf16[16,8,4096]{2,1,0:T(8,128)(2,1)S(1)} %all-to-all-done), kind=kOutput, calls=%fused_computation.26 | convolution fusion | flops 67108864 | bytes 1605632 | tf_op jit(solution)/shard_map/dot_general | solution.py:92
  34.6 0.4 collective-permute-start.1
  35.0 0.5 fusion
  35.5 0.4 collective-permute-done.1
  35.9 0.8 %broadcast_in_dim.15 = bf16[16,72,128]{2,1,0:T(8,128)(2,1)} broadcast(bf16[72,128]{1,0:T(8,128)(2,1)S(1)} %fusion.8), dimensions={1,2} | broadcast | bytes 313344 | tf_op jit(solution)/shard_map/broadcast_in_dim | solution.py:98
  36.7 6.6 %all-to-all-start.1 = ((bf16[16,72,128]{2,1,0:T(8,128)(2,1)}), bf16[16,72,128]{2,1,0:T(8,128)(2,1)S(1)}, u32[]{:S(2)}, u32[]{:S(2)}) async-start(bf16[16,72,128]{2,1,0:T(8,128)(2,1)} %broadcast_in_dim.15), calls=%async_computation.1 | async-start | bytes 589824 | tf_op jit(solution)/shard_map/all_to_all | solution.py:99
  43.2 0.0 collective-permute-done.2.other_ref
  43.2 0.0 copy-start.4
  43.3 0.0 copy-done.3
  43.3 1.0 %copy-done.4 = bf16[128,4096]{1,0:T(8,128)(2,1)} copy-done((bf16[128,4096]{1,0:T(8,128)(2,1)}, bf16[128,4096]{1,0:T(8,128)(2,1)S(1)}, u32[]{:S(2)}) %copy-start.4) | copy-done | bytes 1048600
  44.2 21.6 %shard_map.73 = (f32[128,1792]{1,0:T(8,128)}, f32[128,1792]{1,0:T(8,128)}) custom-call(s32[1]{0:T(128)} %bitcast.10.order_ref, bf16[128,4096]{1,0:T(8,128)(2,1)} %bitcast.33, bf16[128,4096]{1,0:T(8,128)(2,1)} %copy-done.4, bf16[8192,1792]{1,0:T(8,128)(2,1)} %gate_w_ref.1, bf16[8192,1792]{1,0:T(8,128)(2,1)} %up_w_ref.1), custom_call_target="tpu_custom_call" | custom-call | flops 7516192768 | bytes 62652416 | tf_op jit(solution)/shard_map/pallas_call | solution.py:42
  65.9 0.0 copy-start.5
  65.9 0.0 all-to-all-done.1
  65.9 0.1 reshape.89
  66.0 0.0 copy-start.6
  66.0 0.0 copy-start.1
  66.0 2.9 %convolution_bitcast_fusion = f32[128,1792]{1,0:T(8,128)S(1)} fusion(bf16[16,64,1792]{2,1,0:T(8,128)(2,1)} %param.13, bf16[16,72,128]{2,1,0:T(8,128)(2,1)S(1)} %all-to-all-done.1, pred[16,128]{1,0:T(8,128)(4,1)S(1)} %iota_compare_fusion.1), kind=kOutput, calls=%fused_computation.1 | convolution fusion | flops 469893120 | bytes 4851712 | tf_op jit(solution)/shard_map/srt,srh->th/dot_general | solution.py:106
  68.9 0.0 copy-done.5
  68.9 0.0 copy-done.6
  68.9 1.1 %multiply_convert_fusion = bf16[128,1792]{1,0:T(8,128)(2,1)} fusion(f32[128,1792]{1,0:T(8,128)S(1)} %copy-done.6, f32[128,1792]{1,0:T(8,128)S(1)} %convolution_bitcast_fusion, f32[128,1792]{1,0:T(8,128)S(1)} %copy-done.5), kind=kLoop, calls=%fused_computation.2 | loop fusion | flops 1605632 | bytes 3211264 | tf_op jit(solution)/shard_map/convert_element_type | solution.py:107
  70.0 0.0 copy-done.1
  (8 shorter events, 0.1 us)
Async XLA Ops:
  0.0 9.5 %copy-start = (bf16[1,8192,64]{1,2,0:T(8,128)(2,1)S(1)}, bf16[1,8192,64]{1,2,0:T(8,128)(2,1)}, u32[]{:S(2)}) copy-start(bf16[1,8192,64]{1,2,0:T(8,128)(2,1)} %param.12) | copy-start | bytes 3145732
  0.0 10.8 %copy-start.7 = (s32[8,1]{0,1:T(1,128)S(1)}, s32[8,1]{0,1:T(1,128)}, u32[]{:S(2)}) copy-start(s32[8,1]{0,1:T(1,128)} %param.14) | copy-start | bytes 100
  0.0 10.8 %copy-start.2 = (s32[16]{0:T(128)S(1)}, s32[16]{0:T(128)}, u32[]{:S(2)}) copy-start(s32[16]{0:T(128)} %param.15) | copy-start | bytes 196
  2.1 30.3 %all-to-all-start = ((bf16[16,8,4096]{2,1,0:T(8,128)(2,1)}), bf16[16,8,4096]{2,1,0:T(8,128)(2,1)S(1)}, u32[]{:S(2)}, u32[]{:S(2)}) async-start(bf16[16,8,4096]{2,1,0:T(8,128)(2,1)} %bitcast.2), calls=%async_computation | async-start | bytes 2097152 | tf_op jit(solution)/shard_map/all_to_all | solution.py:84
  10.4 22.7 %collective-permute-start = (bf16[4096,64]{0,1:T(8,128)(2,1)}, bf16[4096,64]{0,1:T(8,128)(2,1)}, u32[]{:S(2)}, u32[]{:S(2)}) collective-permute-start(bf16[4096,64]{0,1:T(8,128)(2,1)} %dynamic-slice_bitcast_fusion), channel_id=1, source_target_pairs={{0,1},{1,0},{2,3},{3,2},{4,5},{5,4},{6,7},{7,6},{8,9},{9,8},{10,11... | collective-permute-start | bytes 1572872 | tf_op jit(solution)/shard_map/ppermute | solution.py:90
  32.4 10.8 %copy-start.3 = (bf16[16,8,4096]{2,1,0:T(8,128)(2,1)}, bf16[16,8,4096]{2,1,0:T(8,128)(2,1)S(1)}, u32[]{:S(2)}) copy-start(bf16[16,8,4096]{2,1,0:T(8,128)(2,1)S(1)} %all-to-all-done) | copy-start | bytes 3145732
  32.4 10.8 %collective-permute-start.2 = (bf16[128,4096]{1,0:T(8,128)(2,1)S(1)}, bf16[128,4096]{1,0:T(8,128)(2,1)S(1)}, u32[]{:S(2)}, u32[]{:S(2)}) collective-permute-start(bf16[128,4096]{1,0:T(8,128)(2,1)S(1)} %bitcast.32), channel_id=1, source_target_pairs={{0,1},{1,0},{2,3},{3,2},{4,5},{5,4},{6,7},{7,6},{8,9},{9,8},{10,11... | collective-permute-start | bytes 3145736 | tf_op jit(solution)/shard_map/ppermute | solution.py:85
  34.6 1.3 %collective-permute-start.1 = (f32[128,64]{0,1:T(8,128)S(1)}, f32[128,64]{0,1:T(8,128)S(1)}, u32[]{:S(2)}, u32[]{:S(2)}) collective-permute-start(f32[128,64]{0,1:T(8,128)S(1)} %fusion.12), channel_id=1, source_target_pairs={{0,1},{1,0},{2,3},{3,2},{4,5},{5,4},{6,7},{7,6},{8,9},{9,8},{10,11... | collective-permute-start | bytes 98312 | tf_op jit(solution)/shard_map/ppermute | solution.py:93
  36.7 29.2 %all-to-all-start.1 = ((bf16[16,72,128]{2,1,0:T(8,128)(2,1)}), bf16[16,72,128]{2,1,0:T(8,128)(2,1)S(1)}, u32[]{:S(2)}, u32[]{:S(2)}) async-start(bf16[16,72,128]{2,1,0:T(8,128)(2,1)} %broadcast_in_dim.15), calls=%async_computation.1 | async-start | bytes 589824 | tf_op jit(solution)/shard_map/all_to_all | solution.py:99
  43.2 1.0 %copy-start.4 = (bf16[128,4096]{1,0:T(8,128)(2,1)}, bf16[128,4096]{1,0:T(8,128)(2,1)S(1)}, u32[]{:S(2)}) copy-start(bf16[128,4096]{1,0:T(8,128)(2,1)S(1)} %collective-permute-done.2.other_ref) | copy-start | bytes 3145732
  65.9 3.0 %copy-start.5 = (f32[128,1792]{1,0:T(8,128)S(1)}, f32[128,1792]{1,0:T(8,128)}, u32[]{:S(2)}) copy-start(f32[128,1792]{1,0:T(8,128)} %get-tuple-element.24) | copy-start | bytes 2752516
  66.0 2.9 %copy-start.6 = (f32[128,1792]{1,0:T(8,128)S(1)}, f32[128,1792]{1,0:T(8,128)}, u32[]{:S(2)}) copy-start(f32[128,1792]{1,0:T(8,128)} %get-tuple-element.25) | copy-start | bytes 2752516
  66.0 4.0 %copy-start.1 = (bf16[1,8192,64]{1,2,0:T(8,128)(2,1)S(1)}, bf16[1,8192,64]{1,2,0:T(8,128)(2,1)}, u32[]{:S(2)}) copy-start(bf16[1,8192,64]{1,2,0:T(8,128)(2,1)} %param.12) | copy-start | bytes 3145732

commit v18 on v12

--- a/solution.py
+++ b/solution.py
@@ -25,6 +25,10 @@
 
     pl.when(k < blocks)(lambda: accumulate(mine_ref))
     pl.when(k >= blocks)(lambda: accumulate(other_ref))
+
+    @pl.when(k == 2 * blocks - 1)
+    def _():
+        gate_ref[...] = jax.nn.silu(gate_ref[...])
 
 
 def projections(order, mine, other, gate_weight, up_weight):
@@ -59,7 +63,7 @@
         compiler_params=pltpu.CompilerParams(dimension_semantics=("arbitrary",)),
         cost_estimate=pl.CostEstimate(
             flops=4 * total * 2 * half * hidden,
-            transcendentals=0,
+            transcendentals=total * hidden,
             bytes_accessed=weight_bytes + total * 2 * half * 2 + 2 * total * hidden * 4,
         ),
     )(order, mine, other, gate_weight, up_weight)
@@ -99,9 +103,9 @@
     hits = slots[None, None, :] == jnp.arange(slots_held, dtype=jnp.int32)[:, None, None]
     spread = jnp.where(hits, gathered[:, :rank, :], jnp.zeros((), jnp.bfloat16))
 
-    gate, up = projections(order.reshape(1).astype(jnp.int32), mine, other, gate_weight, up_weight)
+    gated, up = projections(order.reshape(1).astype(jnp.int32), mine, other, gate_weight, up_weight)
     delta = jnp.einsum("srt,srh->th", spread, adapter_up_weight, preferred_element_type=jnp.float32)
-    return (jax.nn.silu(gate) * (up + delta)).astype(jnp.bfloat16)
+    return (gated * (up + delta)).astype(jnp.bfloat16)
 
 
 def solution(mesh):

time: 68.1 us -> 68.1 us (level)
  no operation moved by 1% of the time
where the time goes in v18:
time: 68.1 us; the launch traced here: 67.9 us
  blocking collectives  32 us (47%)
  Pallas kernels  21.8 us (32%)
  starting transfers between devices  5.37 us (8%)
  matrix products  3.84 us (6%)
  local copies, waits for them, and re-layouts  2.58 us (4%)
  waiting for transfers between devices  1.11 us (2%)
  other arithmetic  0.97 us (1%)
    all_to_all x1, blocking collectives, body(): lax.all_to_all(copies, 'tensor', 0, 0, tiled=False)  32 us
    pallas_call x1, Pallas kernels, projections(): pl.pallas_call(_projection_kernel, grid_spec=pltpu.PrefetchScalarGridSpec...  21.8 us
    all_to_all x1, starting transfers between devices, body(): gathered = lax.all_to_all(sent, 'tensor', 0, 0, tiled=False)  4.6 us
    dot_general x1, matrix products, body(): jnp.einsum('srt,srh->th', spread, adapter_up_weight, preferred_element_ty...  2.87 us
  transfers between devices with their start and end apart: 2, of which 1 were waited for; matrix products, arithmetic and copies ran while one was open for 2% of the time, Pallas kernels for 32%

profile of v18, /device:TPU:0, one launch (start us, length us, event | category | flops | bytes accessed | tf_op | source)
XLA Modules:
  0.0 67.9 jit_solution(8128684424774526181)
XLA Ops:
  0.0 0.0 copy-start
  0.0 0.0 copy-start.7
  0.0 0.0 copy-start.2
  0.0 1.0 %slice_bitcast_fusion.1 = (bf16[1,8,4096]{2,1,0:T(8,128)(2,1)S(1)}, bf16[1,8,4096]{2,1,0:T(8,128)(2,1)S(1)}) fusion(bf16[8,8192]{1,0:T(8,128)(2,1)} %param.9), kind=kLoop, calls=%fused_computation.15 | loop fusion | bytes 262144 | tf_op jit(solution)/shard_map/stack | solution.py:86
  1.0 0.1 broadcast_in_dim.14
  1.1 32.0 %all_to_all.10 = bf16[16,8,4096]{2,1,0:T(8,128)(2,1)S(1)} all-to-all(bf16[16,8,4096]{2,1,0:T(8,128)(2,1)S(1)} %bitcast.31), channel_id=1, replica_groups=mesh['groups'=2,'tensor'=16] {'tensor'}, dimensions={0} | all-to-all | bytes 2097152 | tf_op jit(solution)/shard_map/all_to_all | solution.py:88
  33.1 0.0 copy-start.3
  33.1 0.8 %collective-permute-start = (bf16[128,4096]{1,0:T(8,128)(2,1)S(1)}, bf16[128,4096]{1,0:T(8,128)(2,1)S(1)}, u32[]{:S(2)}, u32[]{:S(2)}) collective-permute-start(bf16[128,4096]{1,0:T(8,128)(2,1)S(1)} %bitcast.29), channel_id=1, source_target_pairs={{0,1},{1,0},{2,3},{3,2},{4,5},{5,4},{6,7},{7,6},{8,9},{9,8},{10,11... | collective-permute-start | bytes 3145736 | tf_op jit(solution)/shard_map/ppermute | solution.py:89
  33.9 0.0 copy-done.7
  33.9 0.0 copy-done.2
  33.9 0.6 gather_fusion
  34.6 0.0 copy-done
  34.6 0.5 fusion.2
  35.1 1.1 %collective-permute-done.other_ref = bf16[128,4096]{1,0:T(8,128)(2,1)S(1)} collective-permute-done((bf16[128,4096]{1,0:T(8,128)(2,1)S(1)}, bf16[128,4096]{1,0:T(8,128)(2,1)S(1)}, u32[]{:S(2)}, u32[]{:S(2)}) %collective-permute-start) | collective-permute-done | bytes 1048608 | tf_op jit(solution)/shard_map/ppermute | solution.py:89
  36.2 0.0 copy-start.4
  36.2 0.5 fusion
  36.7 0.8 %broadcast_in_dim.15 = bf16[16,72,128]{2,1,0:T(8,128)(2,1)} broadcast(bf16[72,128]{1,0:T(8,128)(2,1)S(1)} %fusion.9), dimensions={1,2} | broadcast | bytes 313344 | tf_op jit(solution)/shard_map/broadcast_in_dim | solution.py:100
  37.5 4.6 %all-to-all-start.1 = ((bf16[16,72,128]{2,1,0:T(8,128)(2,1)}), bf16[16,72,128]{2,1,0:T(8,128)(2,1)S(1)}, u32[]{:S(2)}, u32[]{:S(2)}) async-start(bf16[16,72,128]{2,1,0:T(8,128)(2,1)} %broadcast_in_dim.15), calls=%async_computation.1 | async-start | bytes 589824 | tf_op jit(solution)/shard_map/all_to_all | solution.py:101
  42.1 0.0 copy-done.3
  42.1 0.0 copy-done.4
  42.1 21.8 %shard_map.73 = (f32[128,1792]{1,0:T(8,128)}, f32[128,1792]{1,0:T(8,128)}) custom-call(s32[1]{0:T(128)} %bitcast.order_ref, bf16[128,4096]{1,0:T(8,128)(2,1)} %bitcast.30, bf16[128,4096]{1,0:T(8,128)(2,1)} %copy-done.4, bf16[8192,1792]{1,0:T(8,128)(2,1)} %gate_w_ref.1, bf16[8192,1792]{1,0:T(8,128)(2,1)} %up_w_ref.1), custom_call_target="tpu_custom_call" | custom-call | flops 7516192768 | bytes 62652416 | tf_op jit(solution)/shard_map/pallas_call | solution.py:46
  63.9 0.0 copy-start.5
  63.9 0.0 all-to-all-done.1
  64.0 0.1 reshape.89
  64.0 0.0 copy-start.6
  64.0 0.0 copy-start.1
  64.1 2.9 %convolution_bitcast_fusion = f32[128,1792]{1,0:T(8,128)S(1)} fusion(bf16[16,64,1792]{2,1,0:T(8,128)(2,1)} %param.13, bf16[16,72,128]{2,1,0:T(8,128)(2,1)S(1)} %all-to-all-done.1, pred[16,128]{1,0:T(8,128)(4,1)S(1)} %iota_compare_fusion.1), kind=kOutput, calls=%fused_computation.1 | convolution fusion | flops 469893120 | bytes 4851712 | tf_op jit(solution)/shard_map/srt,srh->th/dot_general | solution.py:107
  66.9 0.0 copy-done.5
  67.0 0.0 copy-done.6
  67.0 0.9 %multiply_convert_fusion = bf16[128,1792]{1,0:T(8,128)(2,1)} fusion(f32[128,1792]{1,0:T(8,128)S(1)} %copy-done.5, f32[128,1792]{1,0:T(8,128)S(1)} %copy-done.6, f32[128,1792]{1,0:T(8,128)S(1)} %convolution_bitcast_fusion), kind=kLoop, calls=%fused_computation.4 | loop fusion | flops 688128 | bytes 3211264 | tf_op jit(solution)/shard_map/convert_element_type | solution.py:108
  67.9 0.0 copy-done.1
  (7 shorter events, 0.1 us)
Async XLA Ops:
  0.0 34.6 %copy-start = (bf16[1,8192,64]{1,2,0:T(8,128)(2,1)S(1)}, bf16[1,8192,64]{1,2,0:T(8,128)(2,1)}, u32[]{:S(2)}) copy-start(bf16[1,8192,64]{1,2,0:T(8,128)(2,1)} %param.12) | copy-start | bytes 3145732
  0.0 33.9 %copy-start.7 = (s32[8,1]{0,1:T(1,128)S(1)}, s32[8,1]{0,1:T(1,128)}, u32[]{:S(2)}) copy-start(s32[8,1]{0,1:T(1,128)} %param.14) | copy-start | bytes 100
  0.0 33.9 %copy-start.2 = (s32[16]{0:T(128)S(1)}, s32[16]{0:T(128)}, u32[]{:S(2)}) copy-start(s32[16]{0:T(128)} %param.15) | copy-start | bytes 196
  33.1 8.9 %copy-start.3 = (bf16[16,8,4096]{2,1,0:T(8,128)(2,1)}, bf16[16,8,4096]{2,1,0:T(8,128)(2,1)S(1)}, u32[]{:S(2)}) copy-start(bf16[16,8,4096]{2,1,0:T(8,128)(2,1)S(1)} %all_to_all.10) | copy-start | bytes 3145732
  33.1 3.1 %collective-permute-start = (bf16[128,4096]{1,0:T(8,128)(2,1)S(1)}, bf16[128,4096]{1,0:T(8,128)(2,1)S(1)}, u32[]{:S(2)}, u32[]{:S(2)}) collective-permute-start(bf16[128,4096]{1,0:T(8,128)(2,1)S(1)} %bitcast.29), channel_id=1, source_target_pairs={{0,1},{1,0},{2,3},{3,2},{4,5},{5,4},{6,7},{7,6},{8,9},{9,8},{10,11... | collective-permute-start | bytes 3145736 | tf_op jit(solution)/shard_map/ppermute | solution.py:89
  36.2 5.9 %copy-start.4 = (bf16[128,4096]{1,0:T(8,128)(2,1)}, bf16[128,4096]{1,0:T(8,128)(2,1)S(1)}, u32[]{:S(2)}) copy-start(bf16[128,4096]{1,0:T(8,128)(2,1)S(1)} %collective-permute-done.other_ref) | copy-start | bytes 3145732
  37.5 26.4 %all-to-all-start.1 = ((bf16[16,72,128]{2,1,0:T(8,128)(2,1)}), bf16[16,72,128]{2,1,0:T(8,128)(2,1)S(1)}, u32[]{:S(2)}, u32[]{:S(2)}) async-start(bf16[16,72,128]{2,1,0:T(8,128)(2,1)} %broadcast_in_dim.15), calls=%async_computation.1 | async-start | bytes 589824 | tf_op jit(solution)/shard_map/all_to_all | solution.py:101
  63.9 3.0 %copy-start.5 = (f32[128,1792]{1,0:T(8,128)S(1)}, f32[128,1792]{1,0:T(8,128)}, u32[]{:S(2)}) copy-start(f32[128,1792]{1,0:T(8,128)} %get-tuple-element.19) | copy-start | bytes 2752516
  64.0 2.9 %copy-start.6 = (f32[128,1792]{1,0:T(8,128)S(1)}, f32[128,1792]{1,0:T(8,128)}, u32[]{:S(2)}) copy-start(f32[128,1792]{1,0:T(8,128)} %get-tuple-element.20) | copy-start | bytes 2752516
  64.0 3.8 %copy-start.1 = (bf16[1,8192,64]{1,2,0:T(8,128)(2,1)S(1)}, bf16[1,8192,64]{1,2,0:T(8,128)(2,1)}, u32[]{:S(2)}) copy-start(bf16[1,8192,64]{1,2,0:T(8,128)(2,1)} %param.12) | copy-start | bytes 3145732

commit v19 on v12

--- a/solution.py
+++ b/solution.py
@@ -6,7 +6,7 @@
 from jax.sharding import PartitionSpec as P
 
 SUBLANES = 8
-BLOCK_ROWS = 1024
+BLOCK_ROWS = 2048
 
 
 def _projection_kernel(order_ref, mine_ref, other_ref, gate_w_ref, up_w_ref, gate_ref, up_ref):

time: 68.1 us -> 68.3 us (level)
  no operation moved by 1% of the time
where the time goes in v19:
time: 68.3 us; the launch traced here: 68.1 us
  blocking collectives  32 us (47%)
  Pallas kernels  21.9 us (32%)
  starting transfers between devices  5.37 us (8%)
  matrix products  3.84 us (6%)
  local copies, waits for them, and re-layouts  2.58 us (4%)
  other arithmetic  1.12 us (2%)
  waiting for transfers between devices  1.11 us (2%)
    all_to_all x1, blocking collectives, body(): lax.all_to_all(copies, 'tensor', 0, 0, tiled=False)  32 us
    pallas_call x1, Pallas kernels, projections(): pl.pallas_call(_projection_kernel, grid_spec=pltpu.PrefetchScalarGridSpec...  21.9 us
    all_to_all x1, starting transfers between devices, body(): gathered = lax.all_to_all(sent, 'tensor', 0, 0, tiled=False)  4.6 us
    dot_general x1, matrix products, body(): jnp.einsum('srt,srh->th', spread, adapter_up_weight, preferred_element_ty...  2.87 us
  transfers between devices with their start and end apart: 2, of which 1 were waited for; matrix products, arithmetic and copies ran while one was open for 2% of the time, Pallas kernels for 32%

profile of v19, /device:TPU:0, one launch (start us, length us, event | category | flops | bytes accessed | tf_op | source)
XLA Modules:
  0.0 68.1 jit_solution(5028386563753584948)
XLA Ops:
  0.0 0.0 copy-start
  0.0 0.0 copy-start.7
  0.0 0.0 copy-start.2
  0.0 1.0 %slice_bitcast_fusion.1 = (bf16[1,8,4096]{2,1,0:T(8,128)(2,1)S(1)}, bf16[1,8,4096]{2,1,0:T(8,128)(2,1)S(1)}) fusion(bf16[8,8192]{1,0:T(8,128)(2,1)} %param.9), kind=kLoop, calls=%fused_computation.15 | loop fusion | bytes 262144 | tf_op jit(solution)/shard_map/stack | solution.py:82
  1.0 0.1 broadcast_in_dim.14
  1.1 32.0 %all_to_all.10 = bf16[16,8,4096]{2,1,0:T(8,128)(2,1)S(1)} all-to-all(bf16[16,8,4096]{2,1,0:T(8,128)(2,1)S(1)} %bitcast.31), channel_id=1, replica_groups=mesh['groups'=2,'tensor'=16] {'tensor'}, dimensions={0} | all-to-all | bytes 2097152 | tf_op jit(solution)/shard_map/all_to_all | solution.py:84
  33.1 0.0 copy-start.3
  33.1 0.8 %collective-permute-start = (bf16[128,4096]{1,0:T(8,128)(2,1)S(1)}, bf16[128,4096]{1,0:T(8,128)(2,1)S(1)}, u32[]{:S(2)}, u32[]{:S(2)}) collective-permute-start(bf16[128,4096]{1,0:T(8,128)(2,1)S(1)} %bitcast.29), channel_id=1, source_target_pairs={{0,1},{1,0},{2,3},{3,2},{4,5},{5,4},{6,7},{7,6},{8,9},{9,8},{10,11... | collective-permute-start | bytes 3145736 | tf_op jit(solution)/shard_map/ppermute | solution.py:85
  33.9 0.0 copy-done.7
  33.9 0.0 copy-done.2
  33.9 0.6 gather_fusion
  34.6 0.0 copy-done
  34.6 0.5 fusion.2
  35.1 1.1 %collective-permute-done.other_ref = bf16[128,4096]{1,0:T(8,128)(2,1)S(1)} collective-permute-done((bf16[128,4096]{1,0:T(8,128)(2,1)S(1)}, bf16[128,4096]{1,0:T(8,128)(2,1)S(1)}, u32[]{:S(2)}, u32[]{:S(2)}) %collective-permute-start) | collective-permute-done | bytes 1048608 | tf_op jit(solution)/shard_map/ppermute | solution.py:85
  36.2 0.0 copy-start.4
  36.2 0.5 fusion
  36.7 0.8 %broadcast_in_dim.15 = bf16[16,72,128]{2,1,0:T(8,128)(2,1)} broadcast(bf16[72,128]{1,0:T(8,128)(2,1)S(1)} %fusion.9), dimensions={1,2} | broadcast | bytes 313344 | tf_op jit(solution)/shard_map/broadcast_in_dim | solution.py:96
  37.5 4.6 %all-to-all-start.1 = ((bf16[16,72,128]{2,1,0:T(8,128)(2,1)}), bf16[16,72,128]{2,1,0:T(8,128)(2,1)S(1)}, u32[]{:S(2)}, u32[]{:S(2)}) async-start(bf16[16,72,128]{2,1,0:T(8,128)(2,1)} %broadcast_in_dim.15), calls=%async_computation.1 | async-start | bytes 589824 | tf_op jit(solution)/shard_map/all_to_all | solution.py:97
  42.1 0.0 copy-done.3
  42.1 0.0 copy-done.4
  42.1 21.9 %shard_map.73 = (f32[128,1792]{1,0:T(8,128)}, f32[128,1792]{1,0:T(8,128)}) custom-call(s32[1]{0:T(128)} %bitcast.order_ref, bf16[128,4096]{1,0:T(8,128)(2,1)} %bitcast.30, bf16[128,4096]{1,0:T(8,128)(2,1)} %copy-done.4, bf16[8192,1792]{1,0:T(8,128)(2,1)} %gate_w_ref.1, bf16[8192,1792]{1,0:T(8,128)(2,1)} %up_w_ref.1), custom_call_target="tpu_custom_call" | custom-call | flops 7516192768 | bytes 62652416 | tf_op jit(solution)/shard_map/pallas_call | solution.py:42
  64.0 0.0 copy-start.5
  64.0 0.0 all-to-all-done.1
  64.0 0.1 reshape.89
  64.1 0.0 copy-start.6
  64.1 0.0 copy-start.1
  64.1 2.9 %convolution_bitcast_fusion = f32[128,1792]{1,0:T(8,128)S(1)} fusion(bf16[16,64,1792]{2,1,0:T(8,128)(2,1)} %param.13, bf16[16,72,128]{2,1,0:T(8,128)(2,1)S(1)} %all-to-all-done.1, pred[16,128]{1,0:T(8,128)(4,1)S(1)} %iota_compare_fusion.1), kind=kOutput, calls=%fused_computation.1 | convolution fusion | flops 469893120 | bytes 4851712 | tf_op jit(solution)/shard_map/srt,srh->th/dot_general | solution.py:103
  67.0 0.0 copy-done.5
  67.0 0.0 copy-done.6
  67.0 1.0 %multiply_convert_fusion = bf16[128,1792]{1,0:T(8,128)(2,1)} fusion(f32[128,1792]{1,0:T(8,128)S(1)} %copy-done.6, f32[128,1792]{1,0:T(8,128)S(1)} %convolution_bitcast_fusion, f32[128,1792]{1,0:T(8,128)S(1)} %copy-done.5), kind=kLoop, calls=%fused_computation.4 | loop fusion | flops 1605632 | bytes 3211264 | tf_op jit(solution)/shard_map/convert_element_type | solution.py:104
  68.1 0.0 copy-done.1
  (7 shorter events, 0.1 us)
Async XLA Ops:
  0.0 34.6 %copy-start = (bf16[1,8192,64]{1,2,0:T(8,128)(2,1)S(1)}, bf16[1,8192,64]{1,2,0:T(8,128)(2,1)}, u32[]{:S(2)}) copy-start(bf16[1,8192,64]{1,2,0:T(8,128)(2,1)} %param.12) | copy-start | bytes 3145732
  0.0 33.9 %copy-start.7 = (s32[8,1]{0,1:T(1,128)S(1)}, s32[8,1]{0,1:T(1,128)}, u32[]{:S(2)}) copy-start(s32[8,1]{0,1:T(1,128)} %param.14) | copy-start | bytes 100
  0.0 33.9 %copy-start.2 = (s32[16]{0:T(128)S(1)}, s32[16]{0:T(128)}, u32[]{:S(2)}) copy-start(s32[16]{0:T(128)} %param.15) | copy-start | bytes 196
  33.1 8.9 %copy-start.3 = (bf16[16,8,4096]{2,1,0:T(8,128)(2,1)}, bf16[16,8,4096]{2,1,0:T(8,128)(2,1)S(1)}, u32[]{:S(2)}) copy-start(bf16[16,8,4096]{2,1,0:T(8,128)(2,1)S(1)} %all_to_all.10) | copy-start | bytes 3145732
  33.1 3.1 %collective-permute-start = (bf16[128,4096]{1,0:T(8,128)(2,1)S(1)}, bf16[128,4096]{1,0:T(8,128)(2,1)S(1)}, u32[]{:S(2)}, u32[]{:S(2)}) collective-permute-start(bf16[128,4096]{1,0:T(8,128)(2,1)S(1)} %bitcast.29), channel_id=1, source_target_pairs={{0,1},{1,0},{2,3},{3,2},{4,5},{5,4},{6,7},{7,6},{8,9},{9,8},{10,11... | collective-permute-start | bytes 3145736 | tf_op jit(solution)/shard_map/ppermute | solution.py:85
  36.2 5.9 %copy-start.4 = (bf16[128,4096]{1,0:T(8,128)(2,1)}, bf16[128,4096]{1,0:T(8,128)(2,1)S(1)}, u32[]{:S(2)}) copy-start(bf16[128,4096]{1,0:T(8,128)(2,1)S(1)} %collective-permute-done.other_ref) | copy-start | bytes 3145732
  37.5 26.5 %all-to-all-start.1 = ((bf16[16,72,128]{2,1,0:T(8,128)(2,1)}), bf16[16,72,128]{2,1,0:T(8,128)(2,1)S(1)}, u32[]{:S(2)}, u32[]{:S(2)}) async-start(bf16[16,72,128]{2,1,0:T(8,128)(2,1)} %broadcast_in_dim.15), calls=%async_computation.1 | async-start | bytes 589824 | tf_op jit(solution)/shard_map/all_to_all | solution.py:97
  64.0 3.0 %copy-start.5 = (f32[128,1792]{1,0:T(8,128)S(1)}, f32[128,1792]{1,0:T(8,128)}, u32[]{:S(2)}) copy-start(f32[128,1792]{1,0:T(8,128)} %get-tuple-element.19) | copy-start | bytes 2752516
  64.1 2.9 %copy-start.6 = (f32[128,1792]{1,0:T(8,128)S(1)}, f32[128,1792]{1,0:T(8,128)}, u32[]{:S(2)}) copy-start(f32[128,1792]{1,0:T(8,128)} %get-tuple-element.20) | copy-start | bytes 2752516
  64.1 4.0 %copy-start.1 = (bf16[1,8192,64]{1,2,0:T(8,128)(2,1)S(1)}, bf16[1,8192,64]{1,2,0:T(8,128)(2,1)}, u32[]{:S(2)}) copy-start(bf16[1,8192,64]{1,2,0:T(8,128)(2,1)} %param.12) | copy-start | bytes 3145732

commit v20 on v12

--- a/solution.py
+++ b/solution.py
@@ -13,17 +13,18 @@
     k = pl.program_id(0)
     blocks = pl.num_programs(0) // 2
 
-    @pl.when(k == 0)
-    def _():
-        gate_ref[...] = jnp.zeros_like(gate_ref)
-        up_ref[...] = jnp.zeros_like(up_ref)
-
     def accumulate(x_ref):
         x = x_ref[...]
         gate_ref[...] += jnp.dot(x, gate_w_ref[...], preferred_element_type=jnp.float32)
         up_ref[...] += jnp.dot(x, up_w_ref[...], preferred_element_type=jnp.float32)
 
-    pl.when(k < blocks)(lambda: accumulate(mine_ref))
+    @pl.when(k == 0)
+    def _():
+        x = mine_ref[...]
+        gate_ref[...] = jnp.dot(x, gate_w_ref[...], preferred_element_type=jnp.float32)
+        up_ref[...] = jnp.dot(x, up_w_ref[...], preferred_element_type=jnp.float32)
+
+    pl.when((k > 0) & (k < blocks))(lambda: accumulate(mine_ref))
     pl.when(k >= blocks)(lambda: accumulate(other_ref))
 
 

time: 68.1 us -> 68 us (level)
  no operation moved by 1% of the time
where the time goes in v20:
time: 68 us; the launch traced here: 67.7 us
  blocking collectives  32 us (47%)
  Pallas kernels  21.6 us (32%)
  starting transfers between devices  5.37 us (8%)
  matrix products  3.84 us (6%)
  local copies, waits for them, and re-layouts  2.58 us (4%)
  other arithmetic  1.12 us (2%)
  waiting for transfers between devices  1.11 us (2%)
    all_to_all x1, blocking collectives, body(): lax.all_to_all(copies, 'tensor', 0, 0, tiled=False)  32 us
    pallas_call x1, Pallas kernels, projections(): pl.pallas_call(_projection_kernel, grid_spec=pltpu.PrefetchScalarGridSpec...  21.6 us
    all_to_all x1, starting transfers between devices, body(): gathered = lax.all_to_all(sent, 'tensor', 0, 0, tiled=False)  4.6 us
    dot_general x1, matrix products, body(): jnp.einsum('srt,srh->th', spread, adapter_up_weight, preferred_element_ty...  2.87 us
  transfers between devices with their start and end apart: 2, of which 1 were waited for; matrix products, arithmetic and copies ran while one was open for 2% of the time, Pallas kernels for 32%

profile of v20, /device:TPU:0, one launch (start us, length us, event | category | flops | bytes accessed | tf_op | source)
XLA Modules:
  0.0 67.7 jit_solution(16234912499561528401)
XLA Ops:
  0.0 0.0 copy-start
  0.0 0.0 copy-start.7
  0.0 0.0 copy-start.2
  0.0 1.0 %slice_bitcast_fusion.1 = (bf16[1,8,4096]{2,1,0:T(8,128)(2,1)S(1)}, bf16[1,8,4096]{2,1,0:T(8,128)(2,1)S(1)}) fusion(bf16[8,8192]{1,0:T(8,128)(2,1)} %param.9), kind=kLoop, calls=%fused_computation.15 | loop fusion | bytes 262144 | tf_op jit(solution)/shard_map/stack | solution.py:83
  1.0 0.1 broadcast_in_dim.14
  1.1 32.0 %all_to_all.10 = bf16[16,8,4096]{2,1,0:T(8,128)(2,1)S(1)} all-to-all(bf16[16,8,4096]{2,1,0:T(8,128)(2,1)S(1)} %bitcast.31), channel_id=1, replica_groups=mesh['groups'=2,'tensor'=16] {'tensor'}, dimensions={0} | all-to-all | bytes 2097152 | tf_op jit(solution)/shard_map/all_to_all | solution.py:85
  33.1 0.0 copy-start.3
  33.1 0.8 %collective-permute-start = (bf16[128,4096]{1,0:T(8,128)(2,1)S(1)}, bf16[128,4096]{1,0:T(8,128)(2,1)S(1)}, u32[]{:S(2)}, u32[]{:S(2)}) collective-permute-start(bf16[128,4096]{1,0:T(8,128)(2,1)S(1)} %bitcast.29), channel_id=1, source_target_pairs={{0,1},{1,0},{2,3},{3,2},{4,5},{5,4},{6,7},{7,6},{8,9},{9,8},{10,11... | collective-permute-start | bytes 3145736 | tf_op jit(solution)/shard_map/ppermute | solution.py:86
  33.9 0.0 copy-done.7
  33.9 0.0 copy-done.2
  33.9 0.6 gather_fusion
  34.6 0.0 copy-done
  34.6 0.5 fusion.2
  35.1 1.1 %collective-permute-done.other_ref = bf16[128,4096]{1,0:T(8,128)(2,1)S(1)} collective-permute-done((bf16[128,4096]{1,0:T(8,128)(2,1)S(1)}, bf16[128,4096]{1,0:T(8,128)(2,1)S(1)}, u32[]{:S(2)}, u32[]{:S(2)}) %collective-permute-start) | collective-permute-done | bytes 1048608 | tf_op jit(solution)/shard_map/ppermute | solution.py:86
  36.2 0.0 copy-start.4
  36.2 0.5 fusion
  36.7 0.8 %broadcast_in_dim.15 = bf16[16,72,128]{2,1,0:T(8,128)(2,1)} broadcast(bf16[72,128]{1,0:T(8,128)(2,1)S(1)} %fusion.9), dimensions={1,2} | broadcast | bytes 313344 | tf_op jit(solution)/shard_map/broadcast_in_dim | solution.py:97
  37.5 4.6 %all-to-all-start.1 = ((bf16[16,72,128]{2,1,0:T(8,128)(2,1)}), bf16[16,72,128]{2,1,0:T(8,128)(2,1)S(1)}, u32[]{:S(2)}, u32[]{:S(2)}) async-start(bf16[16,72,128]{2,1,0:T(8,128)(2,1)} %broadcast_in_dim.15), calls=%async_computation.1 | async-start | bytes 589824 | tf_op jit(solution)/shard_map/all_to_all | solution.py:98
  42.1 0.0 copy-done.3
  42.1 0.0 copy-done.4
  42.1 21.6 %shard_map.73 = (f32[128,1792]{1,0:T(8,128)}, f32[128,1792]{1,0:T(8,128)}) custom-call(s32[1]{0:T(128)} %bitcast.order_ref, bf16[128,4096]{1,0:T(8,128)(2,1)} %bitcast.30, bf16[128,4096]{1,0:T(8,128)(2,1)} %copy-done.4, bf16[8192,1792]{1,0:T(8,128)(2,1)} %gate_w_ref.1, bf16[8192,1792]{1,0:T(8,128)(2,1)} %up_w_ref.1), custom_call_target="tpu_custom_call" | custom-call | flops 7516192768 | bytes 62652416 | tf_op jit(solution)/shard_map/pallas_call | solution.py:43
  63.6 0.0 copy-start.5
  63.6 0.0 all-to-all-done.1
  63.7 0.1 reshape.89
  63.8 0.0 copy-start.6
  63.8 0.0 copy-start.1
  63.8 2.9 %convolution_bitcast_fusion = f32[128,1792]{1,0:T(8,128)S(1)} fusion(bf16[16,64,1792]{2,1,0:T(8,128)(2,1)} %param.13, bf16[16,72,128]{2,1,0:T(8,128)(2,1)S(1)} %all-to-all-done.1, pred[16,128]{1,0:T(8,128)(4,1)S(1)} %iota_compare_fusion.1), kind=kOutput, calls=%fused_computation.1 | convolution fusion | flops 469893120 | bytes 4851712 | tf_op jit(solution)/shard_map/srt,srh->th/dot_general | solution.py:104
  66.7 0.0 copy-done.5
  66.7 0.0 copy-done.6
  66.7 1.0 %multiply_convert_fusion = bf16[128,1792]{1,0:T(8,128)(2,1)} fusion(f32[128,1792]{1,0:T(8,128)S(1)} %copy-done.6, f32[128,1792]{1,0:T(8,128)S(1)} %convolution_bitcast_fusion, f32[128,1792]{1,0:T(8,128)S(1)} %copy-done.5), kind=kLoop, calls=%fused_computation.4 | loop fusion | flops 1605632 | bytes 3211264 | tf_op jit(solution)/shard_map/convert_element_type | solution.py:105
  67.7 0.0 copy-done.1
  (7 shorter events, 0.1 us)
Async XLA Ops:
  0.0 34.6 %copy-start = (bf16[1,8192,64]{1,2,0:T(8,128)(2,1)S(1)}, bf16[1,8192,64]{1,2,0:T(8,128)(2,1)}, u32[]{:S(2)}) copy-start(bf16[1,8192,64]{1,2,0:T(8,128)(2,1)} %param.12) | copy-start | bytes 3145732
  0.0 33.9 %copy-start.7 = (s32[8,1]{0,1:T(1,128)S(1)}, s32[8,1]{0,1:T(1,128)}, u32[]{:S(2)}) copy-start(s32[8,1]{0,1:T(1,128)} %param.14) | copy-start | bytes 100
  0.0 33.9 %copy-start.2 = (s32[16]{0:T(128)S(1)}, s32[16]{0:T(128)}, u32[]{:S(2)}) copy-start(s32[16]{0:T(128)} %param.15) | copy-start | bytes 196
  33.1 8.9 %copy-start.3 = (bf16[16,8,4096]{2,1,0:T(8,128)(2,1)}, bf16[16,8,4096]{2,1,0:T(8,128)(2,1)S(1)}, u32[]{:S(2)}) copy-start(bf16[16,8,4096]{2,1,0:T(8,128)(2,1)S(1)} %all_to_all.10) | copy-start | bytes 3145732
  33.1 3.1 %collective-permute-start = (bf16[128,4096]{1,0:T(8,128)(2,1)S(1)}, bf16[128,4096]{1,0:T(8,128)(2,1)S(1)}, u32[]{:S(2)}, u32[]{:S(2)}) collective-permute-start(bf16[128,4096]{1,0:T(8,128)(2,1)S(1)} %bitcast.29), channel_id=1, source_target_pairs={{0,1},{1,0},{2,3},{3,2},{4,5},{5,4},{6,7},{7,6},{8,9},{9,8},{10,11... | collective-permute-start | bytes 3145736 | tf_op jit(solution)/shard_map/ppermute | solution.py:86
  36.2 5.9 %copy-start.4 = (bf16[128,4096]{1,0:T(8,128)(2,1)}, bf16[128,4096]{1,0:T(8,128)(2,1)S(1)}, u32[]{:S(2)}) copy-start(bf16[128,4096]{1,0:T(8,128)(2,1)S(1)} %collective-permute-done.other_ref) | copy-start | bytes 3145732
  37.5 26.2 %all-to-all-start.1 = ((bf16[16,72,128]{2,1,0:T(8,128)(2,1)}), bf16[16,72,128]{2,1,0:T(8,128)(2,1)S(1)}, u32[]{:S(2)}, u32[]{:S(2)}) async-start(bf16[16,72,128]{2,1,0:T(8,128)(2,1)} %broadcast_in_dim.15), calls=%async_computation.1 | async-start | bytes 589824 | tf_op jit(solution)/shard_map/all_to_all | solution.py:98
  63.6 3.0 %copy-start.5 = (f32[128,1792]{1,0:T(8,128)S(1)}, f32[128,1792]{1,0:T(8,128)}, u32[]{:S(2)}) copy-start(f32[128,1792]{1,0:T(8,128)} %get-tuple-element.19) | copy-start | bytes 2752516
  63.8 2.9 %copy-start.6 = (f32[128,1792]{1,0:T(8,128)S(1)}, f32[128,1792]{1,0:T(8,128)}, u32[]{:S(2)}) copy-start(f32[128,1792]{1,0:T(8,128)} %get-tuple-element.20) | copy-start | bytes 2752516
  63.8 4.0 %copy-start.1 = (bf16[1,8192,64]{1,2,0:T(8,128)(2,1)S(1)}, bf16[1,8192,64]{1,2,0:T(8,128)(2,1)}, u32[]{:S(2)}) copy-start(bf16[1,8192,64]{1,2,0:T(8,128)(2,1)} %param.12) | copy-start | bytes 3145732
